TPU v7x, 128 devices: a whole 4x4x4 slice. The times are simulated.
128 devices in a mesh: line: 64 (over z, y, x), tile: 2 (over core).
Axes of the slice: x: 4, y: 4, z: 4, core: 2. Of those that a mesh axis runs over, the one named last changes fastest.
Arguments:
- traces: bfloat16 [32768, 2048], P(('line', 'tile')), may hold values from -6 to 6
- trace_line: int32 [32768], P(('line', 'tile')), may hold values from 0 to 63, as said below
- trace_bin: int32 [32768], P(('line', 'tile')), may hold values from 0 to 127, as said below
- block_offset: int32 [256], P(('line', 'tile')), may hold values from 0 to 3
- nmo_coef: bfloat16 [64, 4, 8, 2048], P('line'), may hold values from -4 to 4
- band_shift: int32 [64, 4, 2048], P('line'), may hold values from 0 to 120
- bandpass: float32 [31, 2048], replicated, may hold values from -1 to 1
- fold: int32 [64, 128], P('line', 'tile'), may hold values from 4 to 20
Outputs:
- stack: float32 [64, 128, 2048], P('line', 'tile')
Inputs may be any that keep to these rules, and one draw needn't show every extreme that they name: `trace_line`: of one reader device's 256 traces at most 8 go to one line, and in every draw each device sends exactly 8 to some line. `trace_bin`: the bins of a line form 2 tiles of 64 consecutive bins; of one reader device's traces at most 4 go to one tile of one line, and in every draw each device sends exactly 4 to some tile of some line.
All inputs are finite; a program needn't handle non-finite values.
Results may differ from a plain program's by a relative error of at most 0.0003.
Values may be sent and summed in bfloat16 or wider, within the bound.
No kernel may reach another device: no remote copies, remote signals or barrier semaphores. Data moves between devices by JAX's collectives and lax.ppermute only.
A program may use at most 64 MiB of HBM per device.

v0:
```python
import jax
import jax.numpy as jnp
from jax import lax
from jax.sharding import PartitionSpec as P


def windows(data, left):
    rows_count = data.shape[0]
    length = data.shape[1]
    groups = length // 128
    padded = jnp.concatenate(
        [
            jnp.zeros((rows_count, left), data.dtype),
            data,
            jnp.zeros((rows_count, 256 - left), data.dtype),
        ],
        1,
    )
    first = padded[:, :length].reshape(rows_count, groups, 128)
    second = padded[:, 128 : length + 128].reshape(rows_count, groups, 128)
    return jnp.concatenate([first, second], 2)


def moveout_matrix(coef_rows, shift_rows):
    taps_count = coef_rows.shape[0]
    groups = coef_rows.shape[1] // 128
    column = jnp.arange(128, dtype=jnp.int32).reshape(1, 1, 128)
    position = jnp.arange(256, dtype=jnp.int32).reshape(1, 256, 1)
    shifts = shift_rows.reshape(groups, 1, 128)
    weights = coef_rows.astype(jnp.float32).reshape(taps_count, groups, 1, 128)
    matrix = jnp.zeros((groups, 256, 128), jnp.float32)
    for tap_index in range(taps_count):
        matrix = matrix + jnp.where(
            position == column + shifts + tap_index, weights[tap_index], 0.0
        )
    return matrix.astype(jnp.bfloat16)


def bandpass_matrix(taps):
    taps_count = taps.shape[0]
    groups = taps.shape[1] // 128
    half = (taps_count - 1) // 2
    column = jnp.arange(128, dtype=jnp.int32).reshape(1, 1, 128)
    position = jnp.arange(256, dtype=jnp.int32).reshape(1, 256, 1)
    weights = taps.reshape(taps_count, groups, 1, 128)
    matrix = jnp.zeros((groups, 256, 128), jnp.float32)
    for tap_index in range(taps_count):
        matrix = matrix + jnp.where(
            position == column + 64 + tap_index - half, weights[tap_index], 0.0
        )
    return matrix


def apply_filter(stacked, matrix):
    rows_count = stacked.shape[0]
    result = jnp.einsum(
        "rgw,gwc->rgc",
        windows(stacked, 64),
        matrix,
        precision=lax.Precision.HIGHEST,
        preferred_element_type=jnp.float32,
    )
    return result.reshape(rows_count, -1)


def moveout(received, received_meta, nmo_coef, band_shift, bins_total):
    slot_count, length = received.shape
    window_rows = windows(received, 0)
    slot_class = jnp.where(received_meta >= 0, received_meta // bins_total, -1)
    corrected = jnp.zeros((slot_count, length // 128, 128), jnp.float32)
    for offset_index in range(nmo_coef.shape[1]):
        matrix = moveout_matrix(nmo_coef[0, offset_index], band_shift[0, offset_index])
        product = jnp.einsum(
            "sgw,gwc->sgc", window_rows, matrix, preferred_element_type=jnp.float32
        )
        corrected = corrected + jnp.where((slot_class == offset_index)[:, None, None], product, 0.0)
    return corrected.reshape(slot_count, length)


def ranks(keys, key_count):
    onehot = (keys[:, None] == jnp.arange(key_count, dtype=jnp.int32)[None, :]).astype(jnp.int32)
    running = jnp.cumsum(onehot, 0)
    return jnp.sum(onehot * running, 1) - 1


def slot_sources(slot_of_trace, total_slots, traces, meta_values):
    trace_iota = jnp.arange(traces.shape[0], dtype=jnp.int32)
    match = jnp.arange(total_slots, dtype=jnp.int32)[:, None] == slot_of_trace[None, :]
    source = jnp.sum(jnp.where(match, trace_iota[None, :], 0), 1)
    filled = jnp.any(match, 1)
    rows_out = jnp.where(
        filled[:, None], jnp.take(traces, source, axis=0), jnp.zeros((), traces.dtype)
    )
    meta_out = jnp.where(filled, jnp.take(meta_values, source, axis=0), -1)
    return (rows_out, meta_out)


def body(traces, trace_line, trace_bin, block_offset, nmo_coef, band_shift, bandpass, fold):
    line_count = lax.axis_size("line")
    tile_count = lax.axis_size("tile")
    trace_count, length = traces.shape
    block_rows = trace_count // block_offset.shape[0]
    bin_share = fold.shape[1]
    bins_total = bin_share * tile_count
    capacity = 2 * trace_count // line_count
    trace_class = jnp.repeat(block_offset, block_rows)
    meta_values = trace_class * bins_total + trace_bin
    filter_weights = bandpass_matrix(bandpass)
    fold_share = fold[0].astype(jnp.float32)[:, None]
    slot_of_trace = trace_line * capacity + ranks(trace_line, line_count)
    rows_out, meta_out = slot_sources(slot_of_trace, line_count * capacity, traces, meta_values)
    received, received_meta = (
        lax.all_to_all(
            rows_out.reshape(line_count, capacity, length),
            "line",
            split_axis=0,
            concat_axis=0,
            tiled=True,
        ),
        lax.all_to_all(
            meta_out.reshape(line_count, capacity), "line", split_axis=0, concat_axis=0, tiled=True
        ),
    )
    flat_meta = received_meta.reshape(-1)
    corrected = moveout(received.reshape(-1, length), flat_meta, nmo_coef, band_shift, bins_total)
    bin_ids = jnp.where(flat_meta >= 0, flat_meta % bins_total, -1)
    selector = (jnp.arange(bins_total, dtype=jnp.int32)[:, None] == bin_ids[None, :]).astype(
        jnp.float32
    )
    stacked = jnp.dot(
        selector, corrected, precision=lax.Precision.HIGHEST, preferred_element_type=jnp.float32
    )
    summed = lax.psum_scatter(
        apply_filter(stacked, filter_weights), "tile", scatter_dimension=0, tiled=True
    )
    return (summed / fold_share)[None]


def solution(mesh):
    placed = (
        P(("line", "tile"), None),
        P(("line", "tile")),
        P(("line", "tile")),
        P(("line", "tile")),
        P("line", None, None, None),
        P("line", None, None),
        P(),
        P("line", "tile"),
    )
    return jax.shard_map(
        body, mesh=mesh, in_specs=placed, out_specs=P("line", "tile", None), check_vma=False
    )
```

profile of v0, /device:TPU:1, one launch (start us, length us, event | category | flops | bytes accessed | tf_op | source)
XLA Modules:
  0.0 174.5 jit_solution(17987931186254702680)
XLA Ops:
  6.5 0.8 fusion.207
  8.2 0.8 fusion.206
  8.9 0.7 add_add_fusion
  10.1 0.7 broadcast_multiply_fusion
  10.7 0.7 bitcast_add_fusion
  11.5 3.5 %gather_fusion = s32[512]{0:T(512)S(1)} fusion(s32[256]{0:T(256)S(1)} %bitcast_add_fusion, s32[1024]{0:T(1024)S(1)} %pad_clamp_fusion), kind=kCustom, calls=%fused_computation | custom fusion | bytes 6144 | tf_op jit(solution)/shard_map/jit(_take)/gather | solution.py:94
  15.2 0.6 select_select_fusion
  15.8 12.0 %all-to-all-start = ((s32[64,1,8]{2,1,0:T(1,128)}), s32[64,1,8]{2,1,0:T(1,128)S(1)}, u32[]{:S(2)}, u32[]{:S(2)}) async-start(s32[64,1,8]{2,1,0:T(1,128)} %bitcast.36), calls=%async_computation | async-start | bytes 65536 | tf_op jit(solution)/shard_map/all_to_all | solution.py:120
  28.0 0.8 fusion.218
  28.8 0.7 fusion.219
  36.1 2.5 %gather_fusion.1 = bf16[512,2048]{1,0:T(8,128)(2,1)S(1)} fusion(bf16[256,2048]{1,0:T(8,128)(2,1)S(1)} %copy-done, s32[1024]{0:T(1024)S(1)} %pad_clamp_fusion), kind=kCustom, calls=%fused_computation.1 | custom fusion | bytes 4196352 | tf_op jit(solution)/shard_map/jit(_take)/gather | solution.py:92
  38.6 0.6 iota_add_fusion.3
  39.3 0.6 iota_add_fusion.2
  39.9 0.6 iota_add_fusion.1
  40.6 0.6 iota_add_fusion
  41.5 1.4 iota_compare_fusion.41
  42.9 1.4 iota_compare_fusion.43
  44.3 1.4 iota_compare_fusion.45
  45.7 1.3 iota_compare_fusion.47
  47.0 1.4 iota_compare_fusion.49
  48.4 1.3 iota_compare_fusion.51
  49.8 0.7 iota_compare_fusion.53
  50.5 0.7 iota_compare_fusion.55
  51.2 0.7 iota_compare_fusion.57
  51.9 0.7 iota_compare_fusion.59
  52.7 0.7 iota_compare_fusion.61
  53.4 0.7 iota_compare_fusion.63
  54.1 1.6 fusion.4
  56.3 9.9 %all-to-all-start.1 = ((bf16[64,8,2048]{2,1,0:T(8,128)(2,1)}), bf16[64,8,2048]{2,1,0:T(8,128)(2,1)S(1)}, u32[]{:S(2)}, u32[]{:S(2)}) async-start(bf16[64,8,2048]{2,1,0:T(8,128)(2,1)} %fusion.4), calls=%async_computation.1 | async-start | bytes 4194304 | tf_op jit(solution)/shard_map/all_to_all | solution.py:113
  66.4 1.3 iota_compare_fusion.65
  67.7 0.7 fusion.220
  68.5 0.7 fusion.222
  69.7 0.6 reduce.5
  71.1 23.2 %all-to-all-done.1 = bf16[64,8,2048]{2,1,0:T(8,128)(2,1)S(1)} async-done(((bf16[64,8,2048]{2,1,0:T(8,128)(2,1)}), bf16[64,8,2048]{2,1,0:T(8,128)(2,1)S(1)}, u32[]{:S(2)}, u32[]{:S(2)}) %all-to-all-start.1) | async-done | bytes 2097184 | tf_op jit(solution)/shard_map/all_to_all | solution.py:113
  94.3 1.5 pad_slice_fusion
  95.8 3.9 %copy.36 = bf16[512,2048]{0,1:T(8,128)(2,1)} copy(bf16[512,2048]{1,0:T(8,128)(2,1)} %pad_slice_fusion) | data formatting | bytes 4194304 | tf_op jit(solution)/shard_map/slice | solution.py:20
  99.7 3.9 %copy.38 = bf16[512,16,128]{2,0,1:T(8,128)(2,1)} copy(bf16[512,16,128]{0,2,1:T(8,128)(2,1)} %bitcast.120) | data formatting | bytes 4194304 | tf_op jit(solution)/shard_map/reshape | solution.py:20
  103.7 0.6 copy.45
  105.0 0.9 copy-done.1
  106.1 7.4 %fusion.66 = f32[16,128,512]{2,1,0:T(8,128)S(1)} fusion(f32[16,128]{1,0:T(8,128)S(1)} %bitcast.185, s32[16,128]{1,0:T(8,128)S(1)} %copy-done.76, f32[16,128]{1,0:T(8,128)S(1)} %bitcast.184, s32[16,128]{1,0:T(8,128)S(1)} %copy-done.75, f32[16,128]{1,0:T(8,128)S(1)} %bitcast.183, s32[16,128]{1,0:T(8,128)S(1)} %copy-done.74, f32[16,128]{1,0:T(8,128)S(1)} %bitcast.182, ...), kind=kOutput, calls=%fused_computation.110 | convolution fusion | flops 557842432 | bytes 8519680 | tf_op jit(solution)/shard_map/sgw,gwc->sgc/dot_general | solution.py:73
  113.8 8.3 %fusion.67 = f32[16,128,512]{2,1,0:T(8,128)S(1)} fusion(f32[16,128]{1,0:T(8,128)} %bitcast.188, s32[16,128]{1,0:T(8,128)S(1)} %copy-done.68, f32[16,128]{1,0:T(8,128)} %bitcast.189, s32[16,128]{1,0:T(8,128)S(1)} %copy-done.67, f32[16,128]{1,0:T(8,128)} %bitcast.190, s32[16,128]{1,0:T(8,128)S(1)} %copy-done.66, f32[16,128]{1,0:T(8,128)} %bitcast.191, ...), kind=kOutput, calls=%fused_computation.111 | convolution fusion | flops 557842432 | bytes 8519680 | tf_op jit(solution)/shard_map/sgw,gwc->sgc/dot_general | solution.py:73
  122.4 7.4 %fusion.68 = f32[16,128,512]{2,1,0:T(8,128)S(1)} fusion(f32[16,128]{1,0:T(8,128)S(1)} %bitcast.177, s32[16,128]{1,0:T(8,128)S(1)} %copy-done.60, f32[16,128]{1,0:T(8,128)S(1)} %bitcast.176, s32[16,128]{1,0:T(8,128)S(1)} %copy-done.59, f32[16,128]{1,0:T(8,128)S(1)} %bitcast.175, s32[16,128]{1,0:T(8,128)S(1)} %copy-done.58, f32[16,128]{1,0:T(8,128)S(1)} %bitcast.174, ...), kind=kOutput, calls=%fused_computation.112 | convolution fusion | flops 557842432 | bytes 8519680 | tf_op jit(solution)/shard_map/sgw,gwc->sgc/dot_general | solution.py:73
  130.1 4.7 %select_add_fusion = f32[16,128,512]{2,1,0:T(8,128)S(1)} fusion(f32[16,128,512]{2,1,0:T(8,128)S(1)} %fusion.68, f32[16,128,512]{2,1,0:T(8,128)S(1)} %fusion.67, f32[16,128,512]{2,1,0:T(8,128)S(1)} %fusion.66, pred[512]{0:T(512)(128)(4,1)S(1)} %copy-done.102, pred[512]{0:T(512)(128)(4,1)S(1)} %copy-done.101, pred[512]{0:T(512)(128)(4,1)S(1)} %copy-done.100, ...), kind=kOutput, calls=%fused_computation.3 | convolution fusion | flops 565182464 | bytes 21104640 | tf_op jit(solution)/shard_map/sgw,gwc->sgc/dot_general | solution.py:73
  134.8 2.5 %fusion.203 = f32[128,2048]{1,0:T(8,128)S(1)} fusion(f32[512,2048]{0,1:T(8,128)S(1)} %bitcast.122, s32[512]{0:T(512)S(1)} %fusion.208), kind=kOutput, calls=%fused_computation.253 | convolution fusion | flops 1610678272 | bytes 5244928 | tf_op jit(solution)/shard_map/dot_general | solution.py:130
  139.1 14.6 %fusion = f32[16,128,128]{2,1,0:T(8,128)S(1)} fusion(f32[128,16,128]{2,0,1:T(8,128)S(1)} %bitcast.123, f32[128,16,128]{2,0,1:T(8,128)S(1)} %bitcast.124, f32[16,128]{1,0:T(8,128)} %bitcast.161, f32[16,128]{1,0:T(8,128)} %bitcast.162, f32[16,128]{1,0:T(8,128)S(1)} %bitcast.133, f32[16,128]{1,0:T(8,128)S(1)} %bitcast.134, f32[16,128]{1,0:T(8,128)S(1)} %bitcast.135, ...), kind=kOutput, calls=%fused_computation.5 | convolution fusion | flops 837812224 | bytes 4415488 | tf_op jit(solution)/shard_map/rgw,gwc->rgc/dot_general | solution.py:56
  153.8 1.3 copy.41
  155.1 10.6 %reduce-scatter.2.cloned.1.call-done = f32[64,2048]{1,0:T(8,128)} async-done(((f32[128,2048]{1,0:T(8,128)}), f32[64,2048]{1,0:T(8,128)}) %reduce-scatter.2.cloned.1.call-update) | async-done | bytes 524304 | tf_op jit(solution)/shard_map/reduce_scatter | solution.py:133
  165.7 1.9 %divide_bitcast_fusion = f32[1,64,2048]{2,1,0:T(8,128)} fusion(f32[64,2048]{1,0:T(8,128)} %reduce-scatter.2.cloned.1.call-done, f32[64]{0:T(128)S(1)} %convert_bitcast_fusion), kind=kLoop, calls=%fused_computation.248 | loop fusion | flops 131072 | bytes 1048832 | tf_op jit(solution)/shard_map/broadcast_in_dim | solution.py:136
  (270 shorter events, 12.7 us)
Async XLA Ops:
  6.5 29.5 %copy-start = (bf16[256,2048]{1,0:T(8,128)(2,1)S(1)}, bf16[256,2048]{1,0:T(8,128)(2,1)}, u32[]{:S(2)}) copy-start(bf16[256,2048]{1,0:T(8,128)(2,1)} %param.8) | copy-start | bytes 3145732
  6.5 21.4 %copy-start.2 = (f32[31,2048]{1,0:T(8,128)S(1)}, f32[31,2048]{1,0:T(8,128)}, u32[]{:S(2)}) copy-start(f32[31,2048]{1,0:T(8,128)} %param.14) | copy-start | bytes 761860
  15.8 40.5 %all-to-all-start = ((s32[64,1,8]{2,1,0:T(1,128)}), s32[64,1,8]{2,1,0:T(1,128)S(1)}, u32[]{:S(2)}, u32[]{:S(2)}) async-start(s32[64,1,8]{2,1,0:T(1,128)} %bitcast.36), calls=%async_computation | async-start | bytes 65536 | tf_op jit(solution)/shard_map/all_to_all | solution.py:120
  56.3 11.5 %copy-start.3 = (bf16[1,4,8,2048]{3,2,1,0:T(8,128)(2,1)S(1)}, bf16[1,4,8,2048]{3,2,1,0:T(8,128)(2,1)}, u32[]{:S(2)}) copy-start(bf16[1,4,8,2048]{3,2,1,0:T(8,128)(2,1)} %param.12) | copy-start | bytes 393220
  56.3 38.0 %all-to-all-start.1 = ((bf16[64,8,2048]{2,1,0:T(8,128)(2,1)}), bf16[64,8,2048]{2,1,0:T(8,128)(2,1)S(1)}, u32[]{:S(2)}, u32[]{:S(2)}) async-start(bf16[64,8,2048]{2,1,0:T(8,128)(2,1)} %fusion.4), calls=%async_computation.1 | async-start | bytes 4194304 | tf_op jit(solution)/shard_map/all_to_all | solution.py:113
  66.2 99.6 %reduce-scatter.2.cloned.1.call-start = ((), (), s32[]{:S(2)}) async-start(), calls=%async_computation.3 | async-start | bytes 1572864 | tf_op jit(solution)/shard_map/reduce_scatter | solution.py:133
  106.0 7.5 %copy-start.61 = (s32[16,128]{1,0:T(8,128)S(1)}, s32[16,128]{1,0:T(8,128)}, u32[]{:S(2)}) copy-start(s32[16,128]{1,0:T(8,128)} %get-tuple-element.96) | copy-start | bytes 24580
  106.0 7.5 %copy-start.62 = (s32[16,128]{1,0:T(8,128)S(1)}, s32[16,128]{1,0:T(8,128)}, u32[]{:S(2)}) copy-start(s32[16,128]{1,0:T(8,128)} %get-tuple-element.97) | copy-start | bytes 24580
  106.0 7.5 %copy-start.63 = (s32[16,128]{1,0:T(8,128)S(1)}, s32[16,128]{1,0:T(8,128)}, u32[]{:S(2)}) copy-start(s32[16,128]{1,0:T(8,128)} %get-tuple-element.98) | copy-start | bytes 24580
  106.0 7.5 %copy-start.64 = (s32[16,128]{1,0:T(8,128)S(1)}, s32[16,128]{1,0:T(8,128)}, u32[]{:S(2)}) copy-start(s32[16,128]{1,0:T(8,128)} %get-tuple-element.99) | copy-start | bytes 24580
  106.0 7.5 %copy-start.65 = (s32[16,128]{1,0:T(8,128)S(1)}, s32[16,128]{1,0:T(8,128)}, u32[]{:S(2)}) copy-start(s32[16,128]{1,0:T(8,128)} %get-tuple-element.100) | copy-start | bytes 24580
  106.1 7.5 %copy-start.66 = (s32[16,128]{1,0:T(8,128)S(1)}, s32[16,128]{1,0:T(8,128)}, u32[]{:S(2)}) copy-start(s32[16,128]{1,0:T(8,128)} %get-tuple-element.101) | copy-start | bytes 24580
  106.1 7.5 %copy-start.67 = (s32[16,128]{1,0:T(8,128)S(1)}, s32[16,128]{1,0:T(8,128)}, u32[]{:S(2)}) copy-start(s32[16,128]{1,0:T(8,128)} %get-tuple-element.102) | copy-start | bytes 24580
  113.6 8.4 %copy-start.53 = (s32[16,128]{1,0:T(8,128)S(1)}, s32[16,128]{1,0:T(8,128)}, u32[]{:S(2)}) copy-start(s32[16,128]{1,0:T(8,128)} %get-tuple-element.104) | copy-start | bytes 24580
  113.6 8.4 %copy-start.54 = (s32[16,128]{1,0:T(8,128)S(1)}, s32[16,128]{1,0:T(8,128)}, u32[]{:S(2)}) copy-start(s32[16,128]{1,0:T(8,128)} %get-tuple-element.105) | copy-start | bytes 24580
  113.7 8.4 %copy-start.55 = (s32[16,128]{1,0:T(8,128)S(1)}, s32[16,128]{1,0:T(8,128)}, u32[]{:S(2)}) copy-start(s32[16,128]{1,0:T(8,128)} %get-tuple-element.106) | copy-start | bytes 24580
  113.7 8.4 %copy-start.56 = (s32[16,128]{1,0:T(8,128)S(1)}, s32[16,128]{1,0:T(8,128)}, u32[]{:S(2)}) copy-start(s32[16,128]{1,0:T(8,128)} %get-tuple-element.107) | copy-start | bytes 24580
  113.7 8.4 %copy-start.57 = (s32[16,128]{1,0:T(8,128)S(1)}, s32[16,128]{1,0:T(8,128)}, u32[]{:S(2)}) copy-start(s32[16,128]{1,0:T(8,128)} %get-tuple-element.108) | copy-start | bytes 24580
  113.7 8.4 %copy-start.58 = (s32[16,128]{1,0:T(8,128)S(1)}, s32[16,128]{1,0:T(8,128)}, u32[]{:S(2)}) copy-start(s32[16,128]{1,0:T(8,128)} %get-tuple-element.109) | copy-start | bytes 24580
  113.7 8.4 %copy-start.59 = (s32[16,128]{1,0:T(8,128)S(1)}, s32[16,128]{1,0:T(8,128)}, u32[]{:S(2)}) copy-start(s32[16,128]{1,0:T(8,128)} %get-tuple-element.110) | copy-start | bytes 24580
  113.7 8.4 %copy-start.60 = (s32[16,128]{1,0:T(8,128)S(1)}, s32[16,128]{1,0:T(8,128)}, u32[]{:S(2)}) copy-start(s32[16,128]{1,0:T(8,128)} %get-tuple-element.111) | copy-start | bytes 24580
  113.7 8.4 %copy-start.85 = (f32[1,1,1,2048]{3,2,1,0:T(1,128)S(1)}, f32[1,1,1,2048]{3,2,1,0:T(1,128)}, u32[]{:S(2)}) copy-start(f32[1,1,1,2048]{3,2,1,0:T(1,128)} %get-tuple-element.123) | copy-start | bytes 24580
  113.7 8.4 %copy-start.86 = (f32[1,1,1,2048]{3,2,1,0:T(1,128)S(1)}, f32[1,1,1,2048]{3,2,1,0:T(1,128)}, u32[]{:S(2)}) copy-start(f32[1,1,1,2048]{3,2,1,0:T(1,128)} %get-tuple-element.124) | copy-start | bytes 24580
  113.7 8.4 %copy-start.87 = (f32[1,1,1,2048]{3,2,1,0:T(1,128)S(1)}, f32[1,1,1,2048]{3,2,1,0:T(1,128)}, u32[]{:S(2)}) copy-start(f32[1,1,1,2048]{3,2,1,0:T(1,128)} %get-tuple-element.125) | copy-start | bytes 24580
  113.7 8.4 %copy-start.88 = (f32[1,1,1,2048]{3,2,1,0:T(1,128)S(1)}, f32[1,1,1,2048]{3,2,1,0:T(1,128)}, u32[]{:S(2)}) copy-start(f32[1,1,1,2048]{3,2,1,0:T(1,128)} %get-tuple-element.126) | copy-start | bytes 24580
  113.8 8.4 %copy-start.89 = (f32[1,1,1,2048]{3,2,1,0:T(1,128)S(1)}, f32[1,1,1,2048]{3,2,1,0:T(1,128)}, u32[]{:S(2)}) copy-start(f32[1,1,1,2048]{3,2,1,0:T(1,128)} %get-tuple-element.127) | copy-start | bytes 24580
  113.8 8.4 %copy-start.90 = (f32[1,1,1,2048]{3,2,1,0:T(1,128)S(1)}, f32[1,1,1,2048]{3,2,1,0:T(1,128)}, u32[]{:S(2)}) copy-start(f32[1,1,1,2048]{3,2,1,0:T(1,128)} %get-tuple-element.128) | copy-start | bytes 24580
  113.8 8.4 %copy-start.91 = (f32[1,1,1,2048]{3,2,1,0:T(1,128)S(1)}, f32[1,1,1,2048]{3,2,1,0:T(1,128)}, u32[]{:S(2)}) copy-start(f32[1,1,1,2048]{3,2,1,0:T(1,128)} %get-tuple-element.129) | copy-start | bytes 24580
  113.8 8.4 %copy-start.92 = (f32[1,1,1,2048]{3,2,1,0:T(1,128)S(1)}, f32[1,1,1,2048]{3,2,1,0:T(1,128)}, u32[]{:S(2)}) copy-start(f32[1,1,1,2048]{3,2,1,0:T(1,128)} %get-tuple-element.130) | copy-start | bytes 24580
  122.2 7.6 %copy-start.45 = (s32[16,128]{1,0:T(8,128)S(1)}, s32[16,128]{1,0:T(8,128)}, u32[]{:S(2)}) copy-start(s32[16,128]{1,0:T(8,128)} %get-tuple-element.80) | copy-start | bytes 24580
  122.2 7.6 %copy-start.46 = (s32[16,128]{1,0:T(8,128)S(1)}, s32[16,128]{1,0:T(8,128)}, u32[]{:S(2)}) copy-start(s32[16,128]{1,0:T(8,128)} %get-tuple-element.81) | copy-start | bytes 24580
  122.3 7.6 %copy-start.47 = (s32[16,128]{1,0:T(8,128)S(1)}, s32[16,128]{1,0:T(8,128)}, u32[]{:S(2)}) copy-start(s32[16,128]{1,0:T(8,128)} %get-tuple-element.82) | copy-start | bytes 24580
  122.3 7.6 %copy-start.48 = (s32[16,128]{1,0:T(8,128)S(1)}, s32[16,128]{1,0:T(8,128)}, u32[]{:S(2)}) copy-start(s32[16,128]{1,0:T(8,128)} %get-tuple-element.83) | copy-start | bytes 24580
  122.3 7.6 %copy-start.49 = (s32[16,128]{1,0:T(8,128)S(1)}, s32[16,128]{1,0:T(8,128)}, u32[]{:S(2)}) copy-start(s32[16,128]{1,0:T(8,128)} %get-tuple-element.84) | copy-start | bytes 24580
  122.3 7.6 %copy-start.50 = (s32[16,128]{1,0:T(8,128)S(1)}, s32[16,128]{1,0:T(8,128)}, u32[]{:S(2)}) copy-start(s32[16,128]{1,0:T(8,128)} %get-tuple-element.85) | copy-start | bytes 24580
  122.3 7.6 %copy-start.51 = (s32[16,128]{1,0:T(8,128)S(1)}, s32[16,128]{1,0:T(8,128)}, u32[]{:S(2)}) copy-start(s32[16,128]{1,0:T(8,128)} %get-tuple-element.86) | copy-start | bytes 24580
  122.3 7.6 %copy-start.52 = (s32[16,128]{1,0:T(8,128)S(1)}, s32[16,128]{1,0:T(8,128)}, u32[]{:S(2)}) copy-start(s32[16,128]{1,0:T(8,128)} %get-tuple-element.87) | copy-start | bytes 24580
  122.3 7.6 %copy-start.77 = (f32[1,1,1,2048]{3,2,1,0:T(1,128)S(1)}, f32[1,1,1,2048]{3,2,1,0:T(1,128)}, u32[]{:S(2)}) copy-start(f32[1,1,1,2048]{3,2,1,0:T(1,128)} %get-tuple-element.44) | copy-start | bytes 24580
  122.3 7.6 %copy-start.78 = (f32[1,1,1,2048]{3,2,1,0:T(1,128)S(1)}, f32[1,1,1,2048]{3,2,1,0:T(1,128)}, u32[]{:S(2)}) copy-start(f32[1,1,1,2048]{3,2,1,0:T(1,128)} %get-tuple-element.45) | copy-start | bytes 24580
  122.3 7.6 %copy-start.79 = (f32[1,1,1,2048]{3,2,1,0:T(1,128)S(1)}, f32[1,1,1,2048]{3,2,1,0:T(1,128)}, u32[]{:S(2)}) copy-start(f32[1,1,1,2048]{3,2,1,0:T(1,128)} %get-tuple-element.46) | copy-start | bytes 24580
  122.3 7.6 %copy-start.80 = (f32[1,1,1,2048]{3,2,1,0:T(1,128)S(1)}, f32[1,1,1,2048]{3,2,1,0:T(1,128)}, u32[]{:S(2)}) copy-start(f32[1,1,1,2048]{3,2,1,0:T(1,128)} %get-tuple-element.47) | copy-start | bytes 24580
  122.4 7.6 %copy-start.81 = (f32[1,1,1,2048]{3,2,1,0:T(1,128)S(1)}, f32[1,1,1,2048]{3,2,1,0:T(1,128)}, u32[]{:S(2)}) copy-start(f32[1,1,1,2048]{3,2,1,0:T(1,128)} %get-tuple-element.48) | copy-start | bytes 24580
  122.4 7.6 %copy-start.82 = (f32[1,1,1,2048]{3,2,1,0:T(1,128)S(1)}, f32[1,1,1,2048]{3,2,1,0:T(1,128)}, u32[]{:S(2)}) copy-start(f32[1,1,1,2048]{3,2,1,0:T(1,128)} %get-tuple-element.49) | copy-start | bytes 24580
  122.4 7.6 %copy-start.83 = (f32[1,1,1,2048]{3,2,1,0:T(1,128)S(1)}, f32[1,1,1,2048]{3,2,1,0:T(1,128)}, u32[]{:S(2)}) copy-start(f32[1,1,1,2048]{3,2,1,0:T(1,128)} %get-tuple-element.50) | copy-start | bytes 24580
  122.4 7.6 %copy-start.84 = (f32[1,1,1,2048]{3,2,1,0:T(1,128)S(1)}, f32[1,1,1,2048]{3,2,1,0:T(1,128)}, u32[]{:S(2)}) copy-start(f32[1,1,1,2048]{3,2,1,0:T(1,128)} %get-tuple-element.51) | copy-start | bytes 24580
  122.4 7.6 %copy-start.100 = (pred[512]{0:T(512)(128)(4,1)S(1)}, pred[512]{0:T(512)(128)(4,1)}, u32[]{:S(2)}) copy-start(pred[512]{0:T(512)(128)(4,1)} %get-tuple-element.112) | copy-start | bytes 1540
  122.4 7.6 %copy-start.101 = (pred[512]{0:T(512)(128)(4,1)S(1)}, pred[512]{0:T(512)(128)(4,1)}, u32[]{:S(2)}) copy-start(pred[512]{0:T(512)(128)(4,1)} %get-tuple-element.113) | copy-start | bytes 1540
  122.4 7.6 %copy-start.102 = (pred[512]{0:T(512)(128)(4,1)S(1)}, pred[512]{0:T(512)(128)(4,1)}, u32[]{:S(2)}) copy-start(pred[512]{0:T(512)(128)(4,1)} %get-tuple-element.114) | copy-start | bytes 1540
  (59 other events, 77.2 us)
Sparse Core Ops, SparseCore 0:
  155.2 10.4 reduce-scatter.1
where the time goes:
time: 175 us
  matrix products  45 us (26%)
  other arithmetic  33.9 us (19%)
  waiting for transfers between devices  33.8 us (19%)
  local copies, waits for them, and re-layouts  24.6 us (14%)
  starting transfers between devices  22.1 us (13%)
  between operations  15.1 us (9%)
    dot_general x4, matrix products, moveout(): jnp.einsum('sgw,gwc->sgc', window_rows, matrix, preferred_element_type=jn...  27.9 us
    all_to_all x1, waiting for transfers between devices, body(): lax.all_to_all(rows_out.reshape(line_count, capacity, length), 'line', sp...  23.2 us
    dot_general x1, matrix products, apply_filter(): jnp.einsum('rgw,gwc->rgc', windows(stacked, 64), matrix, precision=lax.Pr...  14.6 us
    eq x16, other arithmetic, bandpass_matrix(): position == column + 64 + tap_index - half  14.2 us
    all_to_all x1, starting transfers between devices, body(): lax.all_to_all(meta_out.reshape(line_count, capacity), 'line', split_axis...  12 us
    reduce_scatter x1, waiting for transfers between devices, body(): lax.psum_scatter(apply_filter(stacked, filter_weights), 'tile', scatter_d...  10.6 us
    all_to_all x1, starting transfers between devices, body(): lax.all_to_all(rows_out.reshape(line_count, capacity, length), 'line', sp...  9.91 us
    sub x31, other arithmetic, bandpass_matrix(): column + 64 + tap_index - half  7.03 us
  transfers between devices with their start and end apart: 3, of which 2 were waited for; matrix products, arithmetic and copies ran while one was open for 19% of the time, Pallas kernels for 0%

commit v1 on v0

--- a/solution.py
+++ b/solution.py
@@ -2,6 +2,8 @@
 import jax.numpy as jnp
 from jax import lax
 from jax.sharding import PartitionSpec as P
+
+META = 128
 
 
 def windows(data, left):
@@ -63,10 +65,9 @@
     return result.reshape(rows_count, -1)
 
 
-def moveout(received, received_meta, nmo_coef, band_shift, bins_total):
-    slot_count, length = received.shape
-    window_rows = windows(received, 0)
-    slot_class = jnp.where(received_meta >= 0, received_meta // bins_total, -1)
+def moveout(rows, slot_class, nmo_coef, band_shift):
+    slot_count, length = rows.shape
+    window_rows = windows(rows, 0)
     corrected = jnp.zeros((slot_count, length // 128, 128), jnp.float32)
     for offset_index in range(nmo_coef.shape[1]):
         matrix = moveout_matrix(nmo_coef[0, offset_index], band_shift[0, offset_index])
@@ -83,57 +84,52 @@
     return jnp.sum(onehot * running, 1) - 1
 
 
-def slot_sources(slot_of_trace, total_slots, traces, meta_values):
-    trace_iota = jnp.arange(traces.shape[0], dtype=jnp.int32)
-    match = jnp.arange(total_slots, dtype=jnp.int32)[:, None] == slot_of_trace[None, :]
-    source = jnp.sum(jnp.where(match, trace_iota[None, :], 0), 1)
-    filled = jnp.any(match, 1)
-    rows_out = jnp.where(
-        filled[:, None], jnp.take(traces, source, axis=0), jnp.zeros((), traces.dtype)
-    )
-    meta_out = jnp.where(filled, jnp.take(meta_values, source, axis=0), -1)
-    return (rows_out, meta_out)
-
-
 def body(traces, trace_line, trace_bin, block_offset, nmo_coef, band_shift, bandpass, fold):
     line_count = lax.axis_size("line")
     tile_count = lax.axis_size("tile")
     trace_count, length = traces.shape
     block_rows = trace_count // block_offset.shape[0]
     bin_share = fold.shape[1]
-    bins_total = bin_share * tile_count
-    capacity = 2 * trace_count // line_count
+    dest_count = line_count * tile_count
+    capacity = 4
+    slots = dest_count * capacity
     trace_class = jnp.repeat(block_offset, block_rows)
-    meta_values = trace_class * bins_total + trace_bin
-    filter_weights = bandpass_matrix(bandpass)
-    fold_share = fold[0].astype(jnp.float32)[:, None]
-    slot_of_trace = trace_line * capacity + ranks(trace_line, line_count)
-    rows_out, meta_out = slot_sources(slot_of_trace, line_count * capacity, traces, meta_values)
-    received, received_meta = (
-        lax.all_to_all(
-            rows_out.reshape(line_count, capacity, length),
-            "line",
-            split_axis=0,
-            concat_axis=0,
-            tiled=True,
-        ),
-        lax.all_to_all(
-            meta_out.reshape(line_count, capacity), "line", split_axis=0, concat_axis=0, tiled=True
-        ),
-    )
-    flat_meta = received_meta.reshape(-1)
-    corrected = moveout(received.reshape(-1, length), flat_meta, nmo_coef, band_shift, bins_total)
-    bin_ids = jnp.where(flat_meta >= 0, flat_meta % bins_total, -1)
-    selector = (jnp.arange(bins_total, dtype=jnp.int32)[:, None] == bin_ids[None, :]).astype(
+    trace_tile = trace_bin // bin_share
+    dest = trace_line * tile_count + trace_tile
+    slot_of_trace = dest * capacity + ranks(dest, dest_count)
+    lane = jnp.arange(META, dtype=jnp.int32)[None, :]
+    meta_block = jnp.where(
+        lane == 0,
+        (trace_bin % bin_share)[:, None],
+        jnp.where(lane == 1, trace_class[:, None], jnp.where(lane == 2, 1, 0)),
+    ).astype(jnp.bfloat16)
+    extended = jnp.concatenate([traces, meta_block], 1)
+    select = (
+        jnp.arange(slots, dtype=jnp.int32)[:, None] == slot_of_trace[None, :]
+    ).astype(jnp.bfloat16)
+    send = jnp.dot(select, extended, preferred_element_type=jnp.float32).astype(jnp.bfloat16)
+    received = lax.all_to_all(
+        send.reshape(dest_count, capacity, length + META),
+        ("line", "tile"),
+        split_axis=0,
+        concat_axis=0,
+        tiled=True,
+    ).reshape(slots, length + META)
+    rows = received[:, :length]
+    meta = received[:, length:length + 3].astype(jnp.int32)
+    valid = meta[:, 2] == 1
+    slot_bin = jnp.where(valid, meta[:, 0], -1)
+    slot_class = jnp.where(valid, meta[:, 1], -1)
+    corrected = moveout(rows, slot_class, nmo_coef, band_shift)
+    selector = (jnp.arange(bin_share, dtype=jnp.int32)[:, None] == slot_bin[None, :]).astype(
         jnp.float32
     )
     stacked = jnp.dot(
         selector, corrected, precision=lax.Precision.HIGHEST, preferred_element_type=jnp.float32
     )
-    summed = lax.psum_scatter(
-        apply_filter(stacked, filter_weights), "tile", scatter_dimension=0, tiled=True
-    )
-    return (summed / fold_share)[None]
+    filtered = apply_filter(stacked, bandpass_matrix(bandpass))
+    fold_share = fold[0].astype(jnp.float32)[:, None]
+    return (filtered / fold_share)[None]
 
 
 def solution(mesh):

time: 175 us -> 100 us (0.57)
  other arithmetic: 33.9 us -> 8.91 us
  matrix products: 45 us -> 28.3 us
  between operations: 15.1 us -> 1.73 us
  starting transfers between devices: 22.1 us -> 11.5 us
  waiting for transfers between devices: 33.8 us -> 24 us
    dot_general x4, matrix products: 27.9 us -> 15.1 us  [moveout(): jnp.einsum('sgw,gwc->sgc', window_rows, matrix, preferred_element_type=jn...]
    eq x16, other arithmetic: 14.2 us -> 1.91 us  [bandpass_matrix(): position == column + 64 + tap_index - half]
    reduce_scatter x1 -> x0, waiting for transfers between devices: 10.6 us -> none  [body(): lax.psum_scatter(apply_filter(stacked, filter_weights), 'tile', scatter_d...]
    all_to_all x2 -> x1, starting transfers between devices: 21.9 us -> 11.5 us  [body(): lax.all_to_all(send.reshape(dest_count, capacity, length + META), ('line'...]
    sub x31, other arithmetic: 7.03 us -> 0.11 us  [bandpass_matrix(): column + 64 + tap_index - half]
    gather x3 -> x0, local copies, waits for them, and re-layouts: 6.05 us -> none  [the longest x2 3.58 us: slot_sources(): meta_out = jnp.where(filled, jnp.take(meta_values, source, axis=0), -1)]
    dot_general x1, matrix products: 14.6 us -> 8.87 us  [apply_filter(): jnp.einsum('rgw,gwc->rgc', windows(stacked, 64), matrix, precision=lax.Pr...]
    reshape x1 -> x2, local copies, waits for them, and re-layouts: 0.09 us -> 4.2 us  [the longest x1 2.11 us: body(): send.reshape(dest_count, capacity, length + META)]
  transfers between devices with their start and end apart: 3 -> 1, of which waited for: 2 -> 1; matrix products, arithmetic and copies ran while one was open for 19% -> 8% of each run, Pallas kernels for 0% -> 0%
where the time goes in v1:
time: 100 us
  matrix products  28.3 us (28%)
  local copies, waits for them, and re-layouts  25.5 us (26%)
  waiting for transfers between devices  24 us (24%)
  starting transfers between devices  11.5 us (12%)
  other arithmetic  8.91 us (9%)
  between operations  1.73 us (2%)
    all_to_all x1, waiting for transfers between devices, body(): lax.all_to_all(send.reshape(dest_count, capacity, length + META), ('line'...  24 us
    dot_general x4, matrix products, moveout(): jnp.einsum('sgw,gwc->sgc', window_rows, matrix, preferred_element_type=jn...  15.1 us
    all_to_all x1, starting transfers between devices, body(): lax.all_to_all(send.reshape(dest_count, capacity, length + META), ('line'...  11.5 us
    dot_general x1, matrix products, apply_filter(): jnp.einsum('rgw,gwc->rgc', windows(stacked, 64), matrix, precision=lax.Pr...  8.87 us
    slice x2, local copies, waits for them, and re-layouts, body(): rows = received[:, :length]  4.22 us
    reshape x2, local copies, waits for them, and re-layouts, windows(): first = padded[:, :length].reshape(rows_count, groups, 128)  4.13 us
    reshape x2, local copies, waits for them, and re-layouts, windows(): second = padded[:, 128:length + 128].reshape(rows_count, groups, 128)  4.09 us
    slice x2, local copies, waits for them, and re-layouts, windows(): second = padded[:, 128:length + 128].reshape(rows_count, groups, 128)  3.95 us
  transfers between devices with their start and end apart: 1, of which 1 were waited for; matrix products, arithmetic and copies ran while one was open for 8% of the time, Pallas kernels for 0%

profile of v1, /device:TPU:1, one launch (start us, length us, event | category | flops | bytes accessed | tf_op | source)
XLA Modules:
  0.0 100.0 jit_solution(2941339722455004460)
XLA Ops:
  0.0 0.6 copy-done
  0.7 0.1 broadcast_bitcast_fusion
  0.7 0.7 fusion.215
  1.4 0.1 copy.27
  1.5 0.2 fusion.209
  1.9 0.3 fusion.210
  2.1 2.0 %convolution_convert_fusion = bf16[512,2176]{1,0:T(8,128)(2,1)S(1)} fusion(bf16[256,128]{1,0:T(8,128)(2,1)S(1)} %get-tuple-element.135, bf16[256,2048]{1,0:T(8,128)(2,1)} %param.8, s32[256]{0:T(256)S(1)} %add_add_fusion), kind=kOutput, calls=%fused_computation | convolution fusion | flops 573898752 | bytes 3343360 | tf_op jit(solution)/shard_map/dot_general | solution.py:110
  4.2 2.1 %reshape.1627 = bf16[128,4,2176]{2,1,0:T(4,128)(2,1)} reshape(bf16[512,2176]{1,0:T(8,128)(2,1)S(1)} %convolution_convert_fusion) | data formatting | bytes 4456448 | tf_op jit(solution)/shard_map/reshape | solution.py:112
  6.3 11.5 %all-to-all-start = ((bf16[128,4,2176]{2,1,0:T(4,128)(2,1)}), bf16[128,4,2176]{2,1,0:T(4,128)(2,1)S(1)}, u32[]{:S(2)}, u32[]{:S(2)}) async-start(bf16[128,4,2176]{2,1,0:T(4,128)(2,1)} %reshape.1627), calls=%async_computation | async-start | bytes 4456448 | tf_op jit(solution)/shard_map/all_to_all | solution.py:111
  18.2 0.6 iota_add_fusion.2
  18.9 0.7 iota_add_fusion
  19.5 0.6 iota_add_fusion.3
  20.2 0.6 iota_add_fusion.1
  21.5 0.7 iota_compare_fusion.62
  22.1 0.7 iota_compare_fusion.64
  22.8 0.7 fusion.224
  23.5 0.7 fusion.223
  24.2 0.7 fusion.225
  25.0 0.7 fusion.227
  25.7 24.0 %all-to-all-done = bf16[128,4,2176]{2,1,0:T(4,128)(2,1)S(1)} async-done(((bf16[128,4,2176]{2,1,0:T(4,128)(2,1)}), bf16[128,4,2176]{2,1,0:T(4,128)(2,1)S(1)}, u32[]{:S(2)}, u32[]{:S(2)}) %all-to-all-start) | async-done | bytes 2228256 | tf_op jit(solution)/shard_map/all_to_all | solution.py:111
  49.7 2.1 %reshape.1628 = bf16[512,2176]{1,0:T(8,128)(2,1)} reshape(bf16[128,4,2176]{2,1,0:T(4,128)(2,1)S(1)} %all-to-all-done) | data formatting | bytes 4456448 | tf_op jit(solution)/shard_map/reshape | solution.py:117
  51.8 0.9 slice_convert_fusion
  52.7 1.7 %slice.434 = bf16[512,2048]{1,0:T(8,128)(2,1)S(1)} slice(bf16[512,2176]{1,0:T(8,128)(2,1)} %reshape.1628), slice={[0:512], [0:2048]} | slice | bytes 4194304 | tf_op jit(solution)/shard_map/slice | solution.py:118
  54.4 1.5 %pad_slice_fusion = bf16[512,2048]{1,0:T(8,128)(2,1)} fusion(bf16[512,2048]{1,0:T(8,128)(2,1)S(1)} %slice.434), kind=kLoop, calls=%fused_computation.3 | loop fusion | bytes 4194304 | tf_op jit(solution)/shard_map/slice | solution.py:22
  55.9 2.5 %copy.29 = bf16[512,2048]{0,1:T(8,128)(2,1)} copy(bf16[512,2048]{1,0:T(8,128)(2,1)S(1)} %slice.434) | data formatting | bytes 4194304 | tf_op jit(solution)/shard_map/slice | solution.py:118
  58.4 0.2 fusion.207
  58.6 1.0 compare_reduce_fusion.3
  59.6 4.1 %copy.31 = bf16[512,16,128]{2,0,1:T(8,128)(2,1)} copy(bf16[512,16,128]{0,2,1:T(8,128)(2,1)} %bitcast.101) | data formatting | bytes 4194304 | tf_op jit(solution)/shard_map/reshape | solution.py:21
  63.7 2.5 %copy.30 = bf16[512,2048]{0,1:T(8,128)(2,1)} copy(bf16[512,2048]{1,0:T(8,128)(2,1)S(1)} %copy-done.1) | data formatting | bytes 4194304 | tf_op jit(solution)/shard_map/slice | solution.py:22
  66.2 4.0 %copy.32 = bf16[512,16,128]{2,0,1:T(8,128)(2,1)} copy(bf16[512,16,128]{0,2,1:T(8,128)(2,1)} %bitcast.102) | data formatting | bytes 4194304 | tf_op jit(solution)/shard_map/reshape | solution.py:22
  70.5 4.2 %fusion.69 = f32[16,128,512]{2,1,0:T(8,128)S(1)} fusion(f32[16,128]{1,0:T(8,128)S(1)} %bitcast.170, s32[16,128]{1,0:T(8,128)S(1)} %copy-done.63, f32[16,128]{1,0:T(8,128)S(1)} %bitcast.171, s32[16,128]{1,0:T(8,128)S(1)} %copy-done.62, f32[16,128]{1,0:T(8,128)S(1)} %bitcast.172, s32[16,128]{1,0:T(8,128)S(1)} %copy-done.61, f32[16,128]{1,0:T(8,128)S(1)} %bitcast.173, ...), kind=kOutput, calls=%fused_computation.107 | convolution fusion | flops 557842432 | bytes 8519680 | tf_op jit(solution)/shard_map/sgw,gwc->sgc/dot_general | solution.py:74
  75.1 3.9 %fusion.70 = f32[16,128,512]{2,1,0:T(8,128)S(1)} fusion(f32[16,128]{1,0:T(8,128)} %bitcast.167, s32[16,128]{1,0:T(8,128)S(1)} %copy-done.71, f32[16,128]{1,0:T(8,128)S(1)} %bitcast.166, s32[16,128]{1,0:T(8,128)S(1)} %copy-done.70, f32[16,128]{1,0:T(8,128)S(1)} %bitcast.165, s32[16,128]{1,0:T(8,128)S(1)} %copy-done.69, f32[16,128]{1,0:T(8,128)S(1)} %bitcast.164, ...), kind=kOutput, calls=%fused_computation.108 | convolution fusion | flops 557842432 | bytes 8519680 | tf_op jit(solution)/shard_map/sgw,gwc->sgc/dot_general | solution.py:74
  79.3 3.3 %fusion.68 = f32[16,128,512]{2,1,0:T(8,128)S(1)} fusion(f32[16,128]{1,0:T(8,128)S(1)} %bitcast.159, s32[16,128]{1,0:T(8,128)S(1)} %copy-done.55, f32[16,128]{1,0:T(8,128)S(1)} %bitcast.158, s32[16,128]{1,0:T(8,128)S(1)} %copy-done.54, f32[16,128]{1,0:T(8,128)S(1)} %bitcast.157, s32[16,128]{1,0:T(8,128)S(1)} %copy-done.53, f32[16,128]{1,0:T(8,128)S(1)} %bitcast.156, ...), kind=kOutput, calls=%fused_computation.106 | convolution fusion | flops 557842432 | bytes 8519680 | tf_op jit(solution)/shard_map/sgw,gwc->sgc/dot_general | solution.py:74
  82.6 3.7 %select_add_fusion = f32[16,128,512]{2,1,0:T(8,128)S(1)} fusion(f32[16,128,512]{2,1,0:T(8,128)S(1)} %fusion.70, f32[16,128,512]{2,1,0:T(8,128)S(1)} %fusion.69, f32[16,128,512]{2,1,0:T(8,128)S(1)} %fusion.68, pred[512]{0:T(512)(128)(4,1)S(1)} %copy-done.89, pred[512]{0:T(512)(128)(4,1)S(1)} %copy-done.88, pred[512]{0:T(512)(128)(4,1)S(1)} %copy-done.87, ...), kind=kOutput, calls=%fused_computation.2 | convolution fusion | flops 565182464 | bytes 21104640 | tf_op jit(solution)/shard_map/sgw,gwc->sgc/dot_general | solution.py:74
  86.3 2.3 %fusion.212 = f32[64,2048]{1,0:T(8,128)S(1)} fusion(f32[512,2048]{0,1:T(8,128)S(1)} %bitcast.103, s32[512]{0:T(512)S(1)} %get-tuple-element.9), kind=kOutput, calls=%fused_computation.300 | convolution fusion | flops 805339136 | bytes 4720640 | tf_op jit(solution)/shard_map/dot_general | solution.py:127
  89.0 0.3 fusion.205
  89.6 0.0 copy-done.27
  89.6 0.0 copy-done.28
  89.6 0.0 copy-done.29
  89.6 0.0 copy-done.30
  89.6 0.0 copy-done.31
  89.6 0.0 copy-done.32
  89.6 0.0 copy-done.33
  89.7 0.0 copy-done.37
  89.8 8.9 %fusion.62 = f32[64,16,128]{2,0,1:T(8,128)S(1)} fusion(f32[64,16,128]{2,0,1:T(8,128)S(1)} %bitcast.106, f32[64,16,128]{2,0,1:T(8,128)S(1)} %bitcast.105, f32[16,128]{1,0:T(8,128)S(1)} %bitcast.124, f32[16,128]{1,0:T(8,128)S(1)} %bitcast.125, f32[16,128]{1,0:T(8,128)S(1)} %bitcast.127, f32[16,128]{1,0:T(8,128)S(1)} %bitcast.128, ...), kind=kOutput, calls=%fused_computation.102 | convolution fusion | flops 434896896 | bytes 2842624 | tf_op jit(solution)/shard_map/rgw,gwc->rgc/dot_general | solution.py:58
  98.7 0.3 copy.39
  99.0 0.1 reshape.1634
  99.1 0.9 broadcast_divide_fusion
  (233 shorter events, 1.3 us)
Async XLA Ops:
  6.3 11.9 %copy-start.90 = (s32[1,64]{1,0:T(1,128)S(1)}, s32[1,64]{1,0:T(1,128)}, u32[]{:S(2)}) copy-start(s32[1,64]{1,0:T(1,128)} %param.15) | copy-start | bytes 772
  6.3 11.9 %copy-start.6 = (s32[1,4,2048]{2,1,0:T(4,128)S(1)}, s32[1,4,2048]{2,1,0:T(4,128)}, u32[]{:S(2)}) copy-start(s32[1,4,2048]{2,1,0:T(4,128)} %param.13) | copy-start | bytes 98308
  6.3 16.5 %copy-start.4 = (f32[31,2048]{1,0:T(8,128)S(1)}, f32[31,2048]{1,0:T(8,128)}, u32[]{:S(2)}) copy-start(f32[31,2048]{1,0:T(8,128)} %param.14) | copy-start | bytes 761860
  6.3 17.9 %copy-start.5 = (bf16[1,4,8,2048]{3,2,1,0:T(8,128)(2,1)S(1)}, bf16[1,4,8,2048]{3,2,1,0:T(8,128)(2,1)}, u32[]{:S(2)}) copy-start(bf16[1,4,8,2048]{3,2,1,0:T(8,128)(2,1)} %param.12) | copy-start | bytes 393220
  6.3 43.4 %all-to-all-start = ((bf16[128,4,2176]{2,1,0:T(4,128)(2,1)}), bf16[128,4,2176]{2,1,0:T(4,128)(2,1)S(1)}, u32[]{:S(2)}, u32[]{:S(2)}) async-start(bf16[128,4,2176]{2,1,0:T(4,128)(2,1)} %reshape.1627), calls=%async_computation | async-start | bytes 4456448 | tf_op jit(solution)/shard_map/all_to_all | solution.py:111
  59.6 4.1 %copy-start.1 = (bf16[512,2048]{1,0:T(8,128)(2,1)S(1)}, bf16[512,2048]{1,0:T(8,128)(2,1)}, u32[]{:S(2)}) copy-start(bf16[512,2048]{1,0:T(8,128)(2,1)} %pad_slice_fusion) | copy-start | bytes 6291460
  66.2 4.1 %copy-start.2 = (bf16[512,16,128]{2,0,1:T(8,128)(2,1)S(1)}, bf16[512,16,128]{2,0,1:T(8,128)(2,1)}, u32[]{:S(2)}) copy-start(bf16[512,16,128]{2,0,1:T(8,128)(2,1)} %copy.31) | copy-start | bytes 6291460
  66.2 4.1 %copy-start.56 = (s32[16,128]{1,0:T(8,128)S(1)}, s32[16,128]{1,0:T(8,128)}, u32[]{:S(2)}) copy-start(s32[16,128]{1,0:T(8,128)} %get-tuple-element.100) | copy-start | bytes 24580
  66.2 4.1 %copy-start.57 = (s32[16,128]{1,0:T(8,128)S(1)}, s32[16,128]{1,0:T(8,128)}, u32[]{:S(2)}) copy-start(s32[16,128]{1,0:T(8,128)} %get-tuple-element.101) | copy-start | bytes 24580
  66.2 4.1 %copy-start.58 = (s32[16,128]{1,0:T(8,128)S(1)}, s32[16,128]{1,0:T(8,128)}, u32[]{:S(2)}) copy-start(s32[16,128]{1,0:T(8,128)} %get-tuple-element.102) | copy-start | bytes 24580
  66.2 4.1 %copy-start.59 = (s32[16,128]{1,0:T(8,128)S(1)}, s32[16,128]{1,0:T(8,128)}, u32[]{:S(2)}) copy-start(s32[16,128]{1,0:T(8,128)} %get-tuple-element.103) | copy-start | bytes 24580
  66.2 4.1 %copy-start.60 = (s32[16,128]{1,0:T(8,128)S(1)}, s32[16,128]{1,0:T(8,128)}, u32[]{:S(2)}) copy-start(s32[16,128]{1,0:T(8,128)} %get-tuple-element.104) | copy-start | bytes 24580
  66.2 4.1 %copy-start.61 = (s32[16,128]{1,0:T(8,128)S(1)}, s32[16,128]{1,0:T(8,128)}, u32[]{:S(2)}) copy-start(s32[16,128]{1,0:T(8,128)} %get-tuple-element.105) | copy-start | bytes 24580
  66.2 4.1 %copy-start.62 = (s32[16,128]{1,0:T(8,128)S(1)}, s32[16,128]{1,0:T(8,128)}, u32[]{:S(2)}) copy-start(s32[16,128]{1,0:T(8,128)} %get-tuple-element.106) | copy-start | bytes 24580
  66.2 4.1 %copy-start.63 = (s32[16,128]{1,0:T(8,128)S(1)}, s32[16,128]{1,0:T(8,128)}, u32[]{:S(2)}) copy-start(s32[16,128]{1,0:T(8,128)} %get-tuple-element.107) | copy-start | bytes 24580
  66.2 4.1 %copy-start.86 = (f32[1,1,1,2048]{3,2,1,0:T(1,128)S(1)}, f32[1,1,1,2048]{3,2,1,0:T(1,128)}, u32[]{:S(2)}) copy-start(f32[1,1,1,2048]{3,2,1,0:T(1,128)} %get-tuple-element.71) | copy-start | bytes 24580
  70.4 4.4 %copy-start.3 = (bf16[512,16,128]{2,0,1:T(8,128)(2,1)S(1)}, bf16[512,16,128]{2,0,1:T(8,128)(2,1)}, u32[]{:S(2)}) copy-start(bf16[512,16,128]{2,0,1:T(8,128)(2,1)} %copy.32) | copy-start | bytes 6291460
  70.4 4.4 %copy-start.64 = (s32[16,128]{1,0:T(8,128)S(1)}, s32[16,128]{1,0:T(8,128)}, u32[]{:S(2)}) copy-start(s32[16,128]{1,0:T(8,128)} %get-tuple-element.108) | copy-start | bytes 24580
  70.4 4.4 %copy-start.65 = (s32[16,128]{1,0:T(8,128)S(1)}, s32[16,128]{1,0:T(8,128)}, u32[]{:S(2)}) copy-start(s32[16,128]{1,0:T(8,128)} %get-tuple-element.109) | copy-start | bytes 24580
  70.4 4.4 %copy-start.66 = (s32[16,128]{1,0:T(8,128)S(1)}, s32[16,128]{1,0:T(8,128)}, u32[]{:S(2)}) copy-start(s32[16,128]{1,0:T(8,128)} %get-tuple-element.110) | copy-start | bytes 24580
  70.4 4.4 %copy-start.67 = (s32[16,128]{1,0:T(8,128)S(1)}, s32[16,128]{1,0:T(8,128)}, u32[]{:S(2)}) copy-start(s32[16,128]{1,0:T(8,128)} %get-tuple-element.111) | copy-start | bytes 24580
  70.4 4.4 %copy-start.68 = (s32[16,128]{1,0:T(8,128)S(1)}, s32[16,128]{1,0:T(8,128)}, u32[]{:S(2)}) copy-start(s32[16,128]{1,0:T(8,128)} %get-tuple-element.112) | copy-start | bytes 24580
  70.4 4.4 %copy-start.69 = (s32[16,128]{1,0:T(8,128)S(1)}, s32[16,128]{1,0:T(8,128)}, u32[]{:S(2)}) copy-start(s32[16,128]{1,0:T(8,128)} %get-tuple-element.113) | copy-start | bytes 24580
  70.4 4.4 %copy-start.70 = (s32[16,128]{1,0:T(8,128)S(1)}, s32[16,128]{1,0:T(8,128)}, u32[]{:S(2)}) copy-start(s32[16,128]{1,0:T(8,128)} %get-tuple-element.114) | copy-start | bytes 24580
  70.4 4.4 %copy-start.71 = (s32[16,128]{1,0:T(8,128)S(1)}, s32[16,128]{1,0:T(8,128)}, u32[]{:S(2)}) copy-start(s32[16,128]{1,0:T(8,128)} %get-tuple-element.115) | copy-start | bytes 24580
  70.5 4.4 %copy-start.80 = (f32[1,1,1,2048]{3,2,1,0:T(1,128)S(1)}, f32[1,1,1,2048]{3,2,1,0:T(1,128)}, u32[]{:S(2)}) copy-start(f32[1,1,1,2048]{3,2,1,0:T(1,128)} %get-tuple-element.126) | copy-start | bytes 24580
  70.5 4.4 %copy-start.81 = (f32[1,1,1,2048]{3,2,1,0:T(1,128)S(1)}, f32[1,1,1,2048]{3,2,1,0:T(1,128)}, u32[]{:S(2)}) copy-start(f32[1,1,1,2048]{3,2,1,0:T(1,128)} %get-tuple-element.127) | copy-start | bytes 24580
  70.5 4.4 %copy-start.82 = (f32[1,1,1,2048]{3,2,1,0:T(1,128)S(1)}, f32[1,1,1,2048]{3,2,1,0:T(1,128)}, u32[]{:S(2)}) copy-start(f32[1,1,1,2048]{3,2,1,0:T(1,128)} %get-tuple-element.128) | copy-start | bytes 24580
  70.5 4.4 %copy-start.83 = (f32[1,1,1,2048]{3,2,1,0:T(1,128)S(1)}, f32[1,1,1,2048]{3,2,1,0:T(1,128)}, u32[]{:S(2)}) copy-start(f32[1,1,1,2048]{3,2,1,0:T(1,128)} %get-tuple-element.129) | copy-start | bytes 24580
  70.5 4.4 %copy-start.84 = (f32[1,1,1,2048]{3,2,1,0:T(1,128)S(1)}, f32[1,1,1,2048]{3,2,1,0:T(1,128)}, u32[]{:S(2)}) copy-start(f32[1,1,1,2048]{3,2,1,0:T(1,128)} %get-tuple-element.130) | copy-start | bytes 24580
  70.5 4.4 %copy-start.85 = (f32[1,1,1,2048]{3,2,1,0:T(1,128)S(1)}, f32[1,1,1,2048]{3,2,1,0:T(1,128)}, u32[]{:S(2)}) copy-start(f32[1,1,1,2048]{3,2,1,0:T(1,128)} %get-tuple-element.131) | copy-start | bytes 24580
  74.9 4.1 %copy-start.48 = (s32[16,128]{1,0:T(8,128)S(1)}, s32[16,128]{1,0:T(8,128)}, u32[]{:S(2)}) copy-start(s32[16,128]{1,0:T(8,128)} %get-tuple-element.92) | copy-start | bytes 24580
  74.9 4.1 %copy-start.49 = (s32[16,128]{1,0:T(8,128)S(1)}, s32[16,128]{1,0:T(8,128)}, u32[]{:S(2)}) copy-start(s32[16,128]{1,0:T(8,128)} %get-tuple-element.93) | copy-start | bytes 24580
  74.9 4.1 %copy-start.50 = (s32[16,128]{1,0:T(8,128)S(1)}, s32[16,128]{1,0:T(8,128)}, u32[]{:S(2)}) copy-start(s32[16,128]{1,0:T(8,128)} %get-tuple-element.94) | copy-start | bytes 24580
  74.9 4.1 %copy-start.51 = (s32[16,128]{1,0:T(8,128)S(1)}, s32[16,128]{1,0:T(8,128)}, u32[]{:S(2)}) copy-start(s32[16,128]{1,0:T(8,128)} %get-tuple-element.95) | copy-start | bytes 24580
  74.9 4.1 %copy-start.52 = (s32[16,128]{1,0:T(8,128)S(1)}, s32[16,128]{1,0:T(8,128)}, u32[]{:S(2)}) copy-start(s32[16,128]{1,0:T(8,128)} %get-tuple-element.96) | copy-start | bytes 24580
  75.0 4.1 %copy-start.53 = (s32[16,128]{1,0:T(8,128)S(1)}, s32[16,128]{1,0:T(8,128)}, u32[]{:S(2)}) copy-start(s32[16,128]{1,0:T(8,128)} %get-tuple-element.97) | copy-start | bytes 24580
  75.0 4.1 %copy-start.54 = (s32[16,128]{1,0:T(8,128)S(1)}, s32[16,128]{1,0:T(8,128)}, u32[]{:S(2)}) copy-start(s32[16,128]{1,0:T(8,128)} %get-tuple-element.98) | copy-start | bytes 24580
  75.0 4.1 %copy-start.55 = (s32[16,128]{1,0:T(8,128)S(1)}, s32[16,128]{1,0:T(8,128)}, u32[]{:S(2)}) copy-start(s32[16,128]{1,0:T(8,128)} %get-tuple-element.99) | copy-start | bytes 24580
  75.0 4.1 %copy-start.72 = (f32[1,1,1,2048]{3,2,1,0:T(1,128)S(1)}, f32[1,1,1,2048]{3,2,1,0:T(1,128)}, u32[]{:S(2)}) copy-start(f32[1,1,1,2048]{3,2,1,0:T(1,128)} %get-tuple-element.118) | copy-start | bytes 24580
  75.0 4.1 %copy-start.73 = (f32[1,1,1,2048]{3,2,1,0:T(1,128)S(1)}, f32[1,1,1,2048]{3,2,1,0:T(1,128)}, u32[]{:S(2)}) copy-start(f32[1,1,1,2048]{3,2,1,0:T(1,128)} %get-tuple-element.119) | copy-start | bytes 24580
  75.0 4.1 %copy-start.74 = (f32[1,1,1,2048]{3,2,1,0:T(1,128)S(1)}, f32[1,1,1,2048]{3,2,1,0:T(1,128)}, u32[]{:S(2)}) copy-start(f32[1,1,1,2048]{3,2,1,0:T(1,128)} %get-tuple-element.120) | copy-start | bytes 24580
  75.0 4.1 %copy-start.75 = (f32[1,1,1,2048]{3,2,1,0:T(1,128)S(1)}, f32[1,1,1,2048]{3,2,1,0:T(1,128)}, u32[]{:S(2)}) copy-start(f32[1,1,1,2048]{3,2,1,0:T(1,128)} %get-tuple-element.121) | copy-start | bytes 24580
  75.0 4.1 %copy-start.76 = (f32[1,1,1,2048]{3,2,1,0:T(1,128)S(1)}, f32[1,1,1,2048]{3,2,1,0:T(1,128)}, u32[]{:S(2)}) copy-start(f32[1,1,1,2048]{3,2,1,0:T(1,128)} %get-tuple-element.122) | copy-start | bytes 24580
  75.0 4.1 %copy-start.77 = (f32[1,1,1,2048]{3,2,1,0:T(1,128)S(1)}, f32[1,1,1,2048]{3,2,1,0:T(1,128)}, u32[]{:S(2)}) copy-start(f32[1,1,1,2048]{3,2,1,0:T(1,128)} %get-tuple-element.123) | copy-start | bytes 24580
  75.0 4.1 %copy-start.78 = (f32[1,1,1,2048]{3,2,1,0:T(1,128)S(1)}, f32[1,1,1,2048]{3,2,1,0:T(1,128)}, u32[]{:S(2)}) copy-start(f32[1,1,1,2048]{3,2,1,0:T(1,128)} %get-tuple-element.124) | copy-start | bytes 24580
  75.1 4.1 %copy-start.79 = (f32[1,1,1,2048]{3,2,1,0:T(1,128)S(1)}, f32[1,1,1,2048]{3,2,1,0:T(1,128)}, u32[]{:S(2)}) copy-start(f32[1,1,1,2048]{3,2,1,0:T(1,128)} %get-tuple-element.125) | copy-start | bytes 24580
  79.2 3.4 %copy-start.10 = (s32[16,128]{1,0:T(8,128)S(1)}, s32[16,128]{1,0:T(8,128)}, u32[]{:S(2)}) copy-start(s32[16,128]{1,0:T(8,128)} %get-tuple-element.85) | copy-start | bytes 24580
  (44 other events, 58.1 us)

commit v2 on v1

--- a/solution.py
+++ b/solution.py
@@ -2,25 +2,9 @@
 import jax.numpy as jnp
 from jax import lax
 from jax.sharding import PartitionSpec as P
+from jax.experimental import pallas as pl
 
 META = 128
-
-
-def windows(data, left):
-    rows_count = data.shape[0]
-    length = data.shape[1]
-    groups = length // 128
-    padded = jnp.concatenate(
-        [
-            jnp.zeros((rows_count, left), data.dtype),
-            data,
-            jnp.zeros((rows_count, 256 - left), data.dtype),
-        ],
-        1,
-    )
-    first = padded[:, :length].reshape(rows_count, groups, 128)
-    second = padded[:, 128 : length + 128].reshape(rows_count, groups, 128)
-    return jnp.concatenate([first, second], 2)
 
 
 def moveout_matrix(coef_rows, shift_rows):
@@ -43,39 +27,102 @@
     groups = taps.shape[1] // 128
     half = (taps_count - 1) // 2
     column = jnp.arange(128, dtype=jnp.int32).reshape(1, 1, 128)
-    position = jnp.arange(256, dtype=jnp.int32).reshape(1, 256, 1)
+    position = jnp.arange(384, dtype=jnp.int32).reshape(1, 384, 1)
     weights = taps.reshape(taps_count, groups, 1, 128)
-    matrix = jnp.zeros((groups, 256, 128), jnp.float32)
+    matrix = jnp.zeros((groups, 384, 128), jnp.float32)
     for tap_index in range(taps_count):
         matrix = matrix + jnp.where(
-            position == column + 64 + tap_index - half, weights[tap_index], 0.0
+            position == column + 128 + tap_index - half, weights[tap_index], 0.0
         )
     return matrix
 
 
-def apply_filter(stacked, matrix):
-    rows_count = stacked.shape[0]
-    result = jnp.einsum(
-        "rgw,gwc->rgc",
-        windows(stacked, 64),
-        matrix,
-        precision=lax.Precision.HIGHEST,
-        preferred_element_type=jnp.float32,
-    )
-    return result.reshape(rows_count, -1)
+def split3(value):
+    high = value.astype(jnp.bfloat16)
+    rest = value - high.astype(jnp.float32)
+    middle = rest.astype(jnp.bfloat16)
+    low = (rest - middle.astype(jnp.float32)).astype(jnp.bfloat16)
+    return high, middle, low
 
 
-def moveout(rows, slot_class, nmo_coef, band_shift):
-    slot_count, length = rows.shape
-    window_rows = windows(rows, 0)
-    corrected = jnp.zeros((slot_count, length // 128, 128), jnp.float32)
-    for offset_index in range(nmo_coef.shape[1]):
-        matrix = moveout_matrix(nmo_coef[0, offset_index], band_shift[0, offset_index])
-        product = jnp.einsum(
-            "sgw,gwc->sgc", window_rows, matrix, preferred_element_type=jnp.float32
-        )
-        corrected = corrected + jnp.where((slot_class == offset_index)[:, None, None], product, 0.0)
-    return corrected.reshape(slot_count, length)
+def dot32(left, right):
+    a = split3(left)
+    b = split3(right)
+    pairs = ((0, 0), (0, 1), (1, 0), (0, 2), (2, 0), (1, 1))
+    total = None
+    for i, j in pairs:
+        part = jnp.dot(a[i], b[j], preferred_element_type=jnp.float32)
+        total = part if total is None else total + part
+    return total
+
+
+def moveout_kernel(rows_ref, class_ref, select_ref, matrix_ref, out_ref):
+    group = pl.program_id(0)
+    length = out_ref.shape[1] * pl.num_programs(0)
+    start = pl.multiple_of(group * 128, 128)
+    window = rows_ref[:, pl.ds(start, 256)]
+    lanes = start + lax.broadcasted_iota(jnp.int32, (1, 256), 1)
+    window = jnp.where(lanes < length, window, jnp.zeros((), window.dtype))
+    slot_class = class_ref[...]
+    corrected = jnp.zeros((window.shape[0], 128), jnp.float32)
+    for offset_index in range(matrix_ref.shape[0]):
+        product = jnp.dot(window, matrix_ref[offset_index, 0], preferred_element_type=jnp.float32)
+        corrected = corrected + jnp.where(slot_class == offset_index, product, 0.0)
+    select = select_ref[...]
+    total = None
+    for part in split3(corrected):
+        piece = jnp.dot(select, part, preferred_element_type=jnp.float32)
+        total = piece if total is None else total + piece
+    out_ref[...] = total
+
+
+def filter_kernel(stack_ref, matrix_ref, fold_ref, out_ref):
+    group = pl.program_id(0)
+    groups = pl.num_programs(0)
+    total = None
+    for step in range(3):
+        index = group + step - 1
+        clipped = jnp.clip(index, 0, groups - 1)
+        block = stack_ref[:, pl.ds(pl.multiple_of(clipped * 128, 128), 128)]
+        keep = jnp.logical_and(index >= 0, index < groups)
+        block = jnp.where(keep, block, 0.0)
+        piece = dot32(block, matrix_ref[0, step * 128:(step + 1) * 128, :])
+        total = piece if total is None else total + piece
+    out_ref[...] = total / fold_ref[...]
+
+
+def moveout_stack(rows, slot_class, select, matrices, length):
+    slot_count, width = rows.shape
+    bins = select.shape[0]
+    classes, groups = matrices.shape[0], matrices.shape[1]
+    return pl.pallas_call(
+        moveout_kernel,
+        grid=(groups,),
+        in_specs=[
+            pl.BlockSpec((slot_count, width), lambda g: (0, 0)),
+            pl.BlockSpec((slot_count, 1), lambda g: (0, 0)),
+            pl.BlockSpec((bins, slot_count), lambda g: (0, 0)),
+            pl.BlockSpec((classes, 1, 256, 128), lambda g: (0, g, 0, 0)),
+        ],
+        out_specs=pl.BlockSpec((bins, 128), lambda g: (0, g)),
+        out_shape=jax.ShapeDtypeStruct((bins, length), jnp.float32),
+    )(rows, slot_class, select, matrices)
+
+
+def filter_stack(stacked, matrix, fold_share):
+    bins, length = stacked.shape
+    groups = matrix.shape[0]
+    return pl.pallas_call(
+        filter_kernel,
+        grid=(groups,),
+        in_specs=[
+            pl.BlockSpec((bins, length), lambda g: (0, 0)),
+            pl.BlockSpec((1, 384, 128), lambda g: (g, 0, 0)),
+            pl.BlockSpec((bins, 1), lambda g: (0, 0)),
+        ],
+        out_specs=pl.BlockSpec((bins, 128), lambda g: (0, g)),
+        out_shape=jax.ShapeDtypeStruct((bins, length), jnp.float32),
+    )(stacked, matrix, fold_share)
 
 
 def ranks(keys, key_count):
@@ -115,21 +162,23 @@
         concat_axis=0,
         tiled=True,
     ).reshape(slots, length + META)
-    rows = received[:, :length]
     meta = received[:, length:length + 3].astype(jnp.int32)
     valid = meta[:, 2] == 1
     slot_bin = jnp.where(valid, meta[:, 0], -1)
     slot_class = jnp.where(valid, meta[:, 1], -1)
-    corrected = moveout(rows, slot_class, nmo_coef, band_shift)
-    selector = (jnp.arange(bin_share, dtype=jnp.int32)[:, None] == slot_bin[None, :]).astype(
-        jnp.float32
+    select = (jnp.arange(bin_share, dtype=jnp.int32)[:, None] == slot_bin[None, :]).astype(
+        jnp.bfloat16
     )
-    stacked = jnp.dot(
-        selector, corrected, precision=lax.Precision.HIGHEST, preferred_element_type=jnp.float32
+    matrices = jnp.stack(
+        [
+            moveout_matrix(nmo_coef[0, offset_index], band_shift[0, offset_index])
+            for offset_index in range(nmo_coef.shape[1])
+        ]
     )
-    filtered = apply_filter(stacked, bandpass_matrix(bandpass))
+    stacked = moveout_stack(received, slot_class[:, None], select, matrices, length)
     fold_share = fold[0].astype(jnp.float32)[:, None]
-    return (filtered / fold_share)[None]
+    filtered = filter_stack(stacked, bandpass_matrix(bandpass), fold_share)
+    return filtered[None]
 
 
 def solution(mesh):

time: 100 us -> 81.3 us (0.81)
  Pallas kernels: 0 us -> 26.6 us
  matrix products: 28.3 us -> 2.01 us
  other arithmetic: 8.91 us -> 28.8 us
  local copies, waits for them, and re-layouts: 25.5 us -> 6.02 us
  waiting for transfers between devices: 24 us -> 4.53 us
  between operations: 1.73 us -> 0.55 us
    pallas_call x0 -> x2, Pallas kernels: none -> 26.6 us  [the longest x1 15.1 us: moveout_stack(): pl.pallas_call(moveout_kernel, grid=(groups,), in_specs=[pl.BlockSpec((sl...]
    dot_general x6 -> x0, matrix products: 26.3 us -> none  [the longest x4 15.1 us: moveout(): jnp.einsum('sgw,gwc->sgc', window_rows, matrix, preferred_element_type=jn...]
    all_to_all x1, waiting for transfers between devices: 24 us -> 4.53 us  [body(): lax.all_to_all(send.reshape(dest_count, capacity, length + META), ('line'...]
    convert_element_type x0 -> x5, other arithmetic: none -> 12.6 us  [the longest x4 11.9 us: moveout_matrix(): return matrix.astype(jnp.bfloat16)]
    add x0 -> x1, other arithmetic: none -> 10.2 us  [bandpass_matrix(): matrix + jnp.where(position == column + 128 + tap_index - half, weights[t...]
    reshape x5 -> x0, local copies, waits for them, and re-layouts: 8.3 us -> none  [the longest x2 4.13 us: windows(): first = padded[:, :length].reshape(rows_count, groups, 128)]
    slice x5 -> x1, local copies, waits for them, and re-layouts: 8.2 us -> 0.03 us  [body(): band_shift[0, offset_index]]
    add x4, other arithmetic: 2.57 us -> 0.04 us  [moveout_matrix(): column + shifts + tap_index]
  transfers between devices with their start and end apart: 1 -> 1, of which waited for: 1 -> 1; matrix products, arithmetic and copies ran while one was open for 8% -> 33% of each run, Pallas kernels for 0% -> 0%
where the time goes in v2:
time: 81.3 us; the launch traced here: 80.4 us
  other arithmetic  28.8 us (35%)
  Pallas kernels  26.6 us (33%)
  starting transfers between devices  11.9 us (15%)
  local copies, waits for them, and re-layouts  6.02 us (7%)
  waiting for transfers between devices  4.53 us (6%)
  matrix products  2.01 us (2%)
    pallas_call x1, Pallas kernels, moveout_stack(): pl.pallas_call(moveout_kernel, grid=(groups,), in_specs=[pl.BlockSpec((sl...  15.1 us
    convert_element_type x4, other arithmetic, moveout_matrix(): return matrix.astype(jnp.bfloat16)  11.9 us
    all_to_all x1, starting transfers between devices, body(): lax.all_to_all(send.reshape(dest_count, capacity, length + META), ('line'...  11.9 us
    pallas_call x1, Pallas kernels, filter_stack(): pl.pallas_call(filter_kernel, grid=(groups,), in_specs=[pl.BlockSpec((bin...  11.5 us
    add x1, other arithmetic, bandpass_matrix(): matrix + jnp.where(position == column + 128 + tap_index - half, weights[t...  10.2 us
    all_to_all x1, waiting for transfers between devices, body(): lax.all_to_all(send.reshape(dest_count, capacity, length + META), ('line'...  4.53 us
    reshape x1, local copies, waits for them, and re-layouts, body(): received = lax.all_to_all(send.reshape(dest_count, capacity, length + MET...  2.58 us
    another operation x1, other arithmetic, body(): jnp.stack([moveout_matrix(nmo_coef[0, offset_index], band_shift[0, offset...  2.23 us
  transfers between devices with their start and end apart: 1, of which 1 were waited for; matrix products, arithmetic and copies ran while one was open for 33% of the time, Pallas kernels for 0%

profile of v2, /device:TPU:1, one launch (start us, length us, event | category | flops | bytes accessed | tf_op | source)
XLA Modules:
  0.0 80.4 jit_solution(8549734537181514942)
XLA Ops:
  0.0 0.0 copy-start
  0.0 0.7 fusion.10
  0.7 0.1 copy.10
  0.9 0.2 fusion.5
  1.2 0.0 copy-done
  1.2 0.1 broadcast_bitcast_fusion
  1.2 0.3 fusion.6
  1.5 2.0 %convolution_convert_fusion = bf16[512,2176]{1,0:T(8,128)(2,1)S(1)} fusion(bf16[256,128]{1,0:T(8,128)(2,1)S(1)} %get-tuple-element.113, bf16[256,2048]{1,0:T(8,128)(2,1)} %param.8, s32[256]{0:T(256)S(1)} %add_add_fusion), kind=kOutput, calls=%fused_computation | convolution fusion | flops 573898752 | bytes 3343360 | tf_op jit(solution)/shard_map/dot_general | solution.py:157
  3.6 2.1 %reshape.1927 = bf16[128,4,2176]{2,1,0:T(4,128)(2,1)} reshape(bf16[512,2176]{1,0:T(8,128)(2,1)S(1)} %convolution_convert_fusion) | data formatting | bytes 4456448 | tf_op jit(solution)/shard_map/reshape | solution.py:159
  5.7 11.9 %all-to-all-start = ((bf16[128,4,2176]{2,1,0:T(4,128)(2,1)}), bf16[128,4,2176]{2,1,0:T(4,128)(2,1)}, u32[]{:S(2)}, u32[]{:S(2)}) async-start(bf16[128,4,2176]{2,1,0:T(4,128)(2,1)} %reshape.1927), calls=%async_computation | async-start | bytes 4456448 | tf_op jit(solution)/shard_map/all_to_all | solution.py:158
  17.6 0.0 copy-done.2
  17.6 0.1 fusion.12
  17.7 0.1 fusion.13
  18.1 0.0 copy-done.3
  18.1 0.0 copy-done.4
  18.3 0.0 copy-done.5
  18.3 0.1 fusion.16
  18.4 0.1 fusion.14
  18.5 0.1 iota_compare_fusion.34
  18.6 0.1 iota_compare_fusion.36
  18.7 0.1 iota_compare_fusion.38
  18.7 0.1 iota_compare_fusion.40
  18.8 0.1 iota_compare_fusion.42
  18.9 0.1 iota_compare_fusion.44
  19.0 0.1 iota_compare_fusion.46
  19.0 0.1 iota_compare_fusion.48
  19.1 0.1 iota_compare_fusion.50
  19.2 0.1 iota_compare_fusion.52
  19.2 0.1 iota_compare_fusion.54
  19.3 0.1 iota_compare_fusion.56
  19.4 0.1 iota_compare_fusion.58
  19.4 0.1 iota_compare_fusion.60
  19.5 2.9 %add_convert_fusion = bf16[1,16,256,128]{3,2,1,0:T(8,128)(2,1)S(1)} fusion(f32[16,128]{1,0:T(8,128)S(1)} %bitcast.147, s32[16,128]{1,0:T(8,128)S(1)} %get-tuple-element.109, f32[16,128]{1,0:T(8,128)S(1)} %bitcast.146, s32[16,128]{1,0:T(8,128)S(1)} %get-tuple-element.108, f32[16,128]{1,0:T(8,128)S(1)} %bitcast.145, s32[16,128]{1,0:T(8,128)S(1)} %get-tuple-element.107, ...), kind=kLoop, calls=%fused_computation.3 | loop fusion | flops 12582912 | bytes 1179648 | tf_op jit(solution)/shard_map/convert_element_type | solution.py:22
  22.4 2.9 %add_convert_fusion.1 = bf16[1,16,256,128]{3,2,1,0:T(8,128)(2,1)S(1)} fusion(f32[16,128]{1,0:T(8,128)S(1)} %bitcast.134, s32[16,128]{1,0:T(8,128)S(1)} %get-tuple-element.101, f32[16,128]{1,0:T(8,128)S(1)} %bitcast.135, s32[16,128]{1,0:T(8,128)S(1)} %get-tuple-element.100, f32[16,128]{1,0:T(8,128)S(1)} %bitcast.136, s32[16,128]{1,0:T(8,128)S(1)} %get-tuple-element.99, ...), kind=kLoop, calls=%fused_computation.12 | loop fusion | flops 12582912 | bytes 1179648 | tf_op jit(solution)/shard_map/convert_element_type | solution.py:22
  25.4 2.9 %add_convert_fusion.2 = bf16[1,16,256,128]{3,2,1,0:T(8,128)(2,1)S(1)} fusion(f32[16,128]{1,0:T(8,128)S(1)} %bitcast.131, s32[16,128]{1,0:T(8,128)S(1)} %get-tuple-element.93, f32[16,128]{1,0:T(8,128)S(1)} %bitcast.130, s32[16,128]{1,0:T(8,128)S(1)} %get-tuple-element.92, f32[16,128]{1,0:T(8,128)S(1)} %bitcast.129, s32[16,128]{1,0:T(8,128)S(1)} %get-tuple-element.91, ...), kind=kLoop, calls=%fused_computation.21 | loop fusion | flops 12582912 | bytes 1179648 | tf_op jit(solution)/shard_map/convert_element_type | solution.py:22
  28.3 3.1 %add_convert_fusion.3 = bf16[1,16,256,128]{3,2,1,0:T(8,128)(2,1)S(1)} fusion(f32[16,128]{1,0:T(8,128)S(1)} %bitcast.118, s32[16,128]{1,0:T(8,128)S(1)} %get-tuple-element.85, f32[16,128]{1,0:T(8,128)S(1)} %bitcast.119, s32[16,128]{1,0:T(8,128)S(1)} %get-tuple-element.84, f32[16,128]{1,0:T(8,128)S(1)} %bitcast.120, s32[16,128]{1,0:T(8,128)S(1)} %get-tuple-element.83, ...), kind=kLoop, calls=%fused_computation.30 | loop fusion | flops 12582912 | bytes 1179648 | tf_op jit(solution)/shard_map/convert_element_type | solution.py:22
  31.4 2.2 %pad_maximum_fusion.matrix_ref = bf16[4,16,256,128]{3,2,1,0:T(8,128)(2,1)} fusion(bf16[1,16,256,128]{3,2,1,0:T(8,128)(2,1)S(1)} %add_convert_fusion, bf16[1,16,256,128]{3,2,1,0:T(8,128)(2,1)S(1)} %add_convert_fusion.1, bf16[1,16,256,128]{3,2,1,0:T(8,128)(2,1)S(1)} %add_convert_fusion.2, bf16[1,16,256,128]{3,2,1,0:T(8,128)(2,1)S(1)} %add_convert_fusion.3), kind=kLoop, calls=%fused_computation.1 | loop fusion | flops 6291456 | bytes 8388608 | tf_op jit(solution)/shard_map/stack | solution.py:172
  33.7 0.7 copy.12.fold_ref
  34.4 0.1 iota_compare_fusion.62
  34.5 10.2 %select_add_fusion.matrix_ref = f32[16,384,128]{2,1,0:T(8,128)} fusion(f32[16,128]{1,0:T(8,128)S(1)} %bitcast.115, f32[16,128]{1,0:T(8,128)S(1)} %bitcast.116, f32[16,128]{1,0:T(8,128)S(1)} %bitcast.87, f32[16,128]{1,0:T(8,128)S(1)} %bitcast.88, f32[16,128]{1,0:T(8,128)S(1)} %bitcast.89, f32[16,128]{1,0:T(8,128)S(1)} %bitcast.90, f32[16,128]{1,0:T(8,128)S(1)} %bitcast.91, ...), kind=kLoop, calls=%fused_computation.2 | loop fusion | flops 47972352 | bytes 4923392 | tf_op jit(solution)/shard_map/add | solution.py:34
  44.6 4.5 %all-to-all-done = bf16[128,4,2176]{2,1,0:T(4,128)(2,1)} async-done(((bf16[128,4,2176]{2,1,0:T(4,128)(2,1)}), bf16[128,4,2176]{2,1,0:T(4,128)(2,1)}, u32[]{:S(2)}, u32[]{:S(2)}) %all-to-all-start) | async-done | bytes 2228256 | tf_op jit(solution)/shard_map/all_to_all | solution.py:158
  49.2 2.6 %reshape.1928.rows_ref = bf16[512,2176]{1,0:T(8,128)(2,1)S(1)} reshape(bf16[128,4,2176]{2,1,0:T(4,128)(2,1)} %all-to-all-done) | data formatting | bytes 4456448 | tf_op jit(solution)/shard_map/reshape | solution.py:164
  51.8 0.0 copy-start.1
  51.8 0.2 fusion.3
  52.0 1.2 %slice_select_fusion.1.class_ref = s32[512,1]{1,0:T(8,128)} fusion(pred[512,1]{1,0:T(8,128)(4,1)S(1)} %get-tuple-element.6, s32[512,3]{1,0:T(8,128)S(1)} %slice_convert_fusion), kind=kLoop, calls=%fused_computation.45 | loop fusion | flops 512 | bytes 4608 | tf_op jit(solution)/shard_map/jit(_where)/select_n | solution.py:168
  53.2 0.6 fusion.8.select_ref
  53.8 15.1 %shard_map.82.stack_ref = f32[64,2048]{1,0:T(8,128)} custom-call(bf16[512,2176]{1,0:T(8,128)(2,1)} %copy-done.1, s32[512,1]{1,0:T(8,128)} %slice_select_fusion.1.class_ref, bf16[64,512]{1,0:T(8,128)(2,1)} %fusion.8.select_ref, bf16[4,16,256,128]{3,2,1,0:T(8,128)(2,1)} %pad_maximum_fusion.matrix_ref), custom_call_target="tpu_custom_call" | custom-call | tf_op jit(solution)/shard_map/pallas_call | solution.py:98
  68.9 11.5 %shard_map.83 = f32[64,2048]{1,0:T(8,128)} custom-call(f32[64,2048]{1,0:T(8,128)} %shard_map.82.stack_ref, f32[16,384,128]{2,1,0:T(8,128)} %select_add_fusion.matrix_ref, f32[64,1]{1,0:T(8,128)} %copy.12.fold_ref), custom_call_target="tpu_custom_call" | custom-call | tf_op jit(solution)/shard_map/pallas_call | solution.py:115
  (55 shorter events, 0.4 us)
Async XLA Ops:
  0.0 1.2 %copy-start = (s32[2]{0:T(128)S(1)}, s32[2]{0:T(128)}, u32[]{:S(2)}) copy-start(s32[2]{0:T(128)} %param.11) | copy-start | bytes 28
  5.7 11.9 %copy-start.2 = (f32[31,2048]{1,0:T(8,128)S(1)}, f32[31,2048]{1,0:T(8,128)}, u32[]{:S(2)}) copy-start(f32[31,2048]{1,0:T(8,128)} %param.14) | copy-start | bytes 761860
  5.7 12.4 %copy-start.3 = (bf16[1,4,8,2048]{3,2,1,0:T(8,128)(2,1)S(1)}, bf16[1,4,8,2048]{3,2,1,0:T(8,128)(2,1)}, u32[]{:S(2)}) copy-start(bf16[1,4,8,2048]{3,2,1,0:T(8,128)(2,1)} %param.12) | copy-start | bytes 393220
  5.7 12.5 %copy-start.4 = (s32[1,4,2048]{2,1,0:T(4,128)S(1)}, s32[1,4,2048]{2,1,0:T(4,128)}, u32[]{:S(2)}) copy-start(s32[1,4,2048]{2,1,0:T(4,128)} %param.13) | copy-start | bytes 98308
  5.7 12.6 %copy-start.5 = (s32[1,64]{1,0:T(1,128)S(1)}, s32[1,64]{1,0:T(1,128)}, u32[]{:S(2)}) copy-start(s32[1,64]{1,0:T(1,128)} %param.15) | copy-start | bytes 772
  5.7 43.5 %all-to-all-start = ((bf16[128,4,2176]{2,1,0:T(4,128)(2,1)}), bf16[128,4,2176]{2,1,0:T(4,128)(2,1)}, u32[]{:S(2)}, u32[]{:S(2)}) async-start(bf16[128,4,2176]{2,1,0:T(4,128)(2,1)} %reshape.1927), calls=%async_computation | async-start | bytes 4456448 | tf_op jit(solution)/shard_map/all_to_all | solution.py:158
  51.8 2.1 %copy-start.1 = (bf16[512,2176]{1,0:T(8,128)(2,1)}, bf16[512,2176]{1,0:T(8,128)(2,1)S(1)}, u32[]{:S(2)}) copy-start(bf16[512,2176]{1,0:T(8,128)(2,1)S(1)} %reshape.1928.rows_ref) | copy-start | bytes 6684676

commit v3 on v2

v3 whole, which is shorter than its diff:
```python
import jax
import jax.numpy as jnp
from jax import lax
from jax.sharding import PartitionSpec as P
from jax.experimental import pallas as pl
from jax.experimental.pallas import tpu as pltpu

META = 128


def moveout_matrix(coef_rows, shift_rows):
    taps_count = coef_rows.shape[0]
    groups = coef_rows.shape[1] // 128
    column = jnp.arange(128, dtype=jnp.int32).reshape(1, 1, 128)
    position = jnp.arange(256, dtype=jnp.int32).reshape(1, 256, 1)
    shifts = shift_rows.reshape(groups, 1, 128)
    weights = coef_rows.astype(jnp.float32).reshape(taps_count, groups, 1, 128)
    matrix = jnp.zeros((groups, 256, 128), jnp.float32)
    for tap_index in range(taps_count):
        matrix = matrix + jnp.where(
            position == column + shifts + tap_index, weights[tap_index], 0.0
        )
    return matrix.astype(jnp.bfloat16)


def split3(value):
    high = value.astype(jnp.bfloat16)
    rest = value - high.astype(jnp.float32)
    middle = rest.astype(jnp.bfloat16)
    low = (rest - middle.astype(jnp.float32)).astype(jnp.bfloat16)
    return high, middle, low


def moveout_kernel(rows_ref, class_ref, select_ref, matrix_ref, taps_ref, fold_ref, out_ref, stack_ref):
    step = pl.program_id(0)
    per_step = matrix_ref.shape[1]
    bins, length = out_ref.shape
    taps_count = taps_ref.shape[0]
    half = (taps_count - 1) // 2

    @pl.when(step == 0)
    def _():
        stack_ref[:, :128] = jnp.zeros((bins, 128), jnp.float32)
        stack_ref[:, length + 128:] = jnp.zeros((bins, 128), jnp.float32)

    slot_class = class_ref[...]
    select = select_ref[...]
    for inner in range(per_step):
        start = pl.multiple_of((step * per_step + inner) * 128, 128)
        window = rows_ref[:, pl.ds(start, 256)]
        lanes = start + lax.broadcasted_iota(jnp.int32, (1, 256), 1)
        window = jnp.where(lanes < length, window, jnp.zeros((), window.dtype))
        corrected = jnp.zeros((window.shape[0], 128), jnp.float32)
        for offset_index in range(matrix_ref.shape[0]):
            product = jnp.dot(
                window, matrix_ref[offset_index, inner], preferred_element_type=jnp.float32
            )
            corrected = corrected + jnp.where(slot_class == offset_index, product, 0.0)
        total = None
        for part in split3(corrected):
            piece = jnp.dot(select, part, preferred_element_type=jnp.float32)
            total = piece if total is None else total + piece
        stack_ref[:, pl.ds(start + 128, 128)] = total

    @pl.when(step == pl.num_programs(0) - 1)
    def _():
        width = length + 256
        for row in range(bins // 8):
            rows_now = stack_ref[row * 8:(row + 1) * 8, :]
            filtered = jnp.zeros((8, length), jnp.float32)
            for tap_index in range(taps_count):
                shift = (-(128 + tap_index - half)) % width
                moved = pltpu.roll(rows_now, shift, 1)[:, :length]
                filtered = filtered + taps_ref[tap_index:tap_index + 1, :] * moved
            out_ref[row * 8:(row + 1) * 8, :] = filtered / fold_ref[row * 8:(row + 1) * 8, :]


def moveout_stack(rows, slot_class, select, matrices, taps, fold_share, length):
    slot_count, width = rows.shape
    bins = select.shape[0]
    classes, groups = matrices.shape[0], matrices.shape[1]
    per_step = 4
    return pl.pallas_call(
        moveout_kernel,
        grid=(groups // per_step,),
        in_specs=[
            pl.BlockSpec((slot_count, width), lambda g: (0, 0)),
            pl.BlockSpec((slot_count, 1), lambda g: (0, 0)),
            pl.BlockSpec((bins, slot_count), lambda g: (0, 0)),
            pl.BlockSpec((classes, per_step, 256, 128), lambda g: (0, g, 0, 0)),
            pl.BlockSpec(taps.shape, lambda g: (0, 0)),
            pl.BlockSpec((bins, 1), lambda g: (0, 0)),
        ],
        out_specs=pl.BlockSpec((bins, length), lambda g: (0, 0)),
        out_shape=jax.ShapeDtypeStruct((bins, length), jnp.float32),
        scratch_shapes=[pltpu.VMEM((bins, length + 256), jnp.float32)],
    )(rows, slot_class, select, matrices, taps, fold_share)


def ranks(keys, key_count):
    onehot = (keys[:, None] == jnp.arange(key_count, dtype=jnp.int32)[None, :]).astype(jnp.int32)
    running = jnp.cumsum(onehot, 0)
    return jnp.sum(onehot * running, 1) - 1


def body(traces, trace_line, trace_bin, block_offset, nmo_coef, band_shift, bandpass, fold):
    line_count = lax.axis_size("line")
    tile_count = lax.axis_size("tile")
    trace_count, length = traces.shape
    block_rows = trace_count // block_offset.shape[0]
    bin_share = fold.shape[1]
    dest_count = line_count * tile_count
    capacity = 4
    slots = dest_count * capacity
    trace_class = jnp.repeat(block_offset, block_rows)
    trace_tile = trace_bin // bin_share
    dest = trace_line * tile_count + trace_tile
    slot_of_trace = dest * capacity + ranks(dest, dest_count)
    lane = jnp.arange(META, dtype=jnp.int32)[None, :]
    meta_block = jnp.where(
        lane == 0,
        (trace_bin % bin_share)[:, None],
        jnp.where(lane == 1, trace_class[:, None], jnp.where(lane == 2, 1, 0)),
    ).astype(jnp.bfloat16)
    extended = jnp.concatenate([traces, meta_block], 1)
    select = (
        jnp.arange(slots, dtype=jnp.int32)[:, None] == slot_of_trace[None, :]
    ).astype(jnp.bfloat16)
    send = jnp.dot(select, extended, preferred_element_type=jnp.float32).astype(jnp.bfloat16)
    received = lax.all_to_all(
        send.reshape(dest_count, capacity, length + META),
        ("line", "tile"),
        split_axis=0,
        concat_axis=0,
        tiled=True,
    ).reshape(slots, length + META)
    meta = received[:, length:length + 3].astype(jnp.int32)
    valid = meta[:, 2] == 1
    slot_bin = jnp.where(valid, meta[:, 0], -1)
    slot_class = jnp.where(valid, meta[:, 1], -1)
    select = (jnp.arange(bin_share, dtype=jnp.int32)[:, None] == slot_bin[None, :]).astype(
        jnp.bfloat16
    )
    matrices = jnp.stack(
        [
            moveout_matrix(nmo_coef[0, offset_index], band_shift[0, offset_index])
            for offset_index in range(nmo_coef.shape[1])
        ]
    )
    fold_share = fold[0].astype(jnp.float32)[:, None]
    filtered = moveout_stack(
        received, slot_class[:, None], select, matrices, bandpass, fold_share, length
    )
    return filtered[None]


def solution(mesh):
    placed = (
        P(("line", "tile"), None),
        P(("line", "tile")),
        P(("line", "tile")),
        P(("line", "tile")),
        P("line", None, None, None),
        P("line", None, None),
        P(),
        P("line", "tile"),
    )
    return jax.shard_map(
        body, mesh=mesh, in_specs=placed, out_specs=P("line", "tile", None), check_vma=False
    )
```

time: 81.3 us -> 70.2 us (0.86)
  waiting for transfers between devices: 4.53 us -> 16.3 us
  other arithmetic: 28.8 us -> 17.6 us
  Pallas kernels: 26.6 us -> 16 us
    all_to_all x1, waiting for transfers between devices: 4.53 us -> 16.3 us  [body(): lax.all_to_all(send.reshape(dest_count, capacity, length + META), ('line'...]
    pallas_call x2 -> x1, Pallas kernels: 26.6 us -> 16 us  [moveout_stack(): pl.pallas_call(moveout_kernel, grid=(groups // per_step,), in_specs=[pl.B...]
    add x1 -> x0, other arithmetic: 10.2 us -> none  [bandpass_matrix(): matrix + jnp.where(position == column + 128 + tap_index - half, weights[t...]
    eq x16 -> x0, other arithmetic: 0.98 us -> none  [bandpass_matrix(): position == column + 128 + tap_index - half]
  transfers between devices with their start and end apart: 1 -> 1, of which waited for: 1 -> 1; matrix products, arithmetic and copies ran while one was open for 33% -> 22% of each run, Pallas kernels for 0% -> 0%
where the time goes in v3:
time: 70.2 us; the launch traced here: 69.9 us
  other arithmetic  17.6 us (25%)
  waiting for transfers between devices  16.3 us (23%)
  Pallas kernels  16 us (23%)
  starting transfers between devices  11.9 us (17%)
  local copies, waits for them, and re-layouts  5.9 us (8%)
  matrix products  2.01 us (3%)
    all_to_all x1, waiting for transfers between devices, body(): lax.all_to_all(send.reshape(dest_count, capacity, length + META), ('line'...  16.3 us
    pallas_call x1, Pallas kernels, moveout_stack(): pl.pallas_call(moveout_kernel, grid=(groups // per_step,), in_specs=[pl.B...  16 us
    convert_element_type x4, other arithmetic, moveout_matrix(): return matrix.astype(jnp.bfloat16)  11.9 us
    all_to_all x1, starting transfers between devices, body(): lax.all_to_all(send.reshape(dest_count, capacity, length + META), ('line'...  11.9 us
    reshape x1, local copies, waits for them, and re-layouts, body(): received = lax.all_to_all(send.reshape(dest_count, capacity, length + MET...  2.58 us
    another operation x1, other arithmetic, body(): jnp.stack([moveout_matrix(nmo_coef[0, offset_index], band_shift[0, offset...  2.24 us
    reshape x1, local copies, waits for them, and re-layouts, body(): send.reshape(dest_count, capacity, length + META)  2.16 us
    dot_general x1, matrix products, body(): jnp.dot(select, extended, preferred_element_type=jnp.float32)  2.01 us
  transfers between devices with their start and end apart: 1, of which 1 were waited for; matrix products, arithmetic and copies ran while one was open for 22% of the time, Pallas kernels for 0%

profile of v3, /device:TPU:1, one launch (start us, length us, event | category | flops | bytes accessed | tf_op | source)
XLA Modules:
  0.0 69.9 jit_solution(14642997283626655433)
XLA Ops:
  0.0 0.0 copy-start
  0.0 0.7 %fusion.10 = (s32[256]{0:T(256)S(1)}, s32[256]{0:T(256)S(1)}) fusion(s32[256]{0:T(256)} %param.10, s32[256]{0:T(256)} %param.9), kind=kLoop, calls=%fused_computation.101 | loop fusion | flops 5376 | bytes 4096 | tf_op jit(solution)/shard_map/add | solution.py:117
  0.7 0.1 copy.10
  0.9 0.2 fusion.5
  1.2 0.0 copy-done
  1.2 0.1 broadcast_bitcast_fusion
  1.2 0.3 fusion.6
  1.5 2.0 %convolution_convert_fusion = bf16[512,2176]{1,0:T(8,128)(2,1)S(1)} fusion(bf16[256,128]{1,0:T(8,128)(2,1)S(1)} %get-tuple-element.82, bf16[256,2048]{1,0:T(8,128)(2,1)} %param.8, s32[256]{0:T(256)S(1)} %add_add_fusion), kind=kOutput, calls=%fused_computation | convolution fusion | flops 573898752 | bytes 3343360 | tf_op jit(solution)/shard_map/dot_general | solution.py:129
  3.6 2.2 %reshape.930 = bf16[128,4,2176]{2,1,0:T(4,128)(2,1)} reshape(bf16[512,2176]{1,0:T(8,128)(2,1)S(1)} %convolution_convert_fusion) | data formatting | bytes 4456448 | tf_op jit(solution)/shard_map/reshape | solution.py:131
  5.7 0.0 copy-start.2
  5.7 0.0 copy-start.3
  5.7 11.9 %all-to-all-start = ((bf16[128,4,2176]{2,1,0:T(4,128)(2,1)}), bf16[128,4,2176]{2,1,0:T(4,128)(2,1)}, u32[]{:S(2)}, u32[]{:S(2)}) async-start(bf16[128,4,2176]{2,1,0:T(4,128)(2,1)} %reshape.930), calls=%async_computation | async-start | bytes 4456448 | tf_op jit(solution)/shard_map/all_to_all | solution.py:130
  17.6 0.0 copy-done.2
  17.6 0.0 copy-start.4
  17.7 0.0 copy-done.3
  17.8 0.1 fusion.14
  17.9 0.1 fusion.12
  18.0 2.9 %add_convert_fusion = bf16[1,16,256,128]{3,2,1,0:T(8,128)(2,1)S(1)} fusion(f32[16,128]{1,0:T(8,128)S(1)} %bitcast.85, s32[16,128]{1,0:T(8,128)S(1)} %get-tuple-element.78, f32[16,128]{1,0:T(8,128)S(1)} %bitcast.84, s32[16,128]{1,0:T(8,128)S(1)} %get-tuple-element.77, f32[16,128]{1,0:T(8,128)S(1)} %bitcast.83, s32[16,128]{1,0:T(8,128)S(1)} %get-tuple-element.76, ...), kind=kLoop, calls=%fused_computation.2 | loop fusion | flops 12582912 | bytes 1179648 | tf_op jit(solution)/shard_map/convert_element_type | solution.py:23
  20.9 0.0 copy-done.4
  20.9 0.7 %copy.12.fold_ref = f32[64,1]{1,0:T(8,128)} copy(f32[64,1]{0,1:T(1,128)S(1)} %convert_bitcast_fusion) | data formatting | bytes 512 | tf_op jit(solution)/shard_map/convert_element_type | solution.py:150
  21.7 2.9 %add_convert_fusion.1 = bf16[1,16,256,128]{3,2,1,0:T(8,128)(2,1)S(1)} fusion(f32[16,128]{1,0:T(8,128)S(1)} %bitcast.72, s32[16,128]{1,0:T(8,128)S(1)} %get-tuple-element.70, f32[16,128]{1,0:T(8,128)S(1)} %bitcast.73, s32[16,128]{1,0:T(8,128)S(1)} %get-tuple-element.69, f32[16,128]{1,0:T(8,128)S(1)} %bitcast.74, s32[16,128]{1,0:T(8,128)S(1)} %get-tuple-element.68, ...), kind=kLoop, calls=%fused_computation.11 | loop fusion | flops 12582912 | bytes 1179648 | tf_op jit(solution)/shard_map/convert_element_type | solution.py:23
  24.6 2.9 %add_convert_fusion.2 = bf16[1,16,256,128]{3,2,1,0:T(8,128)(2,1)S(1)} fusion(f32[16,128]{1,0:T(8,128)S(1)} %bitcast.69, s32[16,128]{1,0:T(8,128)S(1)} %get-tuple-element.62, f32[16,128]{1,0:T(8,128)S(1)} %bitcast.68, s32[16,128]{1,0:T(8,128)S(1)} %get-tuple-element.61, f32[16,128]{1,0:T(8,128)S(1)} %bitcast.67, s32[16,128]{1,0:T(8,128)S(1)} %get-tuple-element.60, ...), kind=kLoop, calls=%fused_computation.20 | loop fusion | flops 12582912 | bytes 1179648 | tf_op jit(solution)/shard_map/convert_element_type | solution.py:23
  27.5 3.1 %add_convert_fusion.3 = bf16[1,16,256,128]{3,2,1,0:T(8,128)(2,1)S(1)} fusion(f32[16,128]{1,0:T(8,128)S(1)} %bitcast.56, s32[16,128]{1,0:T(8,128)S(1)} %get-tuple-element.54, f32[16,128]{1,0:T(8,128)S(1)} %bitcast.57, s32[16,128]{1,0:T(8,128)S(1)} %get-tuple-element.53, f32[16,128]{1,0:T(8,128)S(1)} %bitcast.58, s32[16,128]{1,0:T(8,128)S(1)} %get-tuple-element.52, ...), kind=kLoop, calls=%fused_computation.29 | loop fusion | flops 12582912 | bytes 1179648 | tf_op jit(solution)/shard_map/convert_element_type | solution.py:23
  30.6 2.2 %pad_maximum_fusion.matrix_ref = bf16[4,16,256,128]{3,2,1,0:T(8,128)(2,1)} fusion(bf16[1,16,256,128]{3,2,1,0:T(8,128)(2,1)S(1)} %add_convert_fusion, bf16[1,16,256,128]{3,2,1,0:T(8,128)(2,1)S(1)} %add_convert_fusion.1, bf16[1,16,256,128]{3,2,1,0:T(8,128)(2,1)S(1)} %add_convert_fusion.2, bf16[1,16,256,128]{3,2,1,0:T(8,128)(2,1)S(1)} %add_convert_fusion.3), kind=kLoop, calls=%fused_computation.1 | loop fusion | flops 6291456 | bytes 8388608 | tf_op jit(solution)/shard_map/stack | solution.py:144
  32.9 16.3 %all-to-all-done = bf16[128,4,2176]{2,1,0:T(4,128)(2,1)} async-done(((bf16[128,4,2176]{2,1,0:T(4,128)(2,1)}), bf16[128,4,2176]{2,1,0:T(4,128)(2,1)}, u32[]{:S(2)}, u32[]{:S(2)}) %all-to-all-start) | async-done | bytes 2228256 | tf_op jit(solution)/shard_map/all_to_all | solution.py:130
  49.2 2.6 %reshape.931.rows_ref = bf16[512,2176]{1,0:T(8,128)(2,1)S(1)} reshape(bf16[128,4,2176]{2,1,0:T(4,128)(2,1)} %all-to-all-done) | data formatting | bytes 4456448 | tf_op jit(solution)/shard_map/reshape | solution.py:136
  51.8 0.0 copy-start.1
  51.9 0.2 fusion.3
  52.1 1.2 %slice_select_fusion.1.class_ref = s32[512,1]{1,0:T(8,128)} fusion(pred[512,1]{1,0:T(8,128)(4,1)S(1)} %get-tuple-element.6, s32[512,3]{1,0:T(8,128)S(1)} %slice_convert_fusion), kind=kLoop, calls=%fused_computation.44 | loop fusion | flops 512 | bytes 4608 | tf_op jit(solution)/shard_map/jit(_where)/select_n | solution.py:140
  53.3 0.6 fusion.8.select_ref
  53.9 0.0 copy-done.1
  53.9 16.0 %shard_map.82 = f32[64,2048]{1,0:T(8,128)} custom-call(bf16[512,2176]{1,0:T(8,128)(2,1)} %copy-done.1, s32[512,1]{1,0:T(8,128)} %slice_select_fusion.1.class_ref, bf16[64,512]{1,0:T(8,128)(2,1)} %fusion.8.select_ref, bf16[4,16,256,128]{3,2,1,0:T(8,128)(2,1)} %pad_maximum_fusion.matrix_ref, f32[31,2048]{1,0:T(8,128)} %taps_ref.1, f32[64,1]{1,0:T(8,128)} %copy.12.fold_ref), custom_call_target="tpu_custom_call" | custom-call | tf_op jit(solution)/shard_map/pallas_call | solution.py:83
  (18 shorter events, 0.2 us)
Async XLA Ops:
  0.0 1.2 %copy-start = (s32[2]{0:T(128)S(1)}, s32[2]{0:T(128)}, u32[]{:S(2)}) copy-start(s32[2]{0:T(128)} %param.11) | copy-start | bytes 28
  5.7 11.9 %copy-start.2 = (bf16[1,4,8,2048]{3,2,1,0:T(8,128)(2,1)S(1)}, bf16[1,4,8,2048]{3,2,1,0:T(8,128)(2,1)}, u32[]{:S(2)}) copy-start(bf16[1,4,8,2048]{3,2,1,0:T(8,128)(2,1)} %param.12) | copy-start | bytes 393220
  5.7 12.0 %copy-start.3 = (s32[1,4,2048]{2,1,0:T(4,128)S(1)}, s32[1,4,2048]{2,1,0:T(4,128)}, u32[]{:S(2)}) copy-start(s32[1,4,2048]{2,1,0:T(4,128)} %param.13) | copy-start | bytes 98308
  5.7 43.5 %all-to-all-start = ((bf16[128,4,2176]{2,1,0:T(4,128)(2,1)}), bf16[128,4,2176]{2,1,0:T(4,128)(2,1)}, u32[]{:S(2)}, u32[]{:S(2)}) async-start(bf16[128,4,2176]{2,1,0:T(4,128)(2,1)} %reshape.930), calls=%async_computation | async-start | bytes 4456448 | tf_op jit(solution)/shard_map/all_to_all | solution.py:130
  17.6 3.3 %copy-start.4 = (s32[1,64]{1,0:T(1,128)S(1)}, s32[1,64]{1,0:T(1,128)}, u32[]{:S(2)}) copy-start(s32[1,64]{1,0:T(1,128)} %param.15) | copy-start | bytes 772
  51.8 2.1 %copy-start.1 = (bf16[512,2176]{1,0:T(8,128)(2,1)}, bf16[512,2176]{1,0:T(8,128)(2,1)S(1)}, u32[]{:S(2)}) copy-start(bf16[512,2176]{1,0:T(8,128)(2,1)S(1)} %reshape.931.rows_ref) | copy-start | bytes 6684676

commit v4 on v3

--- a/solution.py
+++ b/solution.py
@@ -23,18 +23,11 @@
     return matrix.astype(jnp.bfloat16)
 
 
-def split3(value):
-    high = value.astype(jnp.bfloat16)
-    rest = value - high.astype(jnp.float32)
-    middle = rest.astype(jnp.bfloat16)
-    low = (rest - middle.astype(jnp.float32)).astype(jnp.bfloat16)
-    return high, middle, low
-
-
-def moveout_kernel(rows_ref, class_ref, select_ref, matrix_ref, taps_ref, fold_ref, out_ref, stack_ref):
+def moveout_kernel(rows_ref, matrix_ref, taps_ref, fold_ref, out_ref, part_ref, stack_ref):
     step = pl.program_id(0)
-    per_step = matrix_ref.shape[1]
+    classes, per_step = matrix_ref.shape[0], matrix_ref.shape[1]
     bins, length = out_ref.shape
+    slot_count, width = rows_ref.shape
     taps_count = taps_ref.shape[0]
     half = (taps_count - 1) // 2
 
@@ -42,42 +35,49 @@
     def _():
         stack_ref[:, :128] = jnp.zeros((bins, 128), jnp.float32)
         stack_ref[:, length + 128:] = jnp.zeros((bins, 128), jnp.float32)
+        meta = rows_ref[:, length:].astype(jnp.float32).T
+        key = jnp.where(meta[2:3, :] == 1.0, meta[1:2, :] * bins + meta[0:1, :], -1.0)
+        keys = lax.broadcasted_iota(jnp.int32, (classes * bins, slot_count), 0).astype(jnp.float32)
+        select = (keys == key).astype(jnp.bfloat16)
+        summed = jnp.dot(select, rows_ref[:, :length], preferred_element_type=jnp.float32)
+        high = summed.astype(jnp.bfloat16)
+        middle = (summed - high.astype(jnp.float32)).astype(jnp.bfloat16)
+        for offset_index in range(classes):
+            base = offset_index * 2 * bins
+            part_ref[base:base + bins, :length] = high[offset_index * bins:(offset_index + 1) * bins]
+            part_ref[base + bins:base + 2 * bins, :length] = middle[
+                offset_index * bins:(offset_index + 1) * bins
+            ]
+        part_ref[:, length:] = jnp.zeros((classes * 2 * bins, width - length), jnp.bfloat16)
 
-    slot_class = class_ref[...]
-    select = select_ref[...]
     for inner in range(per_step):
         start = pl.multiple_of((step * per_step + inner) * 128, 128)
-        window = rows_ref[:, pl.ds(start, 256)]
-        lanes = start + lax.broadcasted_iota(jnp.int32, (1, 256), 1)
-        window = jnp.where(lanes < length, window, jnp.zeros((), window.dtype))
-        corrected = jnp.zeros((window.shape[0], 128), jnp.float32)
-        for offset_index in range(matrix_ref.shape[0]):
+        total = jnp.zeros((bins, 128), jnp.float32)
+        for offset_index in range(classes):
+            base = offset_index * 2 * bins
+            window = part_ref[base:base + 2 * bins, pl.ds(start, 256)]
             product = jnp.dot(
                 window, matrix_ref[offset_index, inner], preferred_element_type=jnp.float32
             )
-            corrected = corrected + jnp.where(slot_class == offset_index, product, 0.0)
-        total = None
-        for part in split3(corrected):
-            piece = jnp.dot(select, part, preferred_element_type=jnp.float32)
-            total = piece if total is None else total + piece
+            total = total + product[:bins] + product[bins:]
         stack_ref[:, pl.ds(start + 128, 128)] = total
 
     @pl.when(step == pl.num_programs(0) - 1)
     def _():
-        width = length + 256
+        span = length + 256
         for row in range(bins // 8):
             rows_now = stack_ref[row * 8:(row + 1) * 8, :]
             filtered = jnp.zeros((8, length), jnp.float32)
             for tap_index in range(taps_count):
-                shift = (-(128 + tap_index - half)) % width
+                shift = (-(128 + tap_index - half)) % span
                 moved = pltpu.roll(rows_now, shift, 1)[:, :length]
                 filtered = filtered + taps_ref[tap_index:tap_index + 1, :] * moved
             out_ref[row * 8:(row + 1) * 8, :] = filtered / fold_ref[row * 8:(row + 1) * 8, :]
 
 
-def moveout_stack(rows, slot_class, select, matrices, taps, fold_share, length):
+def moveout_stack(rows, matrices, taps, fold_share, length):
     slot_count, width = rows.shape
-    bins = select.shape[0]
+    bins = fold_share.shape[0]
     classes, groups = matrices.shape[0], matrices.shape[1]
     per_step = 4
     return pl.pallas_call(
@@ -85,16 +85,17 @@
         grid=(groups // per_step,),
         in_specs=[
             pl.BlockSpec((slot_count, width), lambda g: (0, 0)),
-            pl.BlockSpec((slot_count, 1), lambda g: (0, 0)),
-            pl.BlockSpec((bins, slot_count), lambda g: (0, 0)),
             pl.BlockSpec((classes, per_step, 256, 128), lambda g: (0, g, 0, 0)),
             pl.BlockSpec(taps.shape, lambda g: (0, 0)),
             pl.BlockSpec((bins, 1), lambda g: (0, 0)),
         ],
         out_specs=pl.BlockSpec((bins, length), lambda g: (0, 0)),
         out_shape=jax.ShapeDtypeStruct((bins, length), jnp.float32),
-        scratch_shapes=[pltpu.VMEM((bins, length + 256), jnp.float32)],
-    )(rows, slot_class, select, matrices, taps, fold_share)
+        scratch_shapes=[
+            pltpu.VMEM((classes * 2 * bins, width), jnp.bfloat16),
+            pltpu.VMEM((bins, length + 256), jnp.float32),
+        ],
+    )(rows, matrices, taps, fold_share)
 
 
 def ranks(keys, key_count):
@@ -134,13 +135,6 @@
         concat_axis=0,
         tiled=True,
     ).reshape(slots, length + META)
-    meta = received[:, length:length + 3].astype(jnp.int32)
-    valid = meta[:, 2] == 1
-    slot_bin = jnp.where(valid, meta[:, 0], -1)
-    slot_class = jnp.where(valid, meta[:, 1], -1)
-    select = (jnp.arange(bin_share, dtype=jnp.int32)[:, None] == slot_bin[None, :]).astype(
-        jnp.bfloat16
-    )
     matrices = jnp.stack(
         [
             moveout_matrix(nmo_coef[0, offset_index], band_shift[0, offset_index])
@@ -148,9 +142,7 @@
         ]
     )
     fold_share = fold[0].astype(jnp.float32)[:, None]
-    filtered = moveout_stack(
-        received, slot_class[:, None], select, matrices, bandpass, fold_share, length
-    )
+    filtered = moveout_stack(received, matrices, bandpass, fold_share, length)
     return filtered[None]
 
 

time: 70.2 us -> 62.4 us (0.89)
  Pallas kernels: 16 us -> 10.9 us
  waiting for transfers between devices: 16.3 us -> 14.1 us
  other arithmetic: 17.6 us -> 16.8 us
    pallas_call x1, Pallas kernels: 16 us -> 10.9 us  [moveout_stack(): pl.pallas_call(moveout_kernel, grid=(groups // per_step,), in_specs=[pl.B...]
    all_to_all x1, waiting for transfers between devices: 16.3 us -> 14.1 us  [body(): lax.all_to_all(send.reshape(dest_count, capacity, length + META), ('line'...]
    select_n x2 -> x0, other arithmetic: 1.43 us -> none  [the longest x1 1.2 us: body(): slot_class = jnp.where(valid, meta[:, 1], -1)]
  transfers between devices with their start and end apart: 1 -> 1, of which waited for: 1 -> 1; matrix products, arithmetic and copies ran while one was open for 22% -> 28% of each run, Pallas kernels for 0% -> 0%
where the time goes in v4:
time: 62.4 us; the launch traced here: 62 us
  other arithmetic  16.8 us (27%)
  waiting for transfers between devices  14.1 us (23%)
  starting transfers between devices  11.5 us (18%)
  Pallas kernels  10.9 us (17%)
  local copies, waits for them, and re-layouts  6.55 us (10%)
  matrix products  2.01 us (3%)
    all_to_all x1, waiting for transfers between devices, body(): lax.all_to_all(send.reshape(dest_count, capacity, length + META), ('line'...  14.1 us
    convert_element_type x4, other arithmetic, moveout_matrix(): return matrix.astype(jnp.bfloat16)  12.6 us
    all_to_all x1, starting transfers between devices, body(): lax.all_to_all(send.reshape(dest_count, capacity, length + META), ('line'...  11.5 us
    pallas_call x1, Pallas kernels, moveout_stack(): pl.pallas_call(moveout_kernel, grid=(groups // per_step,), in_specs=[pl.B...  10.9 us
    another operation x1, other arithmetic, body(): jnp.stack([moveout_matrix(nmo_coef[0, offset_index], band_shift[0, offset...  2.22 us
    reshape x1, local copies, waits for them, and re-layouts, body(): send.reshape(dest_count, capacity, length + META)  2.13 us
    reshape x1, local copies, waits for them, and re-layouts, body(): received = lax.all_to_all(send.reshape(dest_count, capacity, length + MET...  2.1 us
    dot_general x1, matrix products, body(): jnp.dot(select, extended, preferred_element_type=jnp.float32)  2.01 us
  transfers between devices with their start and end apart: 1, of which 1 were waited for; matrix products, arithmetic and copies ran while one was open for 28% of the time, Pallas kernels for 0%

profile of v4, /device:TPU:1, one launch (start us, length us, event | category | flops | bytes accessed | tf_op | source)
XLA Modules:
  0.0 62.0 jit_solution(13053118269013620595)
XLA Ops:
  0.0 0.0 copy-start
  0.0 0.7 %fusion.8 = (s32[256]{0:T(256)S(1)}, s32[256]{0:T(256)S(1)}) fusion(s32[256]{0:T(256)} %param.10, s32[256]{0:T(256)} %param.9), kind=kLoop, calls=%fused_computation.94 | loop fusion | flops 5376 | bytes 4096 | tf_op jit(solution)/shard_map/add | solution.py:118
  0.7 0.1 copy.10
  0.9 0.2 fusion.4
  1.2 0.0 copy-done
  1.2 0.1 broadcast_bitcast_fusion
  1.2 0.3 fusion.5
  1.5 2.0 %convolution_convert_fusion = bf16[512,2176]{1,0:T(8,128)(2,1)S(1)} fusion(bf16[256,128]{1,0:T(8,128)(2,1)S(1)} %get-tuple-element.80, bf16[256,2048]{1,0:T(8,128)(2,1)} %param.8, s32[256]{0:T(256)S(1)} %add_add_fusion), kind=kOutput, calls=%fused_computation | convolution fusion | flops 573898752 | bytes 3343360 | tf_op jit(solution)/shard_map/dot_general | solution.py:130
  3.6 2.1 %reshape.916 = bf16[128,4,2176]{2,1,0:T(4,128)(2,1)} reshape(bf16[512,2176]{1,0:T(8,128)(2,1)S(1)} %convolution_convert_fusion) | data formatting | bytes 4456448 | tf_op jit(solution)/shard_map/reshape | solution.py:132
  5.7 0.0 copy-start.1
  5.7 0.0 copy-start.2
  5.7 11.5 %all-to-all-start = ((bf16[128,4,2176]{2,1,0:T(4,128)(2,1)}), bf16[128,4,2176]{2,1,0:T(4,128)(2,1)S(1)}, u32[]{:S(2)}, u32[]{:S(2)}) async-start(bf16[128,4,2176]{2,1,0:T(4,128)(2,1)} %reshape.916), calls=%async_computation | async-start | bytes 4456448 | tf_op jit(solution)/shard_map/all_to_all | solution.py:131
  17.2 0.0 copy-done.1
  17.2 0.0 copy-start.3
  17.2 0.0 copy-done.2
  17.3 0.6 fusion.14
  17.9 0.7 %fusion.12 = (f32[1,1,1,2048]{3,2,1,0:T(1,128)S(1)}, f32[1,1,1,2048]{3,2,1,0:T(1,128)}, f32[1,1,1,2048]{3,2,1,0:T(1,128)}, f32[1,1,1,2048]{3,2,1,0:T(1,128)}, f3...) fusion(f32[1,1,8,2048]{3,2,1,0:T(8,128)S(1)} %get-tuple-element, ...), kind=kLoop, calls=%fused_computation.106 | loop fusion | bytes 262144 | tf_op jit(solution)/shard_map/slice | solution.py:21
  18.6 0.1 fusion.10
  18.7 2.9 %add_convert_fusion = bf16[1,16,256,128]{3,2,1,0:T(8,128)(2,1)S(1)} fusion(f32[16,128]{1,0:T(8,128)S(1)} %bitcast.85, s32[16,128]{1,0:T(8,128)S(1)} %get-tuple-element.76, f32[16,128]{1,0:T(8,128)S(1)} %bitcast.84, s32[16,128]{1,0:T(8,128)S(1)} %get-tuple-element.75, f32[16,128]{1,0:T(8,128)S(1)} %bitcast.83, s32[16,128]{1,0:T(8,128)S(1)} %get-tuple-element.74, ...), kind=kLoop, calls=%fused_computation.2 | loop fusion | flops 12582912 | bytes 1179648 | tf_op jit(solution)/shard_map/convert_element_type | solution.py:23
  21.6 0.0 copy-done.3
  21.7 0.7 %copy.12.fold_ref = f32[64,1]{1,0:T(8,128)} copy(f32[64,1]{0,1:T(1,128)S(1)} %convert_bitcast_fusion) | data formatting | bytes 512 | tf_op jit(solution)/shard_map/convert_element_type | solution.py:144
  22.4 0.7 %iota_add_fusion.3 = (s32[16,128]{1,0:T(8,128)S(1)}, s32[16,128]{1,0:T(8,128)S(1)}, s32[16,128]{1,0:T(8,128)S(1)}, s32[16,128]{1,0:T(8,128)S(1)}, s32[16,128]{1,...) fusion(s32[16,128]{1,0:T(8,128)} %bitcast.87), kind=kLoop, calls=%fused_computation.59 | loop fusion | flops 16384 | bytes 73728 | tf_op jit(solution)/shard_map/add | solution.py:21
  23.1 3.6 %add_convert_fusion.1 = bf16[1,16,256,128]{3,2,1,0:T(8,128)(2,1)S(1)} fusion(f32[16,128]{1,0:T(8,128)} %bitcast.72, s32[16,128]{1,0:T(8,128)S(1)} %get-tuple-element.68, f32[16,128]{1,0:T(8,128)} %bitcast.73, s32[16,128]{1,0:T(8,128)S(1)} %get-tuple-element.67, f32[16,128]{1,0:T(8,128)} %bitcast.74, s32[16,128]{1,0:T(8,128)S(1)} %get-tuple-element.66, ...), kind=kLoop, calls=%fused_computation.11 | loop fusion | flops 12582912 | bytes 1179648 | tf_op jit(solution)/shard_map/convert_element_type | solution.py:23
  26.7 2.9 %add_convert_fusion.2 = bf16[1,16,256,128]{3,2,1,0:T(8,128)(2,1)S(1)} fusion(f32[16,128]{1,0:T(8,128)S(1)} %bitcast.69, s32[16,128]{1,0:T(8,128)S(1)} %get-tuple-element.60, f32[16,128]{1,0:T(8,128)S(1)} %bitcast.68, s32[16,128]{1,0:T(8,128)S(1)} %get-tuple-element.59, f32[16,128]{1,0:T(8,128)S(1)} %bitcast.67, s32[16,128]{1,0:T(8,128)S(1)} %get-tuple-element.58, ...), kind=kLoop, calls=%fused_computation.20 | loop fusion | flops 12582912 | bytes 1179648 | tf_op jit(solution)/shard_map/convert_element_type | solution.py:23
  29.6 3.1 %add_convert_fusion.3 = bf16[1,16,256,128]{3,2,1,0:T(8,128)(2,1)S(1)} fusion(f32[16,128]{1,0:T(8,128)S(1)} %bitcast.56, s32[16,128]{1,0:T(8,128)S(1)} %get-tuple-element.52, f32[16,128]{1,0:T(8,128)S(1)} %bitcast.57, s32[16,128]{1,0:T(8,128)S(1)} %get-tuple-element.51, f32[16,128]{1,0:T(8,128)S(1)} %bitcast.58, s32[16,128]{1,0:T(8,128)S(1)} %get-tuple-element.50, ...), kind=kLoop, calls=%fused_computation.29 | loop fusion | flops 12582912 | bytes 1179648 | tf_op jit(solution)/shard_map/convert_element_type | solution.py:23
  32.7 2.2 %pad_maximum_fusion.matrix_ref = bf16[4,16,256,128]{3,2,1,0:T(8,128)(2,1)} fusion(bf16[1,16,256,128]{3,2,1,0:T(8,128)(2,1)S(1)} %add_convert_fusion, bf16[1,16,256,128]{3,2,1,0:T(8,128)(2,1)S(1)} %add_convert_fusion.1, bf16[1,16,256,128]{3,2,1,0:T(8,128)(2,1)S(1)} %add_convert_fusion.2, bf16[1,16,256,128]{3,2,1,0:T(8,128)(2,1)S(1)} %add_convert_fusion.3), kind=kLoop, calls=%fused_computation.1 | loop fusion | flops 6291456 | bytes 8388608 | tf_op jit(solution)/shard_map/stack | solution.py:138
  34.9 14.1 %all-to-all-done = bf16[128,4,2176]{2,1,0:T(4,128)(2,1)S(1)} async-done(((bf16[128,4,2176]{2,1,0:T(4,128)(2,1)}), bf16[128,4,2176]{2,1,0:T(4,128)(2,1)S(1)}, u32[]{:S(2)}, u32[]{:S(2)}) %all-to-all-start) | async-done | bytes 2228256 | tf_op jit(solution)/shard_map/all_to_all | solution.py:131
  49.1 2.1 %reshape.917.rows_ref = bf16[512,2176]{1,0:T(8,128)(2,1)} reshape(bf16[128,4,2176]{2,1,0:T(4,128)(2,1)S(1)} %all-to-all-done) | data formatting | bytes 4456448 | tf_op jit(solution)/shard_map/reshape | solution.py:137
  51.2 10.9 %shard_map.82 = f32[64,2048]{1,0:T(8,128)} custom-call(bf16[512,2176]{1,0:T(8,128)(2,1)} %reshape.917.rows_ref, bf16[4,16,256,128]{3,2,1,0:T(8,128)(2,1)} %pad_maximum_fusion.matrix_ref, f32[31,2048]{1,0:T(8,128)} %taps_ref.1, f32[64,1]{1,0:T(8,128)} %copy.12.fold_ref), custom_call_target="tpu_custom_call" | custom-call | tf_op jit(solution)/shard_map/pallas_call | solution.py:83
  (15 shorter events, 0.1 us)
Async XLA Ops:
  0.0 1.2 %copy-start = (s32[2]{0:T(128)S(1)}, s32[2]{0:T(128)}, u32[]{:S(2)}) copy-start(s32[2]{0:T(128)} %param.11) | copy-start | bytes 28
  5.7 11.5 %copy-start.1 = (bf16[1,4,8,2048]{3,2,1,0:T(8,128)(2,1)S(1)}, bf16[1,4,8,2048]{3,2,1,0:T(8,128)(2,1)}, u32[]{:S(2)}) copy-start(bf16[1,4,8,2048]{3,2,1,0:T(8,128)(2,1)} %param.12) | copy-start | bytes 393220
  5.7 11.6 %copy-start.2 = (s32[1,4,2048]{2,1,0:T(4,128)S(1)}, s32[1,4,2048]{2,1,0:T(4,128)}, u32[]{:S(2)}) copy-start(s32[1,4,2048]{2,1,0:T(4,128)} %param.13) | copy-start | bytes 98308
  5.7 43.4 %all-to-all-start = ((bf16[128,4,2176]{2,1,0:T(4,128)(2,1)}), bf16[128,4,2176]{2,1,0:T(4,128)(2,1)S(1)}, u32[]{:S(2)}, u32[]{:S(2)}) async-start(bf16[128,4,2176]{2,1,0:T(4,128)(2,1)} %reshape.916), calls=%async_computation | async-start | bytes 4456448 | tf_op jit(solution)/shard_map/all_to_all | solution.py:131
  17.2 4.4 %copy-start.3 = (s32[1,64]{1,0:T(1,128)S(1)}, s32[1,64]{1,0:T(1,128)}, u32[]{:S(2)}) copy-start(s32[1,64]{1,0:T(1,128)} %param.15) | copy-start | bytes 772

commit v5 on v4

--- a/solution.py
+++ b/solution.py
@@ -27,7 +27,8 @@
     step = pl.program_id(0)
     classes, per_step = matrix_ref.shape[0], matrix_ref.shape[1]
     bins, length = out_ref.shape
-    slot_count, width = rows_ref.shape
+    sources, capacity, width = rows_ref.shape
+    slot_count = sources * capacity
     taps_count = taps_ref.shape[0]
     half = (taps_count - 1) // 2
 
@@ -35,11 +36,12 @@
     def _():
         stack_ref[:, :128] = jnp.zeros((bins, 128), jnp.float32)
         stack_ref[:, length + 128:] = jnp.zeros((bins, 128), jnp.float32)
-        meta = rows_ref[:, length:].astype(jnp.float32).T
+        rows_all = rows_ref[...].reshape(slot_count, width)
+        meta = rows_all[:, length:].astype(jnp.float32).T
         key = jnp.where(meta[2:3, :] == 1.0, meta[1:2, :] * bins + meta[0:1, :], -1.0)
         keys = lax.broadcasted_iota(jnp.int32, (classes * bins, slot_count), 0).astype(jnp.float32)
         select = (keys == key).astype(jnp.bfloat16)
-        summed = jnp.dot(select, rows_ref[:, :length], preferred_element_type=jnp.float32)
+        summed = jnp.dot(select, rows_all[:, :length], preferred_element_type=jnp.float32)
         high = summed.astype(jnp.bfloat16)
         middle = (summed - high.astype(jnp.float32)).astype(jnp.bfloat16)
         for offset_index in range(classes):
@@ -76,7 +78,7 @@
 
 
 def moveout_stack(rows, matrices, taps, fold_share, length):
-    slot_count, width = rows.shape
+    sources, capacity, width = rows.shape
     bins = fold_share.shape[0]
     classes, groups = matrices.shape[0], matrices.shape[1]
     per_step = 4
@@ -84,7 +86,7 @@
         moveout_kernel,
         grid=(groups // per_step,),
         in_specs=[
-            pl.BlockSpec((slot_count, width), lambda g: (0, 0)),
+            pl.BlockSpec((sources, capacity, width), lambda g: (0, 0, 0)),
             pl.BlockSpec((classes, per_step, 256, 128), lambda g: (0, g, 0, 0)),
             pl.BlockSpec(taps.shape, lambda g: (0, 0)),
             pl.BlockSpec((bins, 1), lambda g: (0, 0)),
@@ -96,6 +98,27 @@
             pltpu.VMEM((bins, length + 256), jnp.float32),
         ],
     )(rows, matrices, taps, fold_share)
+
+
+def send_kernel(slot_ref, traces_ref, meta_ref, out_ref):
+    dests, capacity, width = out_ref.shape
+    trace_count, length = traces_ref.shape
+    slots = dests * capacity
+    wanted = lax.broadcasted_iota(jnp.int32, (slots, trace_count), 0)
+    select = (wanted == slot_ref[...]).astype(jnp.bfloat16)
+    rows = jnp.dot(select, traces_ref[...], preferred_element_type=jnp.float32)
+    meta = jnp.dot(select, meta_ref[...], preferred_element_type=jnp.float32)
+    out_ref[:, :, :length] = rows.astype(jnp.bfloat16).reshape(dests, capacity, length)
+    out_ref[:, :, length:] = meta.astype(jnp.bfloat16).reshape(dests, capacity, width - length)
+
+
+def build_send(slot_of_trace, traces, meta_block, dests, capacity):
+    trace_count, length = traces.shape
+    width = length + meta_block.shape[1]
+    return pl.pallas_call(
+        send_kernel,
+        out_shape=jax.ShapeDtypeStruct((dests, capacity, width), jnp.bfloat16),
+    )(slot_of_trace[None, :], traces, meta_block)
 
 
 def ranks(keys, key_count):
@@ -123,18 +146,14 @@
         (trace_bin % bin_share)[:, None],
         jnp.where(lane == 1, trace_class[:, None], jnp.where(lane == 2, 1, 0)),
     ).astype(jnp.bfloat16)
-    extended = jnp.concatenate([traces, meta_block], 1)
-    select = (
-        jnp.arange(slots, dtype=jnp.int32)[:, None] == slot_of_trace[None, :]
-    ).astype(jnp.bfloat16)
-    send = jnp.dot(select, extended, preferred_element_type=jnp.float32).astype(jnp.bfloat16)
+    send = build_send(slot_of_trace, traces, meta_block, dest_count, capacity)
     received = lax.all_to_all(
-        send.reshape(dest_count, capacity, length + META),
+        send,
         ("line", "tile"),
         split_axis=0,
         concat_axis=0,
         tiled=True,
-    ).reshape(slots, length + META)
+    )
     matrices = jnp.stack(
         [
             moveout_matrix(nmo_coef[0, offset_index], band_shift[0, offset_index])

time: 62.4 us -> 62.2 us (level)
  Pallas kernels: 10.9 us -> 14.3 us
  local copies, waits for them, and re-layouts: 6.55 us -> 3.73 us
  matrix products: 2.01 us -> 0 us
  other arithmetic: 16.8 us -> 18 us
    reshape x2 -> x0, local copies, waits for them, and re-layouts: 4.23 us -> none  [the longest x1 2.13 us: body(): send.reshape(dest_count, capacity, length + META)]
    pallas_call x0 -> x1, Pallas kernels: none -> 3.41 us  [build_send(): pl.pallas_call(send_kernel, out_shape=jax.ShapeDtypeStruct((dests, capaci...]
    dot_general x1 -> x0, matrix products: 2.01 us -> none  [body(): jnp.dot(select, extended, preferred_element_type=jnp.float32)]
    unnamed x9 -> x11, local copies, waits for them, and re-layouts: 0.02 us -> 1.42 us
    add x1 -> x0, other arithmetic: 0.71 us -> none  [body(): dest = trace_line * tile_count + trace_tile]
    select_n x0 -> x1, other arithmetic: none -> 0.71 us  [body(): trace_bin % bin_share]
    reduce_sum x1, other arithmetic: 0.28 us -> 0.91 us  [ranks(): return jnp.sum(onehot * running, 1) - 1]
  transfers between devices with their start and end apart: 1 -> 1, of which waited for: 1 -> 1; matrix products, arithmetic and copies ran while one was open for 28% -> 29% of each run, Pallas kernels for 0% -> 0%
where the time goes in v5:
time: 62.2 us; the launch traced here: 61.9 us
  other arithmetic  18 us (29%)
  Pallas kernels  14.3 us (23%)
  waiting for transfers between devices  14.1 us (23%)
  starting transfers between devices  11.5 us (18%)
  local copies, waits for them, and re-layouts  3.73 us (6%)
    all_to_all x1, waiting for transfers between devices, body(): lax.all_to_all(send, ('line', 'tile'), split_axis=0, concat_axis=0, tiled...  14.1 us
    convert_element_type x4, other arithmetic, moveout_matrix(): return matrix.astype(jnp.bfloat16)  12.6 us
    all_to_all x1, starting transfers between devices, body(): lax.all_to_all(send, ('line', 'tile'), split_axis=0, concat_axis=0, tiled...  11.5 us
    pallas_call x1, Pallas kernels, moveout_stack(): pl.pallas_call(moveout_kernel, grid=(groups // per_step,), in_specs=[pl.B...  10.9 us
    pallas_call x1, Pallas kernels, build_send(): pl.pallas_call(send_kernel, out_shape=jax.ShapeDtypeStruct((dests, capaci...  3.41 us
    another operation x1, other arithmetic, body(): jnp.stack([moveout_matrix(nmo_coef[0, offset_index], band_shift[0, offset...  2.2 us
    unnamed x11, local copies, waits for them, and re-layouts  1.42 us
  transfers between devices with their start and end apart: 1, of which 1 were waited for; matrix products, arithmetic and copies ran while one was open for 29% of the time, Pallas kernels for 0%

profile of v5, /device:TPU:1, one launch (start us, length us, event | category | flops | bytes accessed | tf_op | source)
XLA Modules:
  0.0 61.9 jit_solution(2715146123845024084)
XLA Ops:
  0.0 0.0 copy-start
  0.0 0.7 %and_select_fusion = (s32[256]{0:T(256)S(1)}, s32[256]{0:T(256)S(1)}) fusion(s32[256]{0:T(256)} %param.10, s32[256]{0:T(256)} %param.9), kind=kLoop, calls=%fused_computation.83 | loop fusion | flops 5376 | bytes 4096 | tf_op jit(solution)/shard_map/jit(remainder)/select_n | solution.py:146
  0.7 0.1 copy.10
  0.9 0.2 fusion
  1.2 0.0 copy-done
  1.2 0.1 broadcast_bitcast_fusion
  1.2 0.9 %fusion.1 = (s32[256]{0:T(256)S(1)}, bf16[256,128]{1,0:T(8,128)(2,1)}) fusion(s32[128,2,128]{0,2,1:T(8,128)S(1)} %copy.11, s32[256]{0:T(256)S(1)} %get-tuple-element.78, s32[128]{0:T(128)S(1)} %compare_select_fusion, s32[256]{0:T(256)S(1)} %broadcast_bitcast_fusion, pred[128]{0:T(512)(128)(4,1)S(1)} %iota_compare_fusion.33, s32[256]{0:T(256)S(1)} %get-tuple-element.77, ...), kind=kLoop, calls=%fused_computation.40 | loop fusion | flops 196352 | bytes 201472 | tf_op jit(solution)/shard_map/reduce_sum | solution.py:127
  2.2 0.6 add_add_fusion
  2.7 3.4 %shard_map.82 = bf16[128,4,2176]{2,1,0:T(4,128)(2,1)} custom-call(s32[1,256]{1,0:T(1,128)} %bitcast.94, bf16[256,2048]{1,0:T(8,128)(2,1)} %traces_ref.1, bf16[256,128]{1,0:T(8,128)(2,1)} %get-tuple-element.80.meta_ref), custom_call_target="tpu_custom_call" | custom-call | tf_op jit(solution)/shard_map/pallas_call | solution.py:118
  6.2 0.0 copy-start.2
  6.2 0.0 copy-start.3
  6.2 11.5 %all-to-all-start = ((bf16[128,4,2176]{2,1,0:T(4,128)(2,1)}), bf16[128,4,2176]{2,1,0:T(4,128)(2,1)S(1)}, u32[]{:S(2)}, u32[]{:S(2)}) async-start(bf16[128,4,2176]{2,1,0:T(4,128)(2,1)} %shard_map.82), calls=%async_computation | async-start | bytes 4456448 | tf_op jit(solution)/shard_map/all_to_all | solution.py:150
  17.7 0.0 copy-done.2
  17.7 0.0 copy-start.4
  17.7 0.0 copy-done.3
  17.7 0.6 %fusion.9 = (s32[1,1,2048]{2,1,0:T(1,128)S(1)}, s32[1,1,2048]{2,1,0:T(1,128)S(1)}, s32[1,1,2048]{2,1,0:T(1,128)}, s32[1,1,2048]{2,1,0:T(1,128)S(1)}) fusion(s32[1,4,2048]{2,1,0:T(4,128)S(1)} %copy-done.3), kind=kLoop, calls=%fused_computation.101 | loop fusion | bytes 65536 | tf_op jit(solution)/shard_map/slice | solution.py:159
  18.4 0.7 %fusion.5 = (f32[1,1,1,2048]{3,2,1,0:T(1,128)S(1)}, f32[1,1,1,2048]{3,2,1,0:T(1,128)S(1)}, f32[1,1,1,2048]{3,2,1,0:T(1,128)S(1)}, f32[1,1,1,2048]{3,2,1,0:T(1,12...) fusion(f32[1,1,8,2048]{3,2,1,0:T(8,128)S(1)} %get-tuple-element, ...), kind=kLoop, calls=%fused_computation.97 | loop fusion | bytes 262144 | tf_op jit(solution)/shard_map/slice | solution.py:21
  19.1 0.1 fusion.7
  19.2 2.9 %add_convert_fusion.3 = bf16[1,16,256,128]{3,2,1,0:T(8,128)(2,1)S(1)} fusion(f32[16,128]{1,0:T(8,128)S(1)} %bitcast.81, s32[16,128]{1,0:T(8,128)S(1)} %get-tuple-element.52, f32[16,128]{1,0:T(8,128)S(1)} %bitcast.82, s32[16,128]{1,0:T(8,128)S(1)} %get-tuple-element.51, f32[16,128]{1,0:T(8,128)S(1)} %bitcast.83, s32[16,128]{1,0:T(8,128)S(1)} %get-tuple-element.50, ...), kind=kLoop, calls=%fused_computation.28 | loop fusion | flops 12582912 | bytes 1179648 | tf_op jit(solution)/shard_map/convert_element_type | solution.py:23
  22.1 0.0 copy-done.4
  22.1 0.7 %copy.12.fold_ref = f32[64,1]{1,0:T(8,128)} copy(f32[64,1]{0,1:T(1,128)S(1)} %convert_bitcast_fusion) | data formatting | bytes 512 | tf_op jit(solution)/shard_map/convert_element_type | solution.py:163
  22.8 0.7 %iota_add_fusion = (s32[16,128]{1,0:T(8,128)S(1)}, s32[16,128]{1,0:T(8,128)S(1)}, s32[16,128]{1,0:T(8,128)S(1)}, s32[16,128]{1,0:T(8,128)S(1)}, s32[16,128]{1,0:...) fusion(s32[16,128]{1,0:T(8,128)} %bitcast.88), kind=kLoop, calls=%fused_computation.50 | loop fusion | flops 16384 | bytes 73728 | tf_op jit(solution)/shard_map/add | solution.py:21
  23.5 3.6 %add_convert_fusion.2 = bf16[1,16,256,128]{3,2,1,0:T(8,128)(2,1)S(1)} fusion(f32[16,128]{1,0:T(8,128)} %bitcast.78, s32[16,128]{1,0:T(8,128)S(1)} %get-tuple-element.60, f32[16,128]{1,0:T(8,128)} %bitcast.77, s32[16,128]{1,0:T(8,128)S(1)} %get-tuple-element.59, f32[16,128]{1,0:T(8,128)} %bitcast.76, s32[16,128]{1,0:T(8,128)S(1)} %get-tuple-element.58, ...), kind=kLoop, calls=%fused_computation.19 | loop fusion | flops 12582912 | bytes 1179648 | tf_op jit(solution)/shard_map/convert_element_type | solution.py:23
  27.2 2.9 %add_convert_fusion.1 = bf16[1,16,256,128]{3,2,1,0:T(8,128)(2,1)S(1)} fusion(f32[16,128]{1,0:T(8,128)S(1)} %bitcast.65, s32[16,128]{1,0:T(8,128)S(1)} %get-tuple-element.68, f32[16,128]{1,0:T(8,128)S(1)} %bitcast.66, s32[16,128]{1,0:T(8,128)S(1)} %get-tuple-element.67, f32[16,128]{1,0:T(8,128)S(1)} %bitcast.67, s32[16,128]{1,0:T(8,128)S(1)} %get-tuple-element.66, ...), kind=kLoop, calls=%fused_computation.10 | loop fusion | flops 12582912 | bytes 1179648 | tf_op jit(solution)/shard_map/convert_element_type | solution.py:23
  30.1 3.1 %add_convert_fusion = bf16[1,16,256,128]{3,2,1,0:T(8,128)(2,1)S(1)} fusion(f32[16,128]{1,0:T(8,128)S(1)} %bitcast.62, s32[16,128]{1,0:T(8,128)S(1)} %get-tuple-element.76, f32[16,128]{1,0:T(8,128)S(1)} %bitcast.61, s32[16,128]{1,0:T(8,128)S(1)} %get-tuple-element.75, f32[16,128]{1,0:T(8,128)S(1)} %bitcast.60, s32[16,128]{1,0:T(8,128)S(1)} %get-tuple-element.74, ...), kind=kLoop, calls=%fused_computation.1 | loop fusion | flops 12582912 | bytes 1179648 | tf_op jit(solution)/shard_map/convert_element_type | solution.py:23
  33.2 2.2 %pad_maximum_fusion.matrix_ref = bf16[4,16,256,128]{3,2,1,0:T(8,128)(2,1)} fusion(bf16[1,16,256,128]{3,2,1,0:T(8,128)(2,1)S(1)} %add_convert_fusion, bf16[1,16,256,128]{3,2,1,0:T(8,128)(2,1)S(1)} %add_convert_fusion.1, bf16[1,16,256,128]{3,2,1,0:T(8,128)(2,1)S(1)} %add_convert_fusion.2, bf16[1,16,256,128]{3,2,1,0:T(8,128)(2,1)S(1)} %add_convert_fusion.3), kind=kLoop, calls=%fused_computation | loop fusion | flops 6291456 | bytes 8388608 | tf_op jit(solution)/shard_map/stack | solution.py:157
  35.4 14.1 %all-to-all-done.rows_ref = bf16[128,4,2176]{2,1,0:T(4,128)(2,1)S(1)} async-done(((bf16[128,4,2176]{2,1,0:T(4,128)(2,1)}), bf16[128,4,2176]{2,1,0:T(4,128)(2,1)S(1)}, u32[]{:S(2)}, u32[]{:S(2)}) %all-to-all-start) | async-done | bytes 2228256 | tf_op jit(solution)/shard_map/all_to_all | solution.py:150
  49.5 0.0 copy-start.1
  49.6 1.4 %copy-done.1 = bf16[128,4,2176]{2,1,0:T(4,128)(2,1)} copy-done((bf16[128,4,2176]{2,1,0:T(4,128)(2,1)}, bf16[128,4,2176]{2,1,0:T(4,128)(2,1)S(1)}, u32[]{:S(2)}) %copy-start.1) | copy-done | bytes 2228248
  50.9 10.9 %shard_map.83 = f32[64,2048]{1,0:T(8,128)} custom-call(bf16[128,4,2176]{2,1,0:T(4,128)(2,1)} %copy-done.1, bf16[4,16,256,128]{3,2,1,0:T(8,128)(2,1)} %pad_maximum_fusion.matrix_ref, f32[31,2048]{1,0:T(8,128)} %taps_ref.1, f32[64,1]{1,0:T(8,128)} %copy.12.fold_ref), custom_call_target="tpu_custom_call" | custom-call | tf_op jit(solution)/shard_map/pallas_call | solution.py:85
  (14 shorter events, 0.1 us)
Async XLA Ops:
  0.0 1.2 %copy-start = (s32[2]{0:T(128)S(1)}, s32[2]{0:T(128)}, u32[]{:S(2)}) copy-start(s32[2]{0:T(128)} %param.11) | copy-start | bytes 28
  6.2 11.5 %copy-start.2 = (bf16[1,4,8,2048]{3,2,1,0:T(8,128)(2,1)S(1)}, bf16[1,4,8,2048]{3,2,1,0:T(8,128)(2,1)}, u32[]{:S(2)}) copy-start(bf16[1,4,8,2048]{3,2,1,0:T(8,128)(2,1)} %param.12) | copy-start | bytes 393220
  6.2 11.6 %copy-start.3 = (s32[1,4,2048]{2,1,0:T(4,128)S(1)}, s32[1,4,2048]{2,1,0:T(4,128)}, u32[]{:S(2)}) copy-start(s32[1,4,2048]{2,1,0:T(4,128)} %param.13) | copy-start | bytes 98308
  6.2 43.4 %all-to-all-start = ((bf16[128,4,2176]{2,1,0:T(4,128)(2,1)}), bf16[128,4,2176]{2,1,0:T(4,128)(2,1)S(1)}, u32[]{:S(2)}, u32[]{:S(2)}) async-start(bf16[128,4,2176]{2,1,0:T(4,128)(2,1)} %shard_map.82), calls=%async_computation | async-start | bytes 4456448 | tf_op jit(solution)/shard_map/all_to_all | solution.py:150
  17.7 4.4 %copy-start.4 = (s32[1,64]{1,0:T(1,128)S(1)}, s32[1,64]{1,0:T(1,128)}, u32[]{:S(2)}) copy-start(s32[1,64]{1,0:T(1,128)} %param.15) | copy-start | bytes 772
  49.5 1.4 %copy-start.1 = (bf16[128,4,2176]{2,1,0:T(4,128)(2,1)}, bf16[128,4,2176]{2,1,0:T(4,128)(2,1)S(1)}, u32[]{:S(2)}) copy-start(bf16[128,4,2176]{2,1,0:T(4,128)(2,1)S(1)} %all-to-all-done.rows_ref) | copy-start | bytes 6684676

commit v6 on v5

--- a/solution.py
+++ b/solution.py
@@ -1,3 +1,5 @@
+import functools
+
 import jax
 import jax.numpy as jnp
 from jax import lax
@@ -100,31 +102,39 @@
     )(rows, matrices, taps, fold_share)
 
 
-def send_kernel(slot_ref, traces_ref, meta_ref, out_ref):
+def send_kernel(ids_ref, traces_ref, out_ref, *, bins, tiles):
     dests, capacity, width = out_ref.shape
     trace_count, length = traces_ref.shape
     slots = dests * capacity
-    wanted = lax.broadcasted_iota(jnp.int32, (slots, trace_count), 0)
-    select = (wanted == slot_ref[...]).astype(jnp.bfloat16)
+    ids = ids_ref[...]
+    line_id, bin_id, class_id = ids[:, 0:1], ids[:, 1:2], ids[:, 2:3]
+    dest = line_id * tiles + bin_id // bins
+    onehot = (dest == lax.broadcasted_iota(jnp.int32, (trace_count, dests), 1)).astype(jnp.bfloat16)
+    row = lax.broadcasted_iota(jnp.int32, (trace_count, trace_count), 0)
+    col = lax.broadcasted_iota(jnp.int32, (trace_count, trace_count), 1)
+    lower = (col <= row).astype(jnp.bfloat16)
+    running = jnp.dot(lower, onehot, preferred_element_type=jnp.float32)
+    rank = jnp.sum(running * onehot.astype(jnp.float32), axis=1, keepdims=True) - 1.0
+    slot = dest.astype(jnp.float32) * capacity + rank
+    wanted = lax.broadcasted_iota(jnp.int32, (trace_count, slots), 1).astype(jnp.float32)
+    select = (wanted == slot).astype(jnp.float32).T.astype(jnp.bfloat16)
+    lane = lax.broadcasted_iota(jnp.int32, (trace_count, width - length), 1)
+    meta = jnp.where(
+        lane == 0, bin_id % bins, jnp.where(lane == 1, class_id, jnp.where(lane == 2, 1, 0))
+    ).astype(jnp.bfloat16)
     rows = jnp.dot(select, traces_ref[...], preferred_element_type=jnp.float32)
-    meta = jnp.dot(select, meta_ref[...], preferred_element_type=jnp.float32)
+    meta_rows = jnp.dot(select, meta, preferred_element_type=jnp.float32)
     out_ref[:, :, :length] = rows.astype(jnp.bfloat16).reshape(dests, capacity, length)
-    out_ref[:, :, length:] = meta.astype(jnp.bfloat16).reshape(dests, capacity, width - length)
+    out_ref[:, :, length:] = meta_rows.astype(jnp.bfloat16).reshape(dests, capacity, width - length)
 
 
-def build_send(slot_of_trace, traces, meta_block, dests, capacity):
+def build_send(ids, traces, dests, capacity, bins, tiles):
     trace_count, length = traces.shape
-    width = length + meta_block.shape[1]
+    width = length + META
     return pl.pallas_call(
-        send_kernel,
+        functools.partial(send_kernel, bins=bins, tiles=tiles),
         out_shape=jax.ShapeDtypeStruct((dests, capacity, width), jnp.bfloat16),
-    )(slot_of_trace[None, :], traces, meta_block)
-
-
-def ranks(keys, key_count):
-    onehot = (keys[:, None] == jnp.arange(key_count, dtype=jnp.int32)[None, :]).astype(jnp.int32)
-    running = jnp.cumsum(onehot, 0)
-    return jnp.sum(onehot * running, 1) - 1
+    )(ids, traces)
 
 
 def body(traces, trace_line, trace_bin, block_offset, nmo_coef, band_shift, bandpass, fold):
@@ -137,16 +147,8 @@
     capacity = 4
     slots = dest_count * capacity
     trace_class = jnp.repeat(block_offset, block_rows)
-    trace_tile = trace_bin // bin_share
-    dest = trace_line * tile_count + trace_tile
-    slot_of_trace = dest * capacity + ranks(dest, dest_count)
-    lane = jnp.arange(META, dtype=jnp.int32)[None, :]
-    meta_block = jnp.where(
-        lane == 0,
-        (trace_bin % bin_share)[:, None],
-        jnp.where(lane == 1, trace_class[:, None], jnp.where(lane == 2, 1, 0)),
-    ).astype(jnp.bfloat16)
-    send = build_send(slot_of_trace, traces, meta_block, dest_count, capacity)
+    ids = jnp.stack([trace_line, trace_bin, trace_class], axis=1)
+    send = build_send(ids, traces, dest_count, capacity, bin_share, tile_count)
     received = lax.all_to_all(
         send,
         ("line", "tile"),

time: 62.2 us -> 62.3 us (level)
  local copies, waits for them, and re-layouts: 3.73 us -> 5.71 us
  other arithmetic: 18 us -> 16.8 us
  waiting for transfers between devices: 14.1 us -> 12.9 us
  Pallas kernels: 14.3 us -> 15 us
    all_to_all x1, waiting for transfers between devices: 14.1 us -> 12.9 us  [body(): lax.all_to_all(send, ('line', 'tile'), split_axis=0, concat_axis=0, tiled...]
    reduce_sum x1 -> x0, other arithmetic: 0.91 us -> none  [ranks(): return jnp.sum(onehot * running, 1) - 1]
    another operation x3 -> x1, local copies, waits for them, and re-layouts: 0.02 us -> 0.8 us  [body(): ids = jnp.stack([trace_line, trace_bin, trace_class], axis=1)]
    select_n x2 -> x0, other arithmetic: 0.71 us -> none  [the longest x1 0.71 us: body(): trace_bin % bin_share]
    convert_element_type x1, local copies, waits for them, and re-layouts: 0.7 us -> 1.36 us  [body(): fold_share = fold[0].astype(jnp.float32)[:, None]]
    broadcast_in_dim x1, local copies, waits for them, and re-layouts: 0.07 us -> 0.72 us  [body(): trace_class = jnp.repeat(block_offset, block_rows)]
    pallas_call x1, Pallas kernels: 3.41 us -> 4.06 us  [build_send(): pl.pallas_call(functools.partial(send_kernel, bins=bins, tiles=tiles), ou...]
    unnamed x11 -> x8, local copies, waits for them, and re-layouts: 1.42 us -> 1.4 us
  transfers between devices with their start and end apart: 1 -> 1, of which waited for: 1 -> 1; matrix products, arithmetic and copies ran while one was open for 29% -> 30% of each run, Pallas kernels for 0% -> 0%
where the time goes in v6:
time: 62.3 us; the launch traced here: 62 us
  other arithmetic  16.8 us (27%)
  Pallas kernels  15 us (24%)
  waiting for transfers between devices  12.9 us (21%)
  starting transfers between devices  11.5 us (18%)
  local copies, waits for them, and re-layouts  5.71 us (9%)
    all_to_all x1, waiting for transfers between devices, body(): lax.all_to_all(send, ('line', 'tile'), split_axis=0, concat_axis=0, tiled...  12.9 us
    convert_element_type x4, other arithmetic, moveout_matrix(): return matrix.astype(jnp.bfloat16)  12.6 us
    all_to_all x1, starting transfers between devices, body(): lax.all_to_all(send, ('line', 'tile'), split_axis=0, concat_axis=0, tiled...  11.5 us
    pallas_call x1, Pallas kernels, moveout_stack(): pl.pallas_call(moveout_kernel, grid=(groups // per_step,), in_specs=[pl.B...  10.9 us
    pallas_call x1, Pallas kernels, build_send(): pl.pallas_call(functools.partial(send_kernel, bins=bins, tiles=tiles), ou...  4.06 us
    another operation x1, other arithmetic, body(): jnp.stack([moveout_matrix(nmo_coef[0, offset_index], band_shift[0, offset...  2.21 us
    unnamed x8, local copies, waits for them, and re-layouts  1.4 us
    convert_element_type x1, local copies, waits for them, and re-layouts, body(): fold_share = fold[0].astype(jnp.float32)[:, None]  1.36 us
  transfers between devices with their start and end apart: 1, of which 1 were waited for; matrix products, arithmetic and copies ran while one was open for 30% of the time, Pallas kernels for 0%

profile of v6, /device:TPU:1, one launch (start us, length us, event | category | flops | bytes accessed | tf_op | source)
XLA Modules:
  0.0 62.0 jit_solution(10239178748172784159)
XLA Ops:
  0.0 0.7 %broadcast_in_dim.269 = s32[2,128]{1,0:T(2,128)S(1)} broadcast(s32[2]{0:T(128)} %param.11), dimensions={0} | broadcast | bytes 1032 | tf_op jit(solution)/shard_map/broadcast_in_dim | solution.py:149
  0.7 0.7 %pad_add_fusion = s32[256,3]{0,1:T(4,128)S(1)} fusion(s32[256,1]{0,1:T(1,128)S(1)} %bitcast.80, s32[256,1]{0,1:T(1,128)} %bitcast.78, s32[256,1]{0,1:T(1,128)} %bitcast.79), kind=kLoop, calls=%fused_computation.45 | loop fusion | flops 1536 | bytes 6144 | tf_op jit(solution)/shard_map/stack | solution.py:150
  1.4 0.8 %copy.14.ids_ref = s32[256,3]{1,0:T(8,128)} copy(s32[256,3]{0,1:T(4,128)S(1)} %pad_add_fusion) | data formatting | bytes 6144 | tf_op jit(solution)/shard_map/stack | solution.py:150
  2.2 4.1 %shard_map.82 = bf16[128,4,2176]{2,1,0:T(4,128)(2,1)} custom-call(s32[256,3]{1,0:T(8,128)} %copy.14.ids_ref, bf16[256,2048]{1,0:T(8,128)(2,1)} %traces_ref.1), custom_call_target="tpu_custom_call" | custom-call | tf_op jit(solution)/shard_map/pallas_call | solution.py:134
  6.3 0.0 copy-start.1
  6.3 0.0 copy-start.2
  6.3 11.5 %all-to-all-start = ((bf16[128,4,2176]{2,1,0:T(4,128)(2,1)}), bf16[128,4,2176]{2,1,0:T(4,128)(2,1)S(1)}, u32[]{:S(2)}, u32[]{:S(2)}) async-start(bf16[128,4,2176]{2,1,0:T(4,128)(2,1)} %shard_map.82), calls=%async_computation | async-start | bytes 4456448 | tf_op jit(solution)/shard_map/all_to_all | solution.py:152
  17.8 0.0 copy-done.1
  17.8 0.0 copy-start.3
  17.8 0.0 copy-done.2
  17.9 0.6 %fusion.4 = (s32[1,1,2048]{2,1,0:T(1,128)S(1)}, s32[1,1,2048]{2,1,0:T(1,128)S(1)}, s32[1,1,2048]{2,1,0:T(1,128)}, s32[1,1,2048]{2,1,0:T(1,128)S(1)}) fusion(s32[1,4,2048]{2,1,0:T(4,128)S(1)} %copy-done.2), kind=kLoop, calls=%fused_computation.79 | loop fusion | bytes 65536 | tf_op jit(solution)/shard_map/slice | solution.py:161
  18.5 0.7 %fusion = (f32[1,1,1,2048]{3,2,1,0:T(1,128)S(1)}, f32[1,1,1,2048]{3,2,1,0:T(1,128)S(1)}, f32[1,1,1,2048]{3,2,1,0:T(1,128)S(1)}, f32[1,1,1,2048]{3,2,1,0:T(1,128)...) fusion(f32[1,1,8,2048]{3,2,1,0:T(8,128)S(1)} %get-tuple-element, ...), kind=kLoop, calls=%fused_computation.75 | loop fusion | bytes 262144 | tf_op jit(solution)/shard_map/slice | solution.py:23
  19.2 0.1 fusion.2
  19.3 2.9 %add_convert_fusion.3 = bf16[1,16,256,128]{3,2,1,0:T(8,128)(2,1)S(1)} fusion(f32[16,128]{1,0:T(8,128)S(1)} %bitcast.67, s32[16,128]{1,0:T(8,128)S(1)} %get-tuple-element.52, f32[16,128]{1,0:T(8,128)S(1)} %bitcast.68, s32[16,128]{1,0:T(8,128)S(1)} %get-tuple-element.51, f32[16,128]{1,0:T(8,128)S(1)} %bitcast.69, s32[16,128]{1,0:T(8,128)S(1)} %get-tuple-element.50, ...), kind=kLoop, calls=%fused_computation.28 | loop fusion | flops 12582912 | bytes 1179648 | tf_op jit(solution)/shard_map/convert_element_type | solution.py:25
  22.3 0.0 copy-done.3
  22.3 0.6 convert_bitcast_fusion
  22.9 1.4 %copy.15.fold_ref = f32[64,1]{1,0:T(8,128)} copy(f32[64,1]{0,1:T(1,128)} %convert_bitcast_fusion) | data formatting | bytes 512 | tf_op jit(solution)/shard_map/convert_element_type | solution.py:165
  24.2 0.7 %iota_add_fusion = (s32[16,128]{1,0:T(8,128)S(1)}, s32[16,128]{1,0:T(8,128)S(1)}, s32[16,128]{1,0:T(8,128)S(1)}, s32[16,128]{1,0:T(8,128)S(1)}, s32[16,128]{1,0:...) fusion(s32[16,128]{1,0:T(8,128)} %bitcast.74), kind=kLoop, calls=%fused_computation.41 | loop fusion | flops 16384 | bytes 73728 | tf_op jit(solution)/shard_map/add | solution.py:23
  24.9 3.6 %add_convert_fusion.2 = bf16[1,16,256,128]{3,2,1,0:T(8,128)(2,1)S(1)} fusion(f32[16,128]{1,0:T(8,128)} %bitcast.64, s32[16,128]{1,0:T(8,128)S(1)} %get-tuple-element.60, f32[16,128]{1,0:T(8,128)} %bitcast.63, s32[16,128]{1,0:T(8,128)S(1)} %get-tuple-element.59, f32[16,128]{1,0:T(8,128)} %bitcast.62, s32[16,128]{1,0:T(8,128)S(1)} %get-tuple-element.58, ...), kind=kLoop, calls=%fused_computation.19 | loop fusion | flops 12582912 | bytes 1179648 | tf_op jit(solution)/shard_map/convert_element_type | solution.py:25
  28.5 2.9 %add_convert_fusion.1 = bf16[1,16,256,128]{3,2,1,0:T(8,128)(2,1)S(1)} fusion(f32[16,128]{1,0:T(8,128)S(1)} %bitcast.51, s32[16,128]{1,0:T(8,128)S(1)} %get-tuple-element.68, f32[16,128]{1,0:T(8,128)S(1)} %bitcast.52, s32[16,128]{1,0:T(8,128)S(1)} %get-tuple-element.67, f32[16,128]{1,0:T(8,128)S(1)} %bitcast.53, s32[16,128]{1,0:T(8,128)S(1)} %get-tuple-element.66, ...), kind=kLoop, calls=%fused_computation.10 | loop fusion | flops 12582912 | bytes 1179648 | tf_op jit(solution)/shard_map/convert_element_type | solution.py:25
  31.4 3.1 %add_convert_fusion = bf16[1,16,256,128]{3,2,1,0:T(8,128)(2,1)S(1)} fusion(f32[16,128]{1,0:T(8,128)S(1)} %bitcast.48, s32[16,128]{1,0:T(8,128)S(1)} %get-tuple-element.76, f32[16,128]{1,0:T(8,128)S(1)} %bitcast.47, s32[16,128]{1,0:T(8,128)S(1)} %get-tuple-element.75, f32[16,128]{1,0:T(8,128)S(1)} %bitcast.46, s32[16,128]{1,0:T(8,128)S(1)} %get-tuple-element.74, ...), kind=kLoop, calls=%fused_computation.1 | loop fusion | flops 12582912 | bytes 1179648 | tf_op jit(solution)/shard_map/convert_element_type | solution.py:25
  34.6 2.2 %pad_maximum_fusion.matrix_ref = bf16[4,16,256,128]{3,2,1,0:T(8,128)(2,1)} fusion(bf16[1,16,256,128]{3,2,1,0:T(8,128)(2,1)S(1)} %add_convert_fusion, bf16[1,16,256,128]{3,2,1,0:T(8,128)(2,1)S(1)} %add_convert_fusion.1, bf16[1,16,256,128]{3,2,1,0:T(8,128)(2,1)S(1)} %add_convert_fusion.2, bf16[1,16,256,128]{3,2,1,0:T(8,128)(2,1)S(1)} %add_convert_fusion.3), kind=kLoop, calls=%fused_computation | loop fusion | flops 6291456 | bytes 8388608 | tf_op jit(solution)/shard_map/stack | solution.py:159
  36.8 12.9 %all-to-all-done.rows_ref = bf16[128,4,2176]{2,1,0:T(4,128)(2,1)S(1)} async-done(((bf16[128,4,2176]{2,1,0:T(4,128)(2,1)}), bf16[128,4,2176]{2,1,0:T(4,128)(2,1)S(1)}, u32[]{:S(2)}, u32[]{:S(2)}) %all-to-all-start) | async-done | bytes 2228256 | tf_op jit(solution)/shard_map/all_to_all | solution.py:152
  49.7 0.0 copy-start
  49.7 1.4 %copy-done = bf16[128,4,2176]{2,1,0:T(4,128)(2,1)} copy-done((bf16[128,4,2176]{2,1,0:T(4,128)(2,1)}, bf16[128,4,2176]{2,1,0:T(4,128)(2,1)S(1)}, u32[]{:S(2)}) %copy-start) | copy-done | bytes 2228248
  51.1 10.9 %shard_map.83 = f32[64,2048]{1,0:T(8,128)} custom-call(bf16[128,4,2176]{2,1,0:T(4,128)(2,1)} %copy-done, bf16[4,16,256,128]{3,2,1,0:T(8,128)(2,1)} %pad_maximum_fusion.matrix_ref, f32[31,2048]{1,0:T(8,128)} %taps_ref.1, f32[64,1]{1,0:T(8,128)} %copy.15.fold_ref), custom_call_target="tpu_custom_call" | custom-call | tf_op jit(solution)/shard_map/pallas_call | solution.py:87
  (4 shorter events, 0.0 us)
Async XLA Ops:
  6.3 11.5 %copy-start.1 = (bf16[1,4,8,2048]{3,2,1,0:T(8,128)(2,1)S(1)}, bf16[1,4,8,2048]{3,2,1,0:T(8,128)(2,1)}, u32[]{:S(2)}) copy-start(bf16[1,4,8,2048]{3,2,1,0:T(8,128)(2,1)} %param.12) | copy-start | bytes 393220
  6.3 11.6 %copy-start.2 = (s32[1,4,2048]{2,1,0:T(4,128)S(1)}, s32[1,4,2048]{2,1,0:T(4,128)}, u32[]{:S(2)}) copy-start(s32[1,4,2048]{2,1,0:T(4,128)} %param.13) | copy-start | bytes 98308
  6.3 43.4 %all-to-all-start = ((bf16[128,4,2176]{2,1,0:T(4,128)(2,1)}), bf16[128,4,2176]{2,1,0:T(4,128)(2,1)S(1)}, u32[]{:S(2)}, u32[]{:S(2)}) async-start(bf16[128,4,2176]{2,1,0:T(4,128)(2,1)} %shard_map.82), calls=%async_computation | async-start | bytes 4456448 | tf_op jit(solution)/shard_map/all_to_all | solution.py:152
  17.8 4.5 %copy-start.3 = (s32[1,64]{1,0:T(1,128)S(1)}, s32[1,64]{1,0:T(1,128)}, u32[]{:S(2)}) copy-start(s32[1,64]{1,0:T(1,128)} %param.15) | copy-start | bytes 772
  49.7 1.4 %copy-start = (bf16[128,4,2176]{2,1,0:T(4,128)(2,1)}, bf16[128,4,2176]{2,1,0:T(4,128)(2,1)S(1)}, u32[]{:S(2)}) copy-start(bf16[128,4,2176]{2,1,0:T(4,128)(2,1)S(1)} %all-to-all-done.rows_ref) | copy-start | bytes 6684676

commit v7 on v6

--- a/solution.py
+++ b/solution.py
@@ -102,12 +102,17 @@
     )(rows, matrices, taps, fold_share)
 
 
-def send_kernel(ids_ref, traces_ref, out_ref, *, bins, tiles):
+def send_kernel(line_ref, bin_ref, offset_ref, traces_ref, out_ref, *, bins, tiles):
     dests, capacity, width = out_ref.shape
     trace_count, length = traces_ref.shape
     slots = dests * capacity
-    ids = ids_ref[...]
-    line_id, bin_id, class_id = ids[:, 0:1], ids[:, 1:2], ids[:, 2:3]
+    block = trace_count // offset_ref.shape[0]
+    line_id = line_ref[...].reshape(trace_count, 1)
+    bin_id = bin_ref[...].reshape(trace_count, 1)
+    trace_index = lax.broadcasted_iota(jnp.int32, (trace_count, 1), 0)
+    class_id = jnp.zeros((trace_count, 1), jnp.int32)
+    for block_index in range(offset_ref.shape[0]):
+        class_id = jnp.where(trace_index // block == block_index, offset_ref[block_index], class_id)
     dest = line_id * tiles + bin_id // bins
     onehot = (dest == lax.broadcasted_iota(jnp.int32, (trace_count, dests), 1)).astype(jnp.bfloat16)
     row = lax.broadcasted_iota(jnp.int32, (trace_count, trace_count), 0)
@@ -128,13 +133,15 @@
     out_ref[:, :, length:] = meta_rows.astype(jnp.bfloat16).reshape(dests, capacity, width - length)
 
 
-def build_send(ids, traces, dests, capacity, bins, tiles):
+def build_send(trace_line, trace_bin, block_offset, traces, dests, capacity, bins, tiles):
     trace_count, length = traces.shape
     width = length + META
+    in_vmem = pl.BlockSpec(memory_space=pltpu.VMEM)
     return pl.pallas_call(
         functools.partial(send_kernel, bins=bins, tiles=tiles),
+        in_specs=[in_vmem, in_vmem, pl.BlockSpec(memory_space=pltpu.SMEM), in_vmem],
         out_shape=jax.ShapeDtypeStruct((dests, capacity, width), jnp.bfloat16),
-    )(ids, traces)
+    )(trace_line, trace_bin, block_offset, traces)
 
 
 def body(traces, trace_line, trace_bin, block_offset, nmo_coef, band_shift, bandpass, fold):
@@ -146,9 +153,9 @@
     dest_count = line_count * tile_count
     capacity = 4
     slots = dest_count * capacity
-    trace_class = jnp.repeat(block_offset, block_rows)
-    ids = jnp.stack([trace_line, trace_bin, trace_class], axis=1)
-    send = build_send(ids, traces, dest_count, capacity, bin_share, tile_count)
+    send = build_send(
+        trace_line, trace_bin, block_offset, traces, dest_count, capacity, bin_share, tile_count
+    )
     received = lax.all_to_all(
         send,
         ("line", "tile"),

time: 62.3 us -> 59.9 us (0.961)
  local copies, waits for them, and re-layouts: 5.71 us -> 4.19 us
  other arithmetic: 16.8 us -> 16.1 us
    another operation x1 -> x0, local copies, waits for them, and re-layouts: 0.8 us -> none  [body(): ids = jnp.stack([trace_line, trace_bin, trace_class], axis=1)]
    broadcast_in_dim x1 -> x0, local copies, waits for them, and re-layouts: 0.72 us -> none  [body(): trace_class = jnp.repeat(block_offset, block_rows)]
    another operation x1 -> x0, other arithmetic: 0.7 us -> none  [body(): ids = jnp.stack([trace_line, trace_bin, trace_class], axis=1)]
  transfers between devices with their start and end apart: 1 -> 1, of which waited for: 1 -> 1; matrix products, arithmetic and copies ran while one was open for 30% -> 32% of each run, Pallas kernels for 0% -> 0%
where the time goes in v7:
time: 59.9 us; the launch traced here: 59.6 us
  other arithmetic  16.1 us (27%)
  Pallas kernels  14.8 us (25%)
  waiting for transfers between devices  12.9 us (22%)
  starting transfers between devices  11.5 us (19%)
  local copies, waits for them, and re-layouts  4.19 us (7%)
    all_to_all x1, waiting for transfers between devices, body(): lax.all_to_all(send, ('line', 'tile'), split_axis=0, concat_axis=0, tiled...  12.9 us
    convert_element_type x4, other arithmetic, moveout_matrix(): return matrix.astype(jnp.bfloat16)  12.6 us
    all_to_all x1, starting transfers between devices, body(): lax.all_to_all(send, ('line', 'tile'), split_axis=0, concat_axis=0, tiled...  11.5 us
    pallas_call x1, Pallas kernels, moveout_stack(): pl.pallas_call(moveout_kernel, grid=(groups // per_step,), in_specs=[pl.B...  10.9 us
    pallas_call x1, Pallas kernels, build_send(): pl.pallas_call(functools.partial(send_kernel, bins=bins, tiles=tiles), in...  3.9 us
    another operation x1, other arithmetic, body(): jnp.stack([moveout_matrix(nmo_coef[0, offset_index], band_shift[0, offset...  2.21 us
    unnamed x8, local copies, waits for them, and re-layouts  1.4 us
    convert_element_type x1, local copies, waits for them, and re-layouts, body(): fold_share = fold[0].astype(jnp.float32)[:, None]  1.36 us
  transfers between devices with their start and end apart: 1, of which 1 were waited for; matrix products, arithmetic and copies ran while one was open for 32% of the time, Pallas kernels for 0%

profile of v7, /device:TPU:1, one launch (start us, length us, event | category | flops | bytes accessed | tf_op | source)
XLA Modules:
  0.0 59.6 jit_solution(4103688191752714886)
XLA Ops:
  0.0 3.9 %shard_map.82 = bf16[128,4,2176]{2,1,0:T(4,128)(2,1)} custom-call(s32[256]{0:T(256)} %line_ref.1, s32[256]{0:T(256)} %bin_ref.1, s32[2]{0:T(128)} %offset_ref.1, bf16[256,2048]{1,0:T(8,128)(2,1)} %traces_ref.1), custom_call_target="tpu_custom_call" | custom-call | tf_op jit(solution)/shard_map/pallas_call | solution.py:140
  3.9 0.0 copy-start.1
  3.9 0.0 copy-start.2
  3.9 11.5 %all-to-all-start = ((bf16[128,4,2176]{2,1,0:T(4,128)(2,1)}), bf16[128,4,2176]{2,1,0:T(4,128)(2,1)S(1)}, u32[]{:S(2)}, u32[]{:S(2)}) async-start(bf16[128,4,2176]{2,1,0:T(4,128)(2,1)} %shard_map.82), calls=%async_computation | async-start | bytes 4456448 | tf_op jit(solution)/shard_map/all_to_all | solution.py:159
  15.4 0.0 copy-done.1
  15.4 0.0 copy-start.3
  15.5 0.0 copy-done.2
  15.5 0.6 %fusion.4 = (s32[1,1,2048]{2,1,0:T(1,128)S(1)}, s32[1,1,2048]{2,1,0:T(1,128)S(1)}, s32[1,1,2048]{2,1,0:T(1,128)}, s32[1,1,2048]{2,1,0:T(1,128)S(1)}) fusion(s32[1,4,2048]{2,1,0:T(4,128)S(1)} %copy-done.2), kind=kLoop, calls=%fused_computation.78 | loop fusion | bytes 65536 | tf_op jit(solution)/shard_map/slice | solution.py:168
  16.1 0.7 %fusion = (f32[1,1,1,2048]{3,2,1,0:T(1,128)S(1)}, f32[1,1,1,2048]{3,2,1,0:T(1,128)S(1)}, f32[1,1,1,2048]{3,2,1,0:T(1,128)S(1)}, f32[1,1,1,2048]{3,2,1,0:T(1,128)...) fusion(f32[1,1,8,2048]{3,2,1,0:T(8,128)S(1)} %get-tuple-element, ...), kind=kLoop, calls=%fused_computation.74 | loop fusion | bytes 262144 | tf_op jit(solution)/shard_map/slice | solution.py:23
  16.8 0.1 fusion.2
  16.9 2.9 %add_convert_fusion.3 = bf16[1,16,256,128]{3,2,1,0:T(8,128)(2,1)S(1)} fusion(f32[16,128]{1,0:T(8,128)S(1)} %bitcast.64, s32[16,128]{1,0:T(8,128)S(1)} %get-tuple-element.52, f32[16,128]{1,0:T(8,128)S(1)} %bitcast.65, s32[16,128]{1,0:T(8,128)S(1)} %get-tuple-element.51, f32[16,128]{1,0:T(8,128)S(1)} %bitcast.66, s32[16,128]{1,0:T(8,128)S(1)} %get-tuple-element.50, ...), kind=kLoop, calls=%fused_computation.28 | loop fusion | flops 12582912 | bytes 1179648 | tf_op jit(solution)/shard_map/convert_element_type | solution.py:25
  19.9 0.0 copy-done.3
  19.9 0.6 convert_bitcast_fusion
  20.5 1.4 %copy.9.fold_ref = f32[64,1]{1,0:T(8,128)} copy(f32[64,1]{0,1:T(1,128)} %convert_bitcast_fusion) | data formatting | bytes 512 | tf_op jit(solution)/shard_map/convert_element_type | solution.py:172
  21.8 0.7 %iota_add_fusion = (s32[16,128]{1,0:T(8,128)S(1)}, s32[16,128]{1,0:T(8,128)S(1)}, s32[16,128]{1,0:T(8,128)S(1)}, s32[16,128]{1,0:T(8,128)S(1)}, s32[16,128]{1,0:...) fusion(s32[16,128]{1,0:T(8,128)} %bitcast.71), kind=kLoop, calls=%fused_computation.41 | loop fusion | flops 16384 | bytes 73728 | tf_op jit(solution)/shard_map/add | solution.py:23
  22.5 3.6 %add_convert_fusion.2 = bf16[1,16,256,128]{3,2,1,0:T(8,128)(2,1)S(1)} fusion(f32[16,128]{1,0:T(8,128)} %bitcast.61, s32[16,128]{1,0:T(8,128)S(1)} %get-tuple-element.60, f32[16,128]{1,0:T(8,128)} %bitcast.60, s32[16,128]{1,0:T(8,128)S(1)} %get-tuple-element.59, f32[16,128]{1,0:T(8,128)} %bitcast.59, s32[16,128]{1,0:T(8,128)S(1)} %get-tuple-element.58, ...), kind=kLoop, calls=%fused_computation.19 | loop fusion | flops 12582912 | bytes 1179648 | tf_op jit(solution)/shard_map/convert_element_type | solution.py:25
  26.1 2.9 %add_convert_fusion.1 = bf16[1,16,256,128]{3,2,1,0:T(8,128)(2,1)S(1)} fusion(f32[16,128]{1,0:T(8,128)S(1)} %bitcast.48, s32[16,128]{1,0:T(8,128)S(1)} %get-tuple-element.68, f32[16,128]{1,0:T(8,128)S(1)} %bitcast.49, s32[16,128]{1,0:T(8,128)S(1)} %get-tuple-element.67, f32[16,128]{1,0:T(8,128)S(1)} %bitcast.50, s32[16,128]{1,0:T(8,128)S(1)} %get-tuple-element.66, ...), kind=kLoop, calls=%fused_computation.10 | loop fusion | flops 12582912 | bytes 1179648 | tf_op jit(solution)/shard_map/convert_element_type | solution.py:25
  29.1 3.1 %add_convert_fusion = bf16[1,16,256,128]{3,2,1,0:T(8,128)(2,1)S(1)} fusion(f32[16,128]{1,0:T(8,128)S(1)} %bitcast.45, s32[16,128]{1,0:T(8,128)S(1)} %get-tuple-element.76, f32[16,128]{1,0:T(8,128)S(1)} %bitcast.44, s32[16,128]{1,0:T(8,128)S(1)} %get-tuple-element.75, f32[16,128]{1,0:T(8,128)S(1)} %bitcast.43, s32[16,128]{1,0:T(8,128)S(1)} %get-tuple-element.74, ...), kind=kLoop, calls=%fused_computation.1 | loop fusion | flops 12582912 | bytes 1179648 | tf_op jit(solution)/shard_map/convert_element_type | solution.py:25
  32.2 2.2 %pad_maximum_fusion.matrix_ref = bf16[4,16,256,128]{3,2,1,0:T(8,128)(2,1)} fusion(bf16[1,16,256,128]{3,2,1,0:T(8,128)(2,1)S(1)} %add_convert_fusion, bf16[1,16,256,128]{3,2,1,0:T(8,128)(2,1)S(1)} %add_convert_fusion.1, bf16[1,16,256,128]{3,2,1,0:T(8,128)(2,1)S(1)} %add_convert_fusion.2, bf16[1,16,256,128]{3,2,1,0:T(8,128)(2,1)S(1)} %add_convert_fusion.3), kind=kLoop, calls=%fused_computation | loop fusion | flops 6291456 | bytes 8388608 | tf_op jit(solution)/shard_map/stack | solution.py:166
  34.4 12.9 %all-to-all-done.rows_ref = bf16[128,4,2176]{2,1,0:T(4,128)(2,1)S(1)} async-done(((bf16[128,4,2176]{2,1,0:T(4,128)(2,1)}), bf16[128,4,2176]{2,1,0:T(4,128)(2,1)S(1)}, u32[]{:S(2)}, u32[]{:S(2)}) %all-to-all-start) | async-done | bytes 2228256 | tf_op jit(solution)/shard_map/all_to_all | solution.py:159
  47.3 0.0 copy-start
  47.3 1.4 %copy-done = bf16[128,4,2176]{2,1,0:T(4,128)(2,1)} copy-done((bf16[128,4,2176]{2,1,0:T(4,128)(2,1)}, bf16[128,4,2176]{2,1,0:T(4,128)(2,1)S(1)}, u32[]{:S(2)}) %copy-start) | copy-done | bytes 2228248
  48.7 10.9 %shard_map.83 = f32[64,2048]{1,0:T(8,128)} custom-call(bf16[128,4,2176]{2,1,0:T(4,128)(2,1)} %copy-done, bf16[4,16,256,128]{3,2,1,0:T(8,128)(2,1)} %pad_maximum_fusion.matrix_ref, f32[31,2048]{1,0:T(8,128)} %taps_ref.1, f32[64,1]{1,0:T(8,128)} %copy.9.fold_ref), custom_call_target="tpu_custom_call" | custom-call | tf_op jit(solution)/shard_map/pallas_call | solution.py:87
  (4 shorter events, 0.0 us)
Async XLA Ops:
  3.9 11.5 %copy-start.1 = (bf16[1,4,8,2048]{3,2,1,0:T(8,128)(2,1)S(1)}, bf16[1,4,8,2048]{3,2,1,0:T(8,128)(2,1)}, u32[]{:S(2)}) copy-start(bf16[1,4,8,2048]{3,2,1,0:T(8,128)(2,1)} %param.12) | copy-start | bytes 393220
  3.9 11.6 %copy-start.2 = (s32[1,4,2048]{2,1,0:T(4,128)S(1)}, s32[1,4,2048]{2,1,0:T(4,128)}, u32[]{:S(2)}) copy-start(s32[1,4,2048]{2,1,0:T(4,128)} %param.13) | copy-start | bytes 98308
  3.9 43.4 %all-to-all-start = ((bf16[128,4,2176]{2,1,0:T(4,128)(2,1)}), bf16[128,4,2176]{2,1,0:T(4,128)(2,1)S(1)}, u32[]{:S(2)}, u32[]{:S(2)}) async-start(bf16[128,4,2176]{2,1,0:T(4,128)(2,1)} %shard_map.82), calls=%async_computation | async-start | bytes 4456448 | tf_op jit(solution)/shard_map/all_to_all | solution.py:159
  15.4 4.5 %copy-start.3 = (s32[1,64]{1,0:T(1,128)S(1)}, s32[1,64]{1,0:T(1,128)}, u32[]{:S(2)}) copy-start(s32[1,64]{1,0:T(1,128)} %param.15) | copy-start | bytes 772
  47.3 1.4 %copy-start = (bf16[128,4,2176]{2,1,0:T(4,128)(2,1)}, bf16[128,4,2176]{2,1,0:T(4,128)(2,1)S(1)}, u32[]{:S(2)}) copy-start(bf16[128,4,2176]{2,1,0:T(4,128)(2,1)S(1)} %all-to-all-done.rows_ref) | copy-start | bytes 6684676

commit v8 on v7

--- a/solution.py
+++ b/solution.py
@@ -8,6 +8,7 @@
 from jax.experimental.pallas import tpu as pltpu
 
 META = 128
+PAD = 16
 
 
 def moveout_matrix(coef_rows, shift_rows):
@@ -31,8 +32,6 @@
     bins, length = out_ref.shape
     sources, capacity, width = rows_ref.shape
     slot_count = sources * capacity
-    taps_count = taps_ref.shape[0]
-    half = (taps_count - 1) // 2
 
     @pl.when(step == 0)
     def _():
@@ -68,15 +67,16 @@
 
     @pl.when(step == pl.num_programs(0) - 1)
     def _():
-        span = length + 256
-        for row in range(bins // 8):
-            rows_now = stack_ref[row * 8:(row + 1) * 8, :]
-            filtered = jnp.zeros((8, length), jnp.float32)
-            for tap_index in range(taps_count):
-                shift = (-(128 + tap_index - half)) % span
-                moved = pltpu.roll(rows_now, shift, 1)[:, :length]
-                filtered = filtered + taps_ref[tap_index:tap_index + 1, :] * moved
-            out_ref[row * 8:(row + 1) * 8, :] = filtered / fold_ref[row * 8:(row + 1) * 8, :]
+        for group in range(length // 128):
+            start = group * 128
+            window = stack_ref[:, start + 128 - PAD:start + 384 - PAD]
+            filtered = jnp.dot(
+                window,
+                taps_ref[group],
+                precision=lax.Precision.HIGHEST,
+                preferred_element_type=jnp.float32,
+            )
+            out_ref[:, start:start + 128] = filtered / fold_ref[...]
 
 
 def moveout_stack(rows, matrices, taps, fold_share, length):
@@ -90,7 +90,7 @@
         in_specs=[
             pl.BlockSpec((sources, capacity, width), lambda g: (0, 0, 0)),
             pl.BlockSpec((classes, per_step, 256, 128), lambda g: (0, g, 0, 0)),
-            pl.BlockSpec(taps.shape, lambda g: (0, 0)),
+            pl.BlockSpec(taps.shape, lambda g: (0, 0, 0)),
             pl.BlockSpec((bins, 1), lambda g: (0, 0)),
         ],
         out_specs=pl.BlockSpec((bins, length), lambda g: (0, 0)),
@@ -100,6 +100,21 @@
             pltpu.VMEM((bins, length + 256), jnp.float32),
         ],
     )(rows, matrices, taps, fold_share)
+
+
+def filter_matrix(taps):
+    taps_count = taps.shape[0]
+    groups = taps.shape[1] // 128
+    half = (taps_count - 1) // 2
+    column = jnp.arange(128, dtype=jnp.int32).reshape(1, 1, 128)
+    position = jnp.arange(256, dtype=jnp.int32).reshape(1, 256, 1)
+    weights = taps.reshape(taps_count, groups, 1, 128)
+    matrix = jnp.zeros((groups, 256, 128), jnp.float32)
+    for tap_index in range(taps_count):
+        matrix = matrix + jnp.where(
+            position == column + PAD + tap_index - half, weights[tap_index], 0.0
+        )
+    return matrix
 
 
 def send_kernel(line_ref, bin_ref, offset_ref, traces_ref, out_ref, *, bins, tiles):
@@ -170,7 +185,7 @@
         ]
     )
     fold_share = fold[0].astype(jnp.float32)[:, None]
-    filtered = moveout_stack(received, matrices, bandpass, fold_share, length)
+    filtered = moveout_stack(received, matrices, filter_matrix(bandpass), fold_share, length)
     return filtered[None]
 
 

time: 59.9 us -> 66.7 us (1.11)
  other arithmetic: 16.1 us -> 37.9 us
  waiting for transfers between devices: 12.9 us -> 0.01 us
  Pallas kernels: 14.8 us -> 12.1 us
  between operations: 0.08 us -> 0.94 us
    all_to_all x1, waiting for transfers between devices: 12.9 us -> 0.01 us  [body(): lax.all_to_all(send, ('line', 'tile'), split_axis=0, concat_axis=0, tiled...]
    eq x0 -> x16, other arithmetic: none -> 10.5 us  [filter_matrix(): position == column + PAD + tap_index - half]
    add x0 -> x1, other arithmetic: none -> 7.81 us  [filter_matrix(): matrix + jnp.where(position == column + PAD + tap_index - half, weights[t...]
    pallas_call x1, Pallas kernels: 10.9 us -> 8.2 us  [moveout_stack(): pl.pallas_call(moveout_kernel, grid=(groups // per_step,), in_specs=[pl.B...]
    convert_element_type x4, other arithmetic: 12.6 us -> 15.1 us  [moveout_matrix(): return matrix.astype(jnp.bfloat16)]
    another operation x1, other arithmetic: 2.21 us -> 3.67 us  [body(): jnp.stack([moveout_matrix(nmo_coef[0, offset_index], band_shift[0, offset...]
    slice x0 -> x2, local copies, waits for them, and re-layouts: none -> 0.8 us  [filter_matrix(): weights[tap_index]]
    add x4, other arithmetic: 0.73 us -> 0.04 us  [moveout_matrix(): column + shifts + tap_index]
  transfers between devices with their start and end apart: 1 -> 1, of which waited for: 1 -> 0; matrix products, arithmetic and copies ran while one was open for 32% -> 61% of each run, Pallas kernels for 0% -> 0%
where the time goes in v8:
time: 66.7 us; the launch traced here: 66.4 us
  other arithmetic  37.9 us (57%)
  Pallas kernels  12.1 us (18%)
  starting transfers between devices  11.5 us (17%)
  local copies, waits for them, and re-layouts  3.96 us (6%)
  between operations  0.94 us (1%)
    convert_element_type x4, other arithmetic, moveout_matrix(): return matrix.astype(jnp.bfloat16)  15.1 us
    all_to_all x1, starting transfers between devices, body(): lax.all_to_all(send, ('line', 'tile'), split_axis=0, concat_axis=0, tiled...  11.5 us
    eq x16, other arithmetic, filter_matrix(): position == column + PAD + tap_index - half  10.5 us
    pallas_call x1, Pallas kernels, moveout_stack(): pl.pallas_call(moveout_kernel, grid=(groups // per_step,), in_specs=[pl.B...  8.2 us
    add x1, other arithmetic, filter_matrix(): matrix + jnp.where(position == column + PAD + tap_index - half, weights[t...  7.81 us
    pallas_call x1, Pallas kernels, build_send(): pl.pallas_call(functools.partial(send_kernel, bins=bins, tiles=tiles), in...  3.92 us
    another operation x1, other arithmetic, body(): jnp.stack([moveout_matrix(nmo_coef[0, offset_index], band_shift[0, offset...  3.67 us
    unnamed x90, local copies, waits for them, and re-layouts  1.6 us
  transfers between devices with their start and end apart: 1, of which 0 were waited for; matrix products, arithmetic and copies ran while one was open for 61% of the time, Pallas kernels for 0%

profile of v8, /device:TPU:1, one launch (start us, length us, event | category | flops | bytes accessed | tf_op | source)
XLA Modules:
  0.0 66.4 jit_solution(16799976465869989072)
XLA Ops:
  0.0 3.9 %shard_map.82 = bf16[128,4,2176]{2,1,0:T(4,128)(2,1)} custom-call(s32[256]{0:T(256)} %line_ref.1, s32[256]{0:T(256)} %bin_ref.1, s32[2]{0:T(128)} %offset_ref.1, bf16[256,2048]{1,0:T(8,128)(2,1)} %traces_ref.1), custom_call_target="tpu_custom_call" | custom-call | tf_op jit(solution)/shard_map/pallas_call | solution.py:155
  3.9 11.5 %all-to-all-start = ((bf16[128,4,2176]{2,1,0:T(4,128)(2,1)}), bf16[128,4,2176]{2,1,0:T(4,128)(2,1)S(1)}, u32[]{:S(2)}, u32[]{:S(2)}) async-start(bf16[128,4,2176]{2,1,0:T(4,128)(2,1)} %shard_map.82), calls=%async_computation | async-start | bytes 4456448 | tf_op jit(solution)/shard_map/all_to_all | solution.py:174
  15.8 0.0 copy-done.33
  15.8 0.0 copy-done.43
  15.9 0.0 copy-done.1
  15.9 0.7 %fusion.1 = (f32[1,2048]{1,0:T(1,128)S(1)}, f32[1,2048]{1,0:T(1,128)S(1)}, f32[1,2048]{1,0:T(1,128)}, f32[1,2048]{1,0:T(1,128)}, f32[1,2048]{1,0:T(1,128)}, /*in...) fusion(f32[31,2048]{1,0:T(8,128)S(1)} %copy-done.1), kind=kLoop, calls=%fused_computation.138 | loop fusion | bytes 196608 | tf_op jit(solution)/shard_map/slice | solution.py:115
  16.6 0.6 iota_compare_fusion.62
  17.2 0.1 fusion.4
  17.3 0.1 fusion.2
  17.4 0.7 iota_compare_fusion.32
  18.1 0.7 iota_compare_fusion.34
  18.8 0.7 iota_compare_fusion.36
  19.4 0.7 iota_compare_fusion.38
  20.1 0.7 iota_compare_fusion.40
  20.7 0.7 %iota_compare_fusion.42 = (pred[256,128]{1,0:T(8,128)(4,1)}, pred[256,128]{1,0:T(8,128)(4,1)}) fusion(s32[128]{0:T(128)S(1)} %iota_add_fusion.14, s32[128]{0:T(128)S(1)} %iota_add_fusion.15), kind=kLoop, calls=%fused_computation.48 | loop fusion | flops 65536 | bytes 66560 | tf_op jit(solution)/shard_map/eq | solution.py:115
  21.4 0.7 iota_compare_fusion.44
  22.1 0.7 iota_compare_fusion.46
  22.7 0.7 iota_compare_fusion.48
  23.4 0.7 iota_compare_fusion.50
  24.0 0.7 iota_compare_fusion.52
  24.7 0.7 iota_compare_fusion.54
  25.4 0.7 iota_compare_fusion.56
  26.0 0.7 iota_compare_fusion.58
  26.7 0.7 iota_compare_fusion.60
  27.3 2.9 %add_convert_fusion = bf16[1,16,256,128]{3,2,1,0:T(8,128)(2,1)S(1)} fusion(f32[16,128]{1,0:T(8,128)S(1)} %bitcast.112, s32[16,128]{1,0:T(8,128)S(1)} %get-tuple-element.107, f32[16,128]{1,0:T(8,128)S(1)} %bitcast.111, s32[16,128]{1,0:T(8,128)S(1)} %get-tuple-element.106, f32[16,128]{1,0:T(8,128)S(1)} %bitcast.110, s32[16,128]{1,0:T(8,128)S(1)} %get-tuple-element.105, ...), kind=kLoop, calls=%fused_computation.2 | loop fusion | flops 12582912 | bytes 1179648 | tf_op jit(solution)/shard_map/convert_element_type | solution.py:26
  30.3 0.0 copy-start.44
  30.3 4.0 %add_convert_fusion.1 = bf16[1,16,256,128]{3,2,1,0:T(8,128)(2,1)} fusion(f32[16,128]{1,0:T(8,128)S(1)} %bitcast.99, s32[16,128]{1,0:T(8,128)S(1)} %get-tuple-element.99, f32[16,128]{1,0:T(8,128)S(1)} %bitcast.100, s32[16,128]{1,0:T(8,128)S(1)} %get-tuple-element.98, f32[16,128]{1,0:T(8,128)S(1)} %bitcast.101, s32[16,128]{1,0:T(8,128)S(1)} %get-tuple-element.97, ...), kind=kLoop, calls=%fused_computation.11 | loop fusion | flops 12582912 | bytes 1179648 | tf_op jit(solution)/shard_map/convert_element_type | solution.py:26
  34.3 4.1 %add_convert_fusion.2 = bf16[1,16,256,128]{3,2,1,0:T(8,128)(2,1)} fusion(f32[16,128]{1,0:T(8,128)S(1)} %bitcast.96, s32[16,128]{1,0:T(8,128)S(1)} %get-tuple-element.91, f32[16,128]{1,0:T(8,128)S(1)} %bitcast.95, s32[16,128]{1,0:T(8,128)S(1)} %get-tuple-element.90, f32[16,128]{1,0:T(8,128)S(1)} %bitcast.94, s32[16,128]{1,0:T(8,128)S(1)} %get-tuple-element.89, ...), kind=kLoop, calls=%fused_computation.20 | loop fusion | flops 12582912 | bytes 1179648 | tf_op jit(solution)/shard_map/convert_element_type | solution.py:26
  38.3 4.1 %add_convert_fusion.3 = bf16[1,16,256,128]{3,2,1,0:T(8,128)(2,1)} fusion(f32[16,128]{1,0:T(8,128)S(1)} %bitcast.83, s32[16,128]{1,0:T(8,128)S(1)} %get-tuple-element.83, f32[16,128]{1,0:T(8,128)S(1)} %bitcast.84, s32[16,128]{1,0:T(8,128)S(1)} %get-tuple-element.82, f32[16,128]{1,0:T(8,128)S(1)} %bitcast.85, s32[16,128]{1,0:T(8,128)S(1)} %get-tuple-element.81, ...), kind=kLoop, calls=%fused_computation.29 | loop fusion | flops 12582912 | bytes 1179648 | tf_op jit(solution)/shard_map/convert_element_type | solution.py:26
  42.5 0.0 copy-done.44
  42.5 0.6 convert_bitcast_fusion
  43.0 1.3 %copy.9.fold_ref = f32[64,1]{1,0:T(8,128)} copy(f32[64,1]{0,1:T(1,128)} %convert_bitcast_fusion) | data formatting | bytes 512 | tf_op jit(solution)/shard_map/convert_element_type | solution.py:187
  44.4 0.0 copy-start.6
  44.4 0.0 copy-start.7
  44.4 0.0 copy-start.8
  44.4 0.0 copy-start.9
  44.5 0.0 copy-start.10
  44.5 0.0 copy-start.11
  44.5 0.0 copy-start.12
  44.5 0.0 copy-start.13
  44.5 0.0 copy-start.14
  44.5 0.0 copy-start.15
  44.8 3.7 %pad_maximum_fusion.matrix_ref = bf16[4,16,256,128]{3,2,1,0:T(8,128)(2,1)} fusion(bf16[1,16,256,128]{3,2,1,0:T(8,128)(2,1)S(1)} %add_convert_fusion, bf16[1,16,256,128]{3,2,1,0:T(8,128)(2,1)} %add_convert_fusion.1, bf16[1,16,256,128]{3,2,1,0:T(8,128)(2,1)} %add_convert_fusion.2, bf16[1,16,256,128]{3,2,1,0:T(8,128)(2,1)} %add_convert_fusion.3), kind=kLoop, calls=%fused_computation | loop fusion | flops 6291456 | bytes 8388608 | tf_op jit(solution)/shard_map/stack | solution.py:181
  48.4 0.1 fusion
  49.0 7.8 %select_add_fusion.taps_ref = f32[16,256,128]{2,1,0:T(8,128)} fusion(f32[16,128]{1,0:T(8,128)S(1)} %bitcast.80, f32[16,128]{1,0:T(8,128)} %bitcast.81, f32[16,128]{1,0:T(8,128)S(1)} %bitcast.115, f32[16,128]{1,0:T(8,128)S(1)} %bitcast.116, f32[16,128]{1,0:T(8,128)S(1)} %bitcast.117, f32[16,128]{1,0:T(8,128)S(1)} %bitcast.118, f32[16,128]{1,0:T(8,128)S(1)} %bitcast.119, ...), kind=kLoop, calls=%fused_computation.1 | loop fusion | flops 31981568 | bytes 3366912 | tf_op jit(solution)/shard_map/add | solution.py:114
  56.8 0.0 all-to-all-done.rows_ref
  56.8 1.4 %copy-done = bf16[128,4,2176]{2,1,0:T(4,128)(2,1)} copy-done((bf16[128,4,2176]{2,1,0:T(4,128)(2,1)}, bf16[128,4,2176]{2,1,0:T(4,128)(2,1)S(1)}, u32[]{:S(2)}) %copy-start) | copy-done | bytes 2228248
  58.2 8.2 %shard_map.83 = f32[64,2048]{1,0:T(8,128)} custom-call(bf16[128,4,2176]{2,1,0:T(4,128)(2,1)} %copy-done, bf16[4,16,256,128]{3,2,1,0:T(8,128)(2,1)} %pad_maximum_fusion.matrix_ref, f32[16,256,128]{2,1,0:T(8,128)} %select_add_fusion.taps_ref, f32[64,1]{1,0:T(8,128)} %copy.9.fold_ref), custom_call_target="tpu_custom_call" | custom-call | tf_op jit(solution)/shard_map/pallas_call | solution.py:87
  (111 shorter events, 0.4 us)
Async XLA Ops:
  3.9 11.8 %copy-start.33 = (bf16[1,4,8,2048]{3,2,1,0:T(8,128)(2,1)S(1)}, bf16[1,4,8,2048]{3,2,1,0:T(8,128)(2,1)}, u32[]{:S(2)}) copy-start(bf16[1,4,8,2048]{3,2,1,0:T(8,128)(2,1)} %param.12) | copy-start | bytes 393220
  3.9 11.9 %copy-start.43 = (s32[1,4,2048]{2,1,0:T(4,128)S(1)}, s32[1,4,2048]{2,1,0:T(4,128)}, u32[]{:S(2)}) copy-start(s32[1,4,2048]{2,1,0:T(4,128)} %param.13) | copy-start | bytes 98308
  3.9 12.0 %copy-start.1 = (f32[31,2048]{1,0:T(8,128)S(1)}, f32[31,2048]{1,0:T(8,128)}, u32[]{:S(2)}) copy-start(f32[31,2048]{1,0:T(8,128)} %param.14) | copy-start | bytes 761860
  3.9 52.8 %all-to-all-start = ((bf16[128,4,2176]{2,1,0:T(4,128)(2,1)}), bf16[128,4,2176]{2,1,0:T(4,128)(2,1)S(1)}, u32[]{:S(2)}, u32[]{:S(2)}) async-start(bf16[128,4,2176]{2,1,0:T(4,128)(2,1)} %shard_map.82), calls=%async_computation | async-start | bytes 4456448 | tf_op jit(solution)/shard_map/all_to_all | solution.py:174
  30.3 12.2 %copy-start.44 = (s32[1,64]{1,0:T(1,128)S(1)}, s32[1,64]{1,0:T(1,128)}, u32[]{:S(2)}) copy-start(s32[1,64]{1,0:T(1,128)} %param.15) | copy-start | bytes 772
  44.4 4.2 %copy-start.2 = (pred[256,128]{1,0:T(8,128)(4,1)S(1)}, pred[256,128]{1,0:T(8,128)(4,1)}, u32[]{:S(2)}) copy-start(pred[256,128]{1,0:T(8,128)(4,1)} %iota_compare_fusion.62) | copy-start | bytes 98308
  44.4 4.2 %copy-start.3 = (pred[256,128]{1,0:T(8,128)(4,1)S(1)}, pred[256,128]{1,0:T(8,128)(4,1)}, u32[]{:S(2)}) copy-start(pred[256,128]{1,0:T(8,128)(4,1)} %get-tuple-element.124) | copy-start | bytes 98308
  44.4 4.2 %copy-start.4 = (pred[256,128]{1,0:T(8,128)(4,1)S(1)}, pred[256,128]{1,0:T(8,128)(4,1)}, u32[]{:S(2)}) copy-start(pred[256,128]{1,0:T(8,128)(4,1)} %get-tuple-element.125) | copy-start | bytes 98308
  44.4 4.2 %copy-start.5 = (pred[256,128]{1,0:T(8,128)(4,1)S(1)}, pred[256,128]{1,0:T(8,128)(4,1)}, u32[]{:S(2)}) copy-start(pred[256,128]{1,0:T(8,128)(4,1)} %get-tuple-element.126) | copy-start | bytes 98308
  44.4 4.2 %copy-start.6 = (pred[256,128]{1,0:T(8,128)(4,1)S(1)}, pred[256,128]{1,0:T(8,128)(4,1)}, u32[]{:S(2)}) copy-start(pred[256,128]{1,0:T(8,128)(4,1)} %get-tuple-element.127) | copy-start | bytes 98308
  44.4 4.2 %copy-start.7 = (pred[256,128]{1,0:T(8,128)(4,1)S(1)}, pred[256,128]{1,0:T(8,128)(4,1)}, u32[]{:S(2)}) copy-start(pred[256,128]{1,0:T(8,128)(4,1)} %get-tuple-element.128) | copy-start | bytes 98308
  44.4 4.2 %copy-start.8 = (pred[256,128]{1,0:T(8,128)(4,1)S(1)}, pred[256,128]{1,0:T(8,128)(4,1)}, u32[]{:S(2)}) copy-start(pred[256,128]{1,0:T(8,128)(4,1)} %get-tuple-element.129) | copy-start | bytes 98308
  44.4 4.2 %copy-start.9 = (pred[256,128]{1,0:T(8,128)(4,1)S(1)}, pred[256,128]{1,0:T(8,128)(4,1)}, u32[]{:S(2)}) copy-start(pred[256,128]{1,0:T(8,128)(4,1)} %get-tuple-element.130) | copy-start | bytes 98308
  44.5 4.2 %copy-start.10 = (pred[256,128]{1,0:T(8,128)(4,1)S(1)}, pred[256,128]{1,0:T(8,128)(4,1)}, u32[]{:S(2)}) copy-start(pred[256,128]{1,0:T(8,128)(4,1)} %get-tuple-element.131) | copy-start | bytes 98308
  44.5 4.2 %copy-start.11 = (pred[256,128]{1,0:T(8,128)(4,1)S(1)}, pred[256,128]{1,0:T(8,128)(4,1)}, u32[]{:S(2)}) copy-start(pred[256,128]{1,0:T(8,128)(4,1)} %get-tuple-element.132) | copy-start | bytes 98308
  44.5 4.2 %copy-start.12 = (pred[256,128]{1,0:T(8,128)(4,1)S(1)}, pred[256,128]{1,0:T(8,128)(4,1)}, u32[]{:S(2)}) copy-start(pred[256,128]{1,0:T(8,128)(4,1)} %get-tuple-element.133) | copy-start | bytes 98308
  44.5 4.2 %copy-start.13 = (pred[256,128]{1,0:T(8,128)(4,1)S(1)}, pred[256,128]{1,0:T(8,128)(4,1)}, u32[]{:S(2)}) copy-start(pred[256,128]{1,0:T(8,128)(4,1)} %get-tuple-element.134) | copy-start | bytes 98308
  44.5 4.2 %copy-start.14 = (pred[256,128]{1,0:T(8,128)(4,1)S(1)}, pred[256,128]{1,0:T(8,128)(4,1)}, u32[]{:S(2)}) copy-start(pred[256,128]{1,0:T(8,128)(4,1)} %get-tuple-element.135) | copy-start | bytes 98308
  44.5 4.2 %copy-start.15 = (pred[256,128]{1,0:T(8,128)(4,1)S(1)}, pred[256,128]{1,0:T(8,128)(4,1)}, u32[]{:S(2)}) copy-start(pred[256,128]{1,0:T(8,128)(4,1)} %get-tuple-element.136) | copy-start | bytes 98308
  44.5 4.2 %copy-start.16 = (pred[256,128]{1,0:T(8,128)(4,1)S(1)}, pred[256,128]{1,0:T(8,128)(4,1)}, u32[]{:S(2)}) copy-start(pred[256,128]{1,0:T(8,128)(4,1)} %get-tuple-element.137) | copy-start | bytes 98308
  44.5 4.2 %copy-start.17 = (pred[256,128]{1,0:T(8,128)(4,1)S(1)}, pred[256,128]{1,0:T(8,128)(4,1)}, u32[]{:S(2)}) copy-start(pred[256,128]{1,0:T(8,128)(4,1)} %get-tuple-element.138) | copy-start | bytes 98308
  44.5 4.2 %copy-start.18 = (pred[256,128]{1,0:T(8,128)(4,1)S(1)}, pred[256,128]{1,0:T(8,128)(4,1)}, u32[]{:S(2)}) copy-start(pred[256,128]{1,0:T(8,128)(4,1)} %get-tuple-element.139) | copy-start | bytes 98308
  44.5 4.2 %copy-start.19 = (pred[256,128]{1,0:T(8,128)(4,1)S(1)}, pred[256,128]{1,0:T(8,128)(4,1)}, u32[]{:S(2)}) copy-start(pred[256,128]{1,0:T(8,128)(4,1)} %get-tuple-element.140) | copy-start | bytes 98308
  44.6 4.2 %copy-start.20 = (pred[256,128]{1,0:T(8,128)(4,1)S(1)}, pred[256,128]{1,0:T(8,128)(4,1)}, u32[]{:S(2)}) copy-start(pred[256,128]{1,0:T(8,128)(4,1)} %get-tuple-element.141) | copy-start | bytes 98308
  44.6 4.2 %copy-start.21 = (pred[256,128]{1,0:T(8,128)(4,1)S(1)}, pred[256,128]{1,0:T(8,128)(4,1)}, u32[]{:S(2)}) copy-start(pred[256,128]{1,0:T(8,128)(4,1)} %get-tuple-element.142) | copy-start | bytes 98308
  44.6 4.2 %copy-start.22 = (pred[256,128]{1,0:T(8,128)(4,1)S(1)}, pred[256,128]{1,0:T(8,128)(4,1)}, u32[]{:S(2)}) copy-start(pred[256,128]{1,0:T(8,128)(4,1)} %get-tuple-element.143) | copy-start | bytes 98308
  44.6 4.2 %copy-start.23 = (pred[256,128]{1,0:T(8,128)(4,1)S(1)}, pred[256,128]{1,0:T(8,128)(4,1)}, u32[]{:S(2)}) copy-start(pred[256,128]{1,0:T(8,128)(4,1)} %get-tuple-element.144) | copy-start | bytes 98308
  44.6 4.2 %copy-start.24 = (pred[256,128]{1,0:T(8,128)(4,1)S(1)}, pred[256,128]{1,0:T(8,128)(4,1)}, u32[]{:S(2)}) copy-start(pred[256,128]{1,0:T(8,128)(4,1)} %get-tuple-element.145) | copy-start | bytes 98308
  44.6 4.2 %copy-start.25 = (pred[256,128]{1,0:T(8,128)(4,1)S(1)}, pred[256,128]{1,0:T(8,128)(4,1)}, u32[]{:S(2)}) copy-start(pred[256,128]{1,0:T(8,128)(4,1)} %get-tuple-element.146) | copy-start | bytes 98308
  44.6 4.2 %copy-start.26 = (pred[256,128]{1,0:T(8,128)(4,1)S(1)}, pred[256,128]{1,0:T(8,128)(4,1)}, u32[]{:S(2)}) copy-start(pred[256,128]{1,0:T(8,128)(4,1)} %get-tuple-element.147) | copy-start | bytes 98308
  44.6 4.2 %copy-start.27 = (pred[256,128]{1,0:T(8,128)(4,1)S(1)}, pred[256,128]{1,0:T(8,128)(4,1)}, u32[]{:S(2)}) copy-start(pred[256,128]{1,0:T(8,128)(4,1)} %get-tuple-element.148) | copy-start | bytes 98308
  44.6 4.2 %copy-start.28 = (pred[256,128]{1,0:T(8,128)(4,1)S(1)}, pred[256,128]{1,0:T(8,128)(4,1)}, u32[]{:S(2)}) copy-start(pred[256,128]{1,0:T(8,128)(4,1)} %get-tuple-element.149) | copy-start | bytes 98308
  44.6 4.2 %copy-start.29 = (pred[256,128]{1,0:T(8,128)(4,1)S(1)}, pred[256,128]{1,0:T(8,128)(4,1)}, u32[]{:S(2)}) copy-start(pred[256,128]{1,0:T(8,128)(4,1)} %get-tuple-element.150) | copy-start | bytes 98308
  44.7 4.2 %copy-start.30 = (pred[256,128]{1,0:T(8,128)(4,1)S(1)}, pred[256,128]{1,0:T(8,128)(4,1)}, u32[]{:S(2)}) copy-start(pred[256,128]{1,0:T(8,128)(4,1)} %get-tuple-element.151) | copy-start | bytes 98308
  44.7 4.2 %copy-start.31 = (pred[256,128]{1,0:T(8,128)(4,1)S(1)}, pred[256,128]{1,0:T(8,128)(4,1)}, u32[]{:S(2)}) copy-start(pred[256,128]{1,0:T(8,128)(4,1)} %get-tuple-element.152) | copy-start | bytes 98308
  44.7 4.2 %copy-start.32 = (pred[256,128]{1,0:T(8,128)(4,1)S(1)}, pred[256,128]{1,0:T(8,128)(4,1)}, u32[]{:S(2)}) copy-start(pred[256,128]{1,0:T(8,128)(4,1)} %get-tuple-element.153) | copy-start | bytes 98308
  44.7 4.2 %copy-start.34 = (f32[1,2048]{1,0:T(1,128)S(1)}, f32[1,2048]{1,0:T(1,128)}, u32[]{:S(2)}) copy-start(f32[1,2048]{1,0:T(1,128)} %get-tuple-element.26) | copy-start | bytes 24580
  44.7 4.2 %copy-start.35 = (f32[1,2048]{1,0:T(1,128)S(1)}, f32[1,2048]{1,0:T(1,128)}, u32[]{:S(2)}) copy-start(f32[1,2048]{1,0:T(1,128)} %get-tuple-element.27) | copy-start | bytes 24580
  44.7 4.2 %copy-start.36 = (f32[1,2048]{1,0:T(1,128)S(1)}, f32[1,2048]{1,0:T(1,128)}, u32[]{:S(2)}) copy-start(f32[1,2048]{1,0:T(1,128)} %get-tuple-element.28) | copy-start | bytes 24580
  44.7 4.2 %copy-start.37 = (f32[1,2048]{1,0:T(1,128)S(1)}, f32[1,2048]{1,0:T(1,128)}, u32[]{:S(2)}) copy-start(f32[1,2048]{1,0:T(1,128)} %get-tuple-element.29) | copy-start | bytes 24580
  44.7 4.2 %copy-start.38 = (f32[1,2048]{1,0:T(1,128)S(1)}, f32[1,2048]{1,0:T(1,128)}, u32[]{:S(2)}) copy-start(f32[1,2048]{1,0:T(1,128)} %get-tuple-element.30) | copy-start | bytes 24580
  44.7 4.2 %copy-start.39 = (f32[1,2048]{1,0:T(1,128)S(1)}, f32[1,2048]{1,0:T(1,128)}, u32[]{:S(2)}) copy-start(f32[1,2048]{1,0:T(1,128)} %get-tuple-element.31) | copy-start | bytes 24580
  44.7 4.2 %copy-start.40 = (f32[1,2048]{1,0:T(1,128)S(1)}, f32[1,2048]{1,0:T(1,128)}, u32[]{:S(2)}) copy-start(f32[1,2048]{1,0:T(1,128)} %get-tuple-element.32) | copy-start | bytes 24580
  44.8 4.2 %copy-start.41 = (f32[1,2048]{1,0:T(1,128)S(1)}, f32[1,2048]{1,0:T(1,128)}, u32[]{:S(2)}) copy-start(f32[1,2048]{1,0:T(1,128)} %get-tuple-element.33) | copy-start | bytes 24580
  44.8 4.2 %copy-start.42 = (f32[1,2048]{1,0:T(1,128)S(1)}, f32[1,2048]{1,0:T(1,128)}, u32[]{:S(2)}) copy-start(f32[1,2048]{1,0:T(1,128)} %get-tuple-element.34) | copy-start | bytes 24580
  56.8 1.4 %copy-start = (bf16[128,4,2176]{2,1,0:T(4,128)(2,1)}, bf16[128,4,2176]{2,1,0:T(4,128)(2,1)S(1)}, u32[]{:S(2)}) copy-start(bf16[128,4,2176]{2,1,0:T(4,128)(2,1)S(1)} %all-to-all-done.rows_ref) | copy-start | bytes 6684676

commit v9 on v8

--- a/solution.py
+++ b/solution.py
@@ -103,18 +103,16 @@
 
 
 def filter_matrix(taps):
-    taps_count = taps.shape[0]
-    groups = taps.shape[1] // 128
+    taps_count, length = taps.shape
+    groups = length // 128
     half = (taps_count - 1) // 2
-    column = jnp.arange(128, dtype=jnp.int32).reshape(1, 1, 128)
-    position = jnp.arange(256, dtype=jnp.int32).reshape(1, 256, 1)
-    weights = taps.reshape(taps_count, groups, 1, 128)
-    matrix = jnp.zeros((groups, 256, 128), jnp.float32)
-    for tap_index in range(taps_count):
-        matrix = matrix + jnp.where(
-            position == column + PAD + tap_index - half, weights[tap_index], 0.0
-        )
-    return matrix
+    span = 384
+    placed = taps.T.reshape(groups, 128, taps_count)
+    lead = PAD - half
+    placed = jnp.pad(placed, ((0, 0), (0, 0), (lead, span - taps_count - lead)))
+    flat = placed.reshape(groups, 128 * span)[:, : 128 * (span - 1)]
+    skewed = flat.reshape(groups, 128, span - 1)[:, :, :256]
+    return jnp.transpose(skewed, (0, 2, 1))
 
 
 def send_kernel(line_ref, bin_ref, offset_ref, traces_ref, out_ref, *, bins, tiles):

time: 66.7 us -> 55.9 us (0.84)
  other arithmetic: 37.9 us -> 15.1 us
  local copies, waits for them, and re-layouts: 3.96 us -> 12 us
  waiting for transfers between devices: 0.01 us -> 4.4 us
  between operations: 0.94 us -> 0.14 us
    eq x16 -> x0, other arithmetic: 10.5 us -> none  [filter_matrix(): position == column + PAD + tap_index - half]
    add x1 -> x0, other arithmetic: 7.81 us -> none  [filter_matrix(): matrix + jnp.where(position == column + PAD + tap_index - half, weights[t...]
    reshape x0 -> x2, local copies, waits for them, and re-layouts: none -> 4.88 us  [the longest x1 4.53 us: filter_matrix(): skewed = flat.reshape(groups, 128, span - 1)[:, :, :256]]
    all_to_all x1, waiting for transfers between devices: 0.01 us -> 4.4 us  [body(): lax.all_to_all(send, ('line', 'tile'), split_axis=0, concat_axis=0, tiled...]
    convert_element_type x4, other arithmetic: 15.1 us -> 12.8 us  [moveout_matrix(): return matrix.astype(jnp.bfloat16)]
    unnamed x90 -> x12, local copies, waits for them, and re-layouts: 1.6 us -> 3.71 us
    another operation x1, other arithmetic: 3.67 us -> 2.23 us  [body(): jnp.stack([moveout_matrix(nmo_coef[0, offset_index], band_shift[0, offset...]
    slice x2 -> x3, local copies, waits for them, and re-layouts: 0.8 us -> 1.79 us  [the longest x2 1.59 us: filter_matrix(): skewed = flat.reshape(groups, 128, span - 1)[:, :, :256]]
  transfers between devices with their start and end apart: 1 -> 1, of which waited for: 0 -> 1; matrix products, arithmetic and copies ran while one was open for 61% -> 46% of each run, Pallas kernels for 0% -> 0%
where the time goes in v9:
time: 55.9 us; the launch traced here: 55.6 us
  other arithmetic  15.1 us (27%)
  Pallas kernels  12.1 us (22%)
  local copies, waits for them, and re-layouts  12 us (21%)
  starting transfers between devices  11.9 us (21%)
  waiting for transfers between devices  4.4 us (8%)
    convert_element_type x4, other arithmetic, moveout_matrix(): return matrix.astype(jnp.bfloat16)  12.8 us
    all_to_all x1, starting transfers between devices, body(): lax.all_to_all(send, ('line', 'tile'), split_axis=0, concat_axis=0, tiled...  11.9 us
    pallas_call x1, Pallas kernels, moveout_stack(): pl.pallas_call(moveout_kernel, grid=(groups // per_step,), in_specs=[pl.B...  8.2 us
    reshape x1, local copies, waits for them, and re-layouts, filter_matrix(): skewed = flat.reshape(groups, 128, span - 1)[:, :, :256]  4.53 us
    all_to_all x1, waiting for transfers between devices, body(): lax.all_to_all(send, ('line', 'tile'), split_axis=0, concat_axis=0, tiled...  4.4 us
    pallas_call x1, Pallas kernels, build_send(): pl.pallas_call(functools.partial(send_kernel, bins=bins, tiles=tiles), in...  3.93 us
    unnamed x12, local copies, waits for them, and re-layouts  3.71 us
    another operation x1, other arithmetic, body(): jnp.stack([moveout_matrix(nmo_coef[0, offset_index], band_shift[0, offset...  2.23 us
  transfers between devices with their start and end apart: 1, of which 1 were waited for; matrix products, arithmetic and copies ran while one was open for 46% of the time, Pallas kernels for 0%

profile of v9, /device:TPU:1, one launch (start us, length us, event | category | flops | bytes accessed | tf_op | source)
XLA Modules:
  0.0 55.6 jit_solution(2408011760165668150)
XLA Ops:
  0.0 3.9 %shard_map.82 = bf16[128,4,2176]{2,1,0:T(4,128)(2,1)} custom-call(s32[256]{0:T(256)} %line_ref.1, s32[256]{0:T(256)} %bin_ref.1, s32[2]{0:T(128)} %offset_ref.1, bf16[256,2048]{1,0:T(8,128)(2,1)} %traces_ref.1), custom_call_target="tpu_custom_call" | custom-call | tf_op jit(solution)/shard_map/pallas_call | solution.py:153
  3.9 0.0 copy-start.2
  3.9 0.0 copy-start.3
  3.9 11.9 %all-to-all-start = ((bf16[128,4,2176]{2,1,0:T(4,128)(2,1)}), bf16[128,4,2176]{2,1,0:T(4,128)(2,1)}, u32[]{:S(2)}, u32[]{:S(2)}) async-start(bf16[128,4,2176]{2,1,0:T(4,128)(2,1)} %shard_map.82), calls=%async_computation | async-start | bytes 4456448 | tf_op jit(solution)/shard_map/all_to_all | solution.py:172
  15.8 0.0 copy-done.2
  15.9 0.0 copy-start.4
  15.9 0.0 copy-start.1
  15.9 0.0 copy-done.3
  16.0 0.1 fusion
  16.1 0.1 fusion.2
  16.2 4.0 %add_convert_fusion.3 = bf16[1,16,256,128]{3,2,1,0:T(8,128)(2,1)} fusion(f32[16,128]{1,0:T(8,128)S(1)} %bitcast.74, s32[16,128]{1,0:T(8,128)S(1)} %get-tuple-element.52, f32[16,128]{1,0:T(8,128)S(1)} %bitcast.75, s32[16,128]{1,0:T(8,128)S(1)} %get-tuple-element.51, f32[16,128]{1,0:T(8,128)S(1)} %bitcast.76, s32[16,128]{1,0:T(8,128)S(1)} %get-tuple-element.50, ...), kind=kLoop, calls=%fused_computation.28 | loop fusion | flops 12582912 | bytes 1179648 | tf_op jit(solution)/shard_map/convert_element_type | solution.py:26
  20.2 0.0 copy-done.4
  20.2 0.0 copy-done.1
  20.2 0.4 copy.13
  20.6 0.7 %pad.4 = f32[16,128,384]{2,1,0:T(8,128)S(1)} pad(f32[16,128,31]{2,1,0:T(8,128)S(1)} %bitcast.47, f32[]{:T(128)} %constant.8.clone.1), padding=0_0x0_0x1_352 | pad | bytes 3399684 | tf_op jit(solution)/shard_map/jit(_pad)/pad | solution.py:112
  21.3 1.8 %copy.15 = f32[2,8,128,384]{3,1,2,0:T(8,128)S(1)} copy(f32[2,8,128,384]{3,2,1,0:T(8,128)S(1)} %bitcast.44) | data formatting | bytes 6291456
  23.1 0.2 slice.264
  23.3 4.5 %reshape.884 = f32[16,128,383]{2,1,0:T(8,128)} reshape(f32[16,49024]{1,0:T(8,128)S(1)} %slice.264) | data formatting | bytes 6275072 | tf_op jit(solution)/shard_map/reshape | solution.py:114
  27.8 0.0 slice-start
  27.8 1.6 %slice-done = f32[16,128,256]{2,1,0:T(8,128)S(1)} async-done(((f32[16,128,383]{2,1,0:T(8,128)}), f32[16,128,256]{2,1,0:T(8,128)S(1)}, s32[]{:S(2)}) %slice-start) | async-done | bytes 2097176 | tf_op jit(solution)/shard_map/slice | solution.py:114
  29.4 1.9 %copy.14 = f32[16,128,256]{1,2,0:T(8,128)} copy(f32[16,128,256]{2,1,0:T(8,128)S(1)} %slice-done) | data formatting | bytes 4194304
  31.3 0.0 copy-start
  31.3 0.7 %copy.12.fold_ref = f32[64,1]{1,0:T(8,128)} copy(f32[64,1]{0,1:T(1,128)S(1)} %convert_bitcast_fusion) | data formatting | bytes 512 | tf_op jit(solution)/shard_map/convert_element_type | solution.py:185
  32.0 2.9 %add_convert_fusion.2 = bf16[1,16,256,128]{3,2,1,0:T(8,128)(2,1)S(1)} fusion(f32[16,128]{1,0:T(8,128)S(1)} %bitcast.71, s32[16,128]{1,0:T(8,128)S(1)} %get-tuple-element.60, f32[16,128]{1,0:T(8,128)S(1)} %bitcast.70, s32[16,128]{1,0:T(8,128)S(1)} %get-tuple-element.59, f32[16,128]{1,0:T(8,128)S(1)} %bitcast.69, s32[16,128]{1,0:T(8,128)S(1)} %get-tuple-element.58, ...), kind=kLoop, calls=%fused_computation.19 | loop fusion | flops 12582912 | bytes 1179648 | tf_op jit(solution)/shard_map/convert_element_type | solution.py:26
  34.9 2.9 %add_convert_fusion.1 = bf16[1,16,256,128]{3,2,1,0:T(8,128)(2,1)S(1)} fusion(f32[16,128]{1,0:T(8,128)S(1)} %bitcast.58, s32[16,128]{1,0:T(8,128)S(1)} %get-tuple-element.68, f32[16,128]{1,0:T(8,128)S(1)} %bitcast.59, s32[16,128]{1,0:T(8,128)S(1)} %get-tuple-element.67, f32[16,128]{1,0:T(8,128)S(1)} %bitcast.60, s32[16,128]{1,0:T(8,128)S(1)} %get-tuple-element.66, ...), kind=kLoop, calls=%fused_computation.10 | loop fusion | flops 12582912 | bytes 1179648 | tf_op jit(solution)/shard_map/convert_element_type | solution.py:26
  37.9 2.9 %add_convert_fusion = bf16[1,16,256,128]{3,2,1,0:T(8,128)(2,1)S(1)} fusion(f32[16,128]{1,0:T(8,128)S(1)} %bitcast.55, s32[16,128]{1,0:T(8,128)S(1)} %get-tuple-element.76, f32[16,128]{1,0:T(8,128)S(1)} %bitcast.54, s32[16,128]{1,0:T(8,128)S(1)} %get-tuple-element.75, f32[16,128]{1,0:T(8,128)S(1)} %bitcast.53, s32[16,128]{1,0:T(8,128)S(1)} %get-tuple-element.74, ...), kind=kLoop, calls=%fused_computation.1 | loop fusion | flops 12582912 | bytes 1179648 | tf_op jit(solution)/shard_map/convert_element_type | solution.py:26
  40.8 0.0 copy-done
  40.8 2.2 %pad_maximum_fusion.matrix_ref = bf16[4,16,256,128]{3,2,1,0:T(8,128)(2,1)} fusion(bf16[1,16,256,128]{3,2,1,0:T(8,128)(2,1)S(1)} %add_convert_fusion, bf16[1,16,256,128]{3,2,1,0:T(8,128)(2,1)S(1)} %add_convert_fusion.1, bf16[1,16,256,128]{3,2,1,0:T(8,128)(2,1)S(1)} %add_convert_fusion.2, bf16[1,16,256,128]{3,2,1,0:T(8,128)(2,1)S(1)} %copy-done), kind=kLoop, calls=%fused_computation | loop fusion | flops 6291456 | bytes 8388608 | tf_op jit(solution)/shard_map/stack | solution.py:179
  43.0 4.4 %all-to-all-done.rows_ref = bf16[128,4,2176]{2,1,0:T(4,128)(2,1)} async-done(((bf16[128,4,2176]{2,1,0:T(4,128)(2,1)}), bf16[128,4,2176]{2,1,0:T(4,128)(2,1)}, u32[]{:S(2)}, u32[]{:S(2)}) %all-to-all-start) | async-done | bytes 2228256 | tf_op jit(solution)/shard_map/all_to_all | solution.py:172
  47.4 8.2 %shard_map.83 = f32[64,2048]{1,0:T(8,128)} custom-call(bf16[128,4,2176]{2,1,0:T(4,128)(2,1)} %all-to-all-done.rows_ref, bf16[4,16,256,128]{3,2,1,0:T(8,128)(2,1)} %pad_maximum_fusion.matrix_ref, f32[16,256,128]{2,1,0:T(8,128)} %bitcast.46, f32[64,1]{1,0:T(8,128)} %copy.12.fold_ref), custom_call_target="tpu_custom_call" | custom-call | tf_op jit(solution)/shard_map/pallas_call | solution.py:87
  (7 shorter events, 0.1 us)
Async XLA Ops:
  3.9 11.9 %copy-start.2 = (bf16[1,4,8,2048]{3,2,1,0:T(8,128)(2,1)S(1)}, bf16[1,4,8,2048]{3,2,1,0:T(8,128)(2,1)}, u32[]{:S(2)}) copy-start(bf16[1,4,8,2048]{3,2,1,0:T(8,128)(2,1)} %param.12) | copy-start | bytes 393220
  3.9 12.0 %copy-start.3 = (s32[1,4,2048]{2,1,0:T(4,128)S(1)}, s32[1,4,2048]{2,1,0:T(4,128)}, u32[]{:S(2)}) copy-start(s32[1,4,2048]{2,1,0:T(4,128)} %param.13) | copy-start | bytes 98308
  3.9 43.5 %all-to-all-start = ((bf16[128,4,2176]{2,1,0:T(4,128)(2,1)}), bf16[128,4,2176]{2,1,0:T(4,128)(2,1)}, u32[]{:S(2)}, u32[]{:S(2)}) async-start(bf16[128,4,2176]{2,1,0:T(4,128)(2,1)} %shard_map.82), calls=%async_computation | async-start | bytes 4456448 | tf_op jit(solution)/shard_map/all_to_all | solution.py:172
  15.9 4.4 %copy-start.4 = (s32[1,64]{1,0:T(1,128)S(1)}, s32[1,64]{1,0:T(1,128)}, u32[]{:S(2)}) copy-start(s32[1,64]{1,0:T(1,128)} %param.15) | copy-start | bytes 772
  15.9 4.4 %copy-start.1 = (f32[31,2048]{1,0:T(8,128)S(1)}, f32[31,2048]{1,0:T(8,128)}, u32[]{:S(2)}) copy-start(f32[31,2048]{1,0:T(8,128)} %param.14) | copy-start | bytes 761860
  27.8 1.6 %slice-start = ((f32[16,128,383]{2,1,0:T(8,128)}), f32[16,128,256]{2,1,0:T(8,128)S(1)}, s32[]{:S(2)}) async-start(f32[16,128,383]{2,1,0:T(8,128)} %reshape.884), calls=%async_computation.1 | async-start | bytes 4194304 | tf_op jit(solution)/shard_map/slice | solution.py:114
  31.3 9.5 %copy-start = (bf16[1,16,256,128]{3,2,1,0:T(8,128)(2,1)S(1)}, bf16[1,16,256,128]{3,2,1,0:T(8,128)(2,1)}, u32[]{:S(2)}) copy-start(bf16[1,16,256,128]{3,2,1,0:T(8,128)(2,1)} %add_convert_fusion.3) | copy-start | bytes 3145732

commit v10 on v9

--- a/solution.py
+++ b/solution.py
@@ -28,8 +28,9 @@
 
 def moveout_kernel(rows_ref, matrix_ref, taps_ref, fold_ref, out_ref, part_ref, stack_ref):
     step = pl.program_id(0)
+    last = pl.num_programs(0) - 1
     classes, per_step = matrix_ref.shape[0], matrix_ref.shape[1]
-    bins, length = out_ref.shape
+    bins, length = stack_ref.shape[0], stack_ref.shape[1] - 256
     sources, capacity, width = rows_ref.shape
     slot_count = sources * capacity
 
@@ -53,30 +54,32 @@
             ]
         part_ref[:, length:] = jnp.zeros((classes * 2 * bins, width - length), jnp.bfloat16)
 
-    for inner in range(per_step):
-        start = pl.multiple_of((step * per_step + inner) * 128, 128)
-        total = jnp.zeros((bins, 128), jnp.float32)
-        for offset_index in range(classes):
-            base = offset_index * 2 * bins
-            window = part_ref[base:base + 2 * bins, pl.ds(start, 256)]
-            product = jnp.dot(
-                window, matrix_ref[offset_index, inner], preferred_element_type=jnp.float32
-            )
-            total = total + product[:bins] + product[bins:]
-        stack_ref[:, pl.ds(start + 128, 128)] = total
-
-    @pl.when(step == pl.num_programs(0) - 1)
+    @pl.when(step < last)
     def _():
-        for group in range(length // 128):
-            start = group * 128
-            window = stack_ref[:, start + 128 - PAD:start + 384 - PAD]
+        for inner in range(per_step):
+            start = pl.multiple_of((step * per_step + inner) * 128, 128)
+            total = jnp.zeros((bins, 128), jnp.float32)
+            for offset_index in range(classes):
+                base = offset_index * 2 * bins
+                window = part_ref[base:base + 2 * bins, pl.ds(start, 256)]
+                product = jnp.dot(
+                    window, matrix_ref[offset_index, inner], preferred_element_type=jnp.float32
+                )
+                total = total + product[:bins] + product[bins:]
+            stack_ref[:, pl.ds(start + 128, 128)] = total
+
+    @pl.when(step > 0)
+    def _():
+        for inner in range(per_step):
+            start = pl.multiple_of(((step - 1) * per_step + inner) * 128, 128)
+            window = stack_ref[:, pl.ds(start, 384)][:, 128 - PAD:384 - PAD]
             filtered = jnp.dot(
                 window,
-                taps_ref[group],
+                taps_ref[inner],
                 precision=lax.Precision.HIGHEST,
                 preferred_element_type=jnp.float32,
             )
-            out_ref[:, start:start + 128] = filtered / fold_ref[...]
+            out_ref[:, inner * 128:(inner + 1) * 128] = filtered / fold_ref[...]
 
 
 def moveout_stack(rows, matrices, taps, fold_share, length):
@@ -84,16 +87,19 @@
     bins = fold_share.shape[0]
     classes, groups = matrices.shape[0], matrices.shape[1]
     per_step = 4
+    steps = groups // per_step
     return pl.pallas_call(
         moveout_kernel,
-        grid=(groups // per_step,),
+        grid=(steps + 1,),
         in_specs=[
             pl.BlockSpec((sources, capacity, width), lambda g: (0, 0, 0)),
-            pl.BlockSpec((classes, per_step, 256, 128), lambda g: (0, g, 0, 0)),
-            pl.BlockSpec(taps.shape, lambda g: (0, 0, 0)),
+            pl.BlockSpec(
+                (classes, per_step, 256, 128), lambda g: (0, jnp.minimum(g, steps - 1), 0, 0)
+            ),
+            pl.BlockSpec((per_step, 256, 128), lambda g: (jnp.maximum(g - 1, 0), 0, 0)),
             pl.BlockSpec((bins, 1), lambda g: (0, 0)),
         ],
-        out_specs=pl.BlockSpec((bins, length), lambda g: (0, 0)),
+        out_specs=pl.BlockSpec((bins, per_step * 128), lambda g: (0, jnp.maximum(g - 1, 0))),
         out_shape=jax.ShapeDtypeStruct((bins, length), jnp.float32),
         scratch_shapes=[
             pltpu.VMEM((classes * 2 * bins, width), jnp.bfloat16),
@@ -126,16 +132,20 @@
     class_id = jnp.zeros((trace_count, 1), jnp.int32)
     for block_index in range(offset_ref.shape[0]):
         class_id = jnp.where(trace_index // block == block_index, offset_ref[block_index], class_id)
-    dest = line_id * tiles + bin_id // bins
-    onehot = (dest == lax.broadcasted_iota(jnp.int32, (trace_count, dests), 1)).astype(jnp.bfloat16)
+    line_row = line_ref[...].reshape(1, trace_count)
+    bin_row = bin_ref[...].reshape(1, trace_count)
+    dest_row = line_row * tiles + bin_row // bins
+    onehot = (lax.broadcasted_iota(jnp.int32, (dests, trace_count), 0) == dest_row).astype(
+        jnp.bfloat16
+    )
     row = lax.broadcasted_iota(jnp.int32, (trace_count, trace_count), 0)
     col = lax.broadcasted_iota(jnp.int32, (trace_count, trace_count), 1)
-    lower = (col <= row).astype(jnp.bfloat16)
-    running = jnp.dot(lower, onehot, preferred_element_type=jnp.float32)
-    rank = jnp.sum(running * onehot.astype(jnp.float32), axis=1, keepdims=True) - 1.0
-    slot = dest.astype(jnp.float32) * capacity + rank
-    wanted = lax.broadcasted_iota(jnp.int32, (trace_count, slots), 1).astype(jnp.float32)
-    select = (wanted == slot).astype(jnp.float32).T.astype(jnp.bfloat16)
+    upper = (row <= col).astype(jnp.bfloat16)
+    running = jnp.dot(onehot, upper, preferred_element_type=jnp.float32)
+    rank = jnp.sum(running * onehot.astype(jnp.float32), axis=0, keepdims=True) - 1.0
+    slot = dest_row.astype(jnp.float32) * capacity + rank
+    wanted = lax.broadcasted_iota(jnp.int32, (slots, trace_count), 0).astype(jnp.float32)
+    select = (wanted == slot).astype(jnp.bfloat16)
     lane = lax.broadcasted_iota(jnp.int32, (trace_count, width - length), 1)
     meta = jnp.where(
         lane == 0, bin_id % bins, jnp.where(lane == 1, class_id, jnp.where(lane == 2, 1, 0))

time: 55.9 us -> 55.4 us (level)
  no operation moved by 1% of the time
where the time goes in v10:
time: 55.4 us; the launch traced here: 55.1 us
  other arithmetic  15.1 us (27%)
  local copies, waits for them, and re-layouts  12 us (22%)
  starting transfers between devices  11.9 us (21%)
  Pallas kernels  11.6 us (21%)
  waiting for transfers between devices  4.4 us (8%)
    convert_element_type x4, other arithmetic, moveout_matrix(): return matrix.astype(jnp.bfloat16)  12.8 us
    all_to_all x1, starting transfers between devices, body(): lax.all_to_all(send, ('line', 'tile'), split_axis=0, concat_axis=0, tiled...  11.9 us
    pallas_call x1, Pallas kernels, moveout_stack(): pl.pallas_call(moveout_kernel, grid=(steps + 1,), in_specs=[pl.BlockSpec(...  7.91 us
    reshape x1, local copies, waits for them, and re-layouts, filter_matrix(): skewed = flat.reshape(groups, 128, span - 1)[:, :, :256]  4.53 us
    all_to_all x1, waiting for transfers between devices, body(): lax.all_to_all(send, ('line', 'tile'), split_axis=0, concat_axis=0, tiled...  4.4 us
    unnamed x12, local copies, waits for them, and re-layouts  3.71 us
    pallas_call x1, Pallas kernels, build_send(): pl.pallas_call(functools.partial(send_kernel, bins=bins, tiles=tiles), in...  3.67 us
    another operation x1, other arithmetic, body(): jnp.stack([moveout_matrix(nmo_coef[0, offset_index], band_shift[0, offset...  2.23 us
  transfers between devices with their start and end apart: 1, of which 1 were waited for; matrix products, arithmetic and copies ran while one was open for 46% of the time, Pallas kernels for 0%

profile of v10, /device:TPU:1, one launch (start us, length us, event | category | flops | bytes accessed | tf_op | source)
XLA Modules:
  0.0 55.1 jit_solution(14713113529513098076)
XLA Ops:
  0.0 3.7 %shard_map.82 = bf16[128,4,2176]{2,1,0:T(4,128)(2,1)} custom-call(s32[256]{0:T(256)} %line_ref.1, s32[256]{0:T(256)} %bin_ref.1, s32[2]{0:T(128)} %offset_ref.1, bf16[256,2048]{1,0:T(8,128)(2,1)} %traces_ref.1), custom_call_target="tpu_custom_call" | custom-call | tf_op jit(solution)/shard_map/pallas_call | solution.py:163
  3.7 0.0 copy-start.2
  3.7 0.0 copy-start.3
  3.7 11.9 %all-to-all-start = ((bf16[128,4,2176]{2,1,0:T(4,128)(2,1)}), bf16[128,4,2176]{2,1,0:T(4,128)(2,1)}, u32[]{:S(2)}, u32[]{:S(2)}) async-start(bf16[128,4,2176]{2,1,0:T(4,128)(2,1)} %shard_map.82), calls=%async_computation | async-start | bytes 4456448 | tf_op jit(solution)/shard_map/all_to_all | solution.py:182
  15.6 0.0 copy-done.2
  15.6 0.0 copy-start.4
  15.6 0.0 copy-start.1
  15.6 0.0 copy-done.3
  15.7 0.1 fusion
  15.8 0.1 fusion.2
  15.9 4.0 %add_convert_fusion.3 = bf16[1,16,256,128]{3,2,1,0:T(8,128)(2,1)} fusion(f32[16,128]{1,0:T(8,128)S(1)} %bitcast.74, s32[16,128]{1,0:T(8,128)S(1)} %get-tuple-element.52, f32[16,128]{1,0:T(8,128)S(1)} %bitcast.75, s32[16,128]{1,0:T(8,128)S(1)} %get-tuple-element.51, f32[16,128]{1,0:T(8,128)S(1)} %bitcast.76, s32[16,128]{1,0:T(8,128)S(1)} %get-tuple-element.50, ...), kind=kLoop, calls=%fused_computation.28 | loop fusion | flops 12582912 | bytes 1179648 | tf_op jit(solution)/shard_map/convert_element_type | solution.py:26
  20.0 0.0 copy-done.4
  20.0 0.0 copy-done.1
  20.0 0.4 copy.13
  20.3 0.7 %pad.4 = f32[16,128,384]{2,1,0:T(8,128)S(1)} pad(f32[16,128,31]{2,1,0:T(8,128)S(1)} %bitcast.47, f32[]{:T(128)} %constant.8.clone.1), padding=0_0x0_0x1_352 | pad | bytes 3399684 | tf_op jit(solution)/shard_map/jit(_pad)/pad | solution.py:118
  21.0 1.8 %copy.15 = f32[2,8,128,384]{3,1,2,0:T(8,128)S(1)} copy(f32[2,8,128,384]{3,2,1,0:T(8,128)S(1)} %bitcast.44) | data formatting | bytes 6291456
  22.8 0.2 slice.264
  23.0 4.5 %reshape.884 = f32[16,128,383]{2,1,0:T(8,128)} reshape(f32[16,49024]{1,0:T(8,128)S(1)} %slice.264) | data formatting | bytes 6275072 | tf_op jit(solution)/shard_map/reshape | solution.py:120
  27.6 0.0 slice-start
  27.6 1.6 %slice-done = f32[16,128,256]{2,1,0:T(8,128)S(1)} async-done(((f32[16,128,383]{2,1,0:T(8,128)}), f32[16,128,256]{2,1,0:T(8,128)S(1)}, s32[]{:S(2)}) %slice-start) | async-done | bytes 2097176 | tf_op jit(solution)/shard_map/slice | solution.py:120
  29.1 1.9 %copy.14 = f32[16,128,256]{1,2,0:T(8,128)} copy(f32[16,128,256]{2,1,0:T(8,128)S(1)} %slice-done) | data formatting | bytes 4194304
  31.0 0.0 copy-start
  31.0 0.7 %copy.12.fold_ref = f32[64,1]{1,0:T(8,128)} copy(f32[64,1]{0,1:T(1,128)S(1)} %convert_bitcast_fusion) | data formatting | bytes 512 | tf_op jit(solution)/shard_map/convert_element_type | solution.py:195
  31.7 2.9 %add_convert_fusion.2 = bf16[1,16,256,128]{3,2,1,0:T(8,128)(2,1)S(1)} fusion(f32[16,128]{1,0:T(8,128)S(1)} %bitcast.71, s32[16,128]{1,0:T(8,128)S(1)} %get-tuple-element.60, f32[16,128]{1,0:T(8,128)S(1)} %bitcast.70, s32[16,128]{1,0:T(8,128)S(1)} %get-tuple-element.59, f32[16,128]{1,0:T(8,128)S(1)} %bitcast.69, s32[16,128]{1,0:T(8,128)S(1)} %get-tuple-element.58, ...), kind=kLoop, calls=%fused_computation.19 | loop fusion | flops 12582912 | bytes 1179648 | tf_op jit(solution)/shard_map/convert_element_type | solution.py:26
  34.7 2.9 %add_convert_fusion.1 = bf16[1,16,256,128]{3,2,1,0:T(8,128)(2,1)S(1)} fusion(f32[16,128]{1,0:T(8,128)S(1)} %bitcast.58, s32[16,128]{1,0:T(8,128)S(1)} %get-tuple-element.68, f32[16,128]{1,0:T(8,128)S(1)} %bitcast.59, s32[16,128]{1,0:T(8,128)S(1)} %get-tuple-element.67, f32[16,128]{1,0:T(8,128)S(1)} %bitcast.60, s32[16,128]{1,0:T(8,128)S(1)} %get-tuple-element.66, ...), kind=kLoop, calls=%fused_computation.10 | loop fusion | flops 12582912 | bytes 1179648 | tf_op jit(solution)/shard_map/convert_element_type | solution.py:26
  37.6 2.9 %add_convert_fusion = bf16[1,16,256,128]{3,2,1,0:T(8,128)(2,1)S(1)} fusion(f32[16,128]{1,0:T(8,128)S(1)} %bitcast.55, s32[16,128]{1,0:T(8,128)S(1)} %get-tuple-element.76, f32[16,128]{1,0:T(8,128)S(1)} %bitcast.54, s32[16,128]{1,0:T(8,128)S(1)} %get-tuple-element.75, f32[16,128]{1,0:T(8,128)S(1)} %bitcast.53, s32[16,128]{1,0:T(8,128)S(1)} %get-tuple-element.74, ...), kind=kLoop, calls=%fused_computation.1 | loop fusion | flops 12582912 | bytes 1179648 | tf_op jit(solution)/shard_map/convert_element_type | solution.py:26
  40.5 0.0 copy-done
  40.5 2.2 %pad_maximum_fusion.matrix_ref = bf16[4,16,256,128]{3,2,1,0:T(8,128)(2,1)} fusion(bf16[1,16,256,128]{3,2,1,0:T(8,128)(2,1)S(1)} %add_convert_fusion, bf16[1,16,256,128]{3,2,1,0:T(8,128)(2,1)S(1)} %add_convert_fusion.1, bf16[1,16,256,128]{3,2,1,0:T(8,128)(2,1)S(1)} %add_convert_fusion.2, bf16[1,16,256,128]{3,2,1,0:T(8,128)(2,1)S(1)} %copy-done), kind=kLoop, calls=%fused_computation | loop fusion | flops 6291456 | bytes 8388608 | tf_op jit(solution)/shard_map/stack | solution.py:189
  42.8 4.4 %all-to-all-done.rows_ref = bf16[128,4,2176]{2,1,0:T(4,128)(2,1)} async-done(((bf16[128,4,2176]{2,1,0:T(4,128)(2,1)}), bf16[128,4,2176]{2,1,0:T(4,128)(2,1)}, u32[]{:S(2)}, u32[]{:S(2)}) %all-to-all-start) | async-done | bytes 2228256 | tf_op jit(solution)/shard_map/all_to_all | solution.py:182
  47.2 7.9 %shard_map.83 = f32[64,2048]{1,0:T(8,128)} custom-call(bf16[128,4,2176]{2,1,0:T(4,128)(2,1)} %all-to-all-done.rows_ref, bf16[4,16,256,128]{3,2,1,0:T(8,128)(2,1)} %pad_maximum_fusion.matrix_ref, f32[16,256,128]{2,1,0:T(8,128)} %bitcast.46, f32[64,1]{1,0:T(8,128)} %copy.12.fold_ref), custom_call_target="tpu_custom_call" | custom-call | tf_op jit(solution)/shard_map/pallas_call | solution.py:91
  (7 shorter events, 0.1 us)
Async XLA Ops:
  3.7 11.9 %copy-start.2 = (bf16[1,4,8,2048]{3,2,1,0:T(8,128)(2,1)S(1)}, bf16[1,4,8,2048]{3,2,1,0:T(8,128)(2,1)}, u32[]{:S(2)}) copy-start(bf16[1,4,8,2048]{3,2,1,0:T(8,128)(2,1)} %param.12) | copy-start | bytes 393220
  3.7 12.0 %copy-start.3 = (s32[1,4,2048]{2,1,0:T(4,128)S(1)}, s32[1,4,2048]{2,1,0:T(4,128)}, u32[]{:S(2)}) copy-start(s32[1,4,2048]{2,1,0:T(4,128)} %param.13) | copy-start | bytes 98308
  3.7 43.5 %all-to-all-start = ((bf16[128,4,2176]{2,1,0:T(4,128)(2,1)}), bf16[128,4,2176]{2,1,0:T(4,128)(2,1)}, u32[]{:S(2)}, u32[]{:S(2)}) async-start(bf16[128,4,2176]{2,1,0:T(4,128)(2,1)} %shard_map.82), calls=%async_computation | async-start | bytes 4456448 | tf_op jit(solution)/shard_map/all_to_all | solution.py:182
  15.6 4.4 %copy-start.4 = (s32[1,64]{1,0:T(1,128)S(1)}, s32[1,64]{1,0:T(1,128)}, u32[]{:S(2)}) copy-start(s32[1,64]{1,0:T(1,128)} %param.15) | copy-start | bytes 772
  15.6 4.4 %copy-start.1 = (f32[31,2048]{1,0:T(8,128)S(1)}, f32[31,2048]{1,0:T(8,128)}, u32[]{:S(2)}) copy-start(f32[31,2048]{1,0:T(8,128)} %param.14) | copy-start | bytes 761860
  27.6 1.6 %slice-start = ((f32[16,128,383]{2,1,0:T(8,128)}), f32[16,128,256]{2,1,0:T(8,128)S(1)}, s32[]{:S(2)}) async-start(f32[16,128,383]{2,1,0:T(8,128)} %reshape.884), calls=%async_computation.1 | async-start | bytes 4194304 | tf_op jit(solution)/shard_map/slice | solution.py:120
  31.0 9.5 %copy-start = (bf16[1,16,256,128]{3,2,1,0:T(8,128)(2,1)S(1)}, bf16[1,16,256,128]{3,2,1,0:T(8,128)(2,1)}, u32[]{:S(2)}) copy-start(bf16[1,16,256,128]{3,2,1,0:T(8,128)(2,1)} %add_convert_fusion.3) | copy-start | bytes 3145732

commit v11 on v10

--- a/solution.py
+++ b/solution.py
@@ -134,7 +134,7 @@
         class_id = jnp.where(trace_index // block == block_index, offset_ref[block_index], class_id)
     line_row = line_ref[...].reshape(1, trace_count)
     bin_row = bin_ref[...].reshape(1, trace_count)
-    dest_row = line_row * tiles + bin_row // bins
+    dest_row = (bin_row // bins) * (dests // tiles) + line_row
     onehot = (lax.broadcasted_iota(jnp.int32, (dests, trace_count), 0) == dest_row).astype(
         jnp.bfloat16
     )
@@ -181,7 +181,7 @@
     )
     received = lax.all_to_all(
         send,
-        ("line", "tile"),
+        ("tile", "line"),
         split_axis=0,
         concat_axis=0,
         tiled=True,

time: 55.4 us -> 53.4 us (0.964)
  waiting for transfers between devices: 4.4 us -> 2.43 us
    all_to_all x1, waiting for transfers between devices: 4.4 us -> 2.43 us  [body(): lax.all_to_all(send, ('tile', 'line'), split_axis=0, concat_axis=0, tiled...]
  transfers between devices with their start and end apart: 1 -> 1, of which waited for: 1 -> 1; matrix products, arithmetic and copies ran while one was open for 46% -> 48% of each run, Pallas kernels for 0% -> 0%
where the time goes in v11:
time: 53.4 us; the launch traced here: 53.1 us
  other arithmetic  15.1 us (28%)
  local copies, waits for them, and re-layouts  12 us (22%)
  starting transfers between devices  11.9 us (22%)
  Pallas kernels  11.6 us (22%)
  waiting for transfers between devices  2.43 us (5%)
    convert_element_type x4, other arithmetic, moveout_matrix(): return matrix.astype(jnp.bfloat16)  12.8 us
    all_to_all x1, starting transfers between devices, body(): lax.all_to_all(send, ('tile', 'line'), split_axis=0, concat_axis=0, tiled...  11.9 us
    pallas_call x1, Pallas kernels, moveout_stack(): pl.pallas_call(moveout_kernel, grid=(steps + 1,), in_specs=[pl.BlockSpec(...  7.91 us
    reshape x1, local copies, waits for them, and re-layouts, filter_matrix(): skewed = flat.reshape(groups, 128, span - 1)[:, :, :256]  4.53 us
    unnamed x12, local copies, waits for them, and re-layouts  3.71 us
    pallas_call x1, Pallas kernels, build_send(): pl.pallas_call(functools.partial(send_kernel, bins=bins, tiles=tiles), in...  3.67 us
    all_to_all x1, waiting for transfers between devices, body(): lax.all_to_all(send, ('tile', 'line'), split_axis=0, concat_axis=0, tiled...  2.43 us
    another operation x1, other arithmetic, body(): jnp.stack([moveout_matrix(nmo_coef[0, offset_index], band_shift[0, offset...  2.23 us
  transfers between devices with their start and end apart: 1, of which 1 were waited for; matrix products, arithmetic and copies ran while one was open for 48% of the time, Pallas kernels for 0%

profile of v11, /device:TPU:1, one launch (start us, length us, event | category | flops | bytes accessed | tf_op | source)
XLA Modules:
  0.0 53.1 jit_solution(12258200471576090860)
XLA Ops:
  0.0 3.7 %shard_map.82 = bf16[128,4,2176]{2,1,0:T(4,128)(2,1)} custom-call(s32[256]{0:T(256)} %line_ref.1, s32[256]{0:T(256)} %bin_ref.1, s32[2]{0:T(128)} %offset_ref.1, bf16[256,2048]{1,0:T(8,128)(2,1)} %traces_ref.1), custom_call_target="tpu_custom_call" | custom-call | tf_op jit(solution)/shard_map/pallas_call | solution.py:163
  3.7 0.0 copy-start.2
  3.7 0.0 copy-start.3
  3.7 11.9 %all-to-all-start = ((bf16[128,4,2176]{2,1,0:T(4,128)(2,1)}), bf16[128,4,2176]{2,1,0:T(4,128)(2,1)}, u32[]{:S(2)}, u32[]{:S(2)}) async-start(bf16[128,4,2176]{2,1,0:T(4,128)(2,1)} %shard_map.82), calls=%async_computation | async-start | bytes 4456448 | tf_op jit(solution)/shard_map/all_to_all | solution.py:182
  15.6 0.0 copy-done.2
  15.6 0.0 copy-start.4
  15.6 0.0 copy-start.1
  15.6 0.0 copy-done.3
  15.7 0.1 fusion
  15.8 0.1 fusion.2
  15.9 4.0 %add_convert_fusion.3 = bf16[1,16,256,128]{3,2,1,0:T(8,128)(2,1)} fusion(f32[16,128]{1,0:T(8,128)S(1)} %bitcast.74, s32[16,128]{1,0:T(8,128)S(1)} %get-tuple-element.52, f32[16,128]{1,0:T(8,128)S(1)} %bitcast.75, s32[16,128]{1,0:T(8,128)S(1)} %get-tuple-element.51, f32[16,128]{1,0:T(8,128)S(1)} %bitcast.76, s32[16,128]{1,0:T(8,128)S(1)} %get-tuple-element.50, ...), kind=kLoop, calls=%fused_computation.28 | loop fusion | flops 12582912 | bytes 1179648 | tf_op jit(solution)/shard_map/convert_element_type | solution.py:26
  20.0 0.0 copy-done.4
  20.0 0.0 copy-done.1
  20.0 0.4 copy.13
  20.3 0.7 %pad.4 = f32[16,128,384]{2,1,0:T(8,128)S(1)} pad(f32[16,128,31]{2,1,0:T(8,128)S(1)} %bitcast.47, f32[]{:T(128)} %constant.8.clone.1), padding=0_0x0_0x1_352 | pad | bytes 3399684 | tf_op jit(solution)/shard_map/jit(_pad)/pad | solution.py:118
  21.0 1.8 %copy.15 = f32[2,8,128,384]{3,1,2,0:T(8,128)S(1)} copy(f32[2,8,128,384]{3,2,1,0:T(8,128)S(1)} %bitcast.44) | data formatting | bytes 6291456
  22.8 0.2 slice.264
  23.0 4.5 %reshape.884 = f32[16,128,383]{2,1,0:T(8,128)} reshape(f32[16,49024]{1,0:T(8,128)S(1)} %slice.264) | data formatting | bytes 6275072 | tf_op jit(solution)/shard_map/reshape | solution.py:120
  27.6 0.0 slice-start
  27.6 1.6 %slice-done = f32[16,128,256]{2,1,0:T(8,128)S(1)} async-done(((f32[16,128,383]{2,1,0:T(8,128)}), f32[16,128,256]{2,1,0:T(8,128)S(1)}, s32[]{:S(2)}) %slice-start) | async-done | bytes 2097176 | tf_op jit(solution)/shard_map/slice | solution.py:120
  29.1 1.9 %copy.14 = f32[16,128,256]{1,2,0:T(8,128)} copy(f32[16,128,256]{2,1,0:T(8,128)S(1)} %slice-done) | data formatting | bytes 4194304
  31.0 0.0 copy-start
  31.0 0.7 %copy.12.fold_ref = f32[64,1]{1,0:T(8,128)} copy(f32[64,1]{0,1:T(1,128)S(1)} %convert_bitcast_fusion) | data formatting | bytes 512 | tf_op jit(solution)/shard_map/convert_element_type | solution.py:195
  31.7 2.9 %add_convert_fusion.2 = bf16[1,16,256,128]{3,2,1,0:T(8,128)(2,1)S(1)} fusion(f32[16,128]{1,0:T(8,128)S(1)} %bitcast.71, s32[16,128]{1,0:T(8,128)S(1)} %get-tuple-element.60, f32[16,128]{1,0:T(8,128)S(1)} %bitcast.70, s32[16,128]{1,0:T(8,128)S(1)} %get-tuple-element.59, f32[16,128]{1,0:T(8,128)S(1)} %bitcast.69, s32[16,128]{1,0:T(8,128)S(1)} %get-tuple-element.58, ...), kind=kLoop, calls=%fused_computation.19 | loop fusion | flops 12582912 | bytes 1179648 | tf_op jit(solution)/shard_map/convert_element_type | solution.py:26
  34.7 2.9 %add_convert_fusion.1 = bf16[1,16,256,128]{3,2,1,0:T(8,128)(2,1)S(1)} fusion(f32[16,128]{1,0:T(8,128)S(1)} %bitcast.58, s32[16,128]{1,0:T(8,128)S(1)} %get-tuple-element.68, f32[16,128]{1,0:T(8,128)S(1)} %bitcast.59, s32[16,128]{1,0:T(8,128)S(1)} %get-tuple-element.67, f32[16,128]{1,0:T(8,128)S(1)} %bitcast.60, s32[16,128]{1,0:T(8,128)S(1)} %get-tuple-element.66, ...), kind=kLoop, calls=%fused_computation.10 | loop fusion | flops 12582912 | bytes 1179648 | tf_op jit(solution)/shard_map/convert_element_type | solution.py:26
  37.6 2.9 %add_convert_fusion = bf16[1,16,256,128]{3,2,1,0:T(8,128)(2,1)S(1)} fusion(f32[16,128]{1,0:T(8,128)S(1)} %bitcast.55, s32[16,128]{1,0:T(8,128)S(1)} %get-tuple-element.76, f32[16,128]{1,0:T(8,128)S(1)} %bitcast.54, s32[16,128]{1,0:T(8,128)S(1)} %get-tuple-element.75, f32[16,128]{1,0:T(8,128)S(1)} %bitcast.53, s32[16,128]{1,0:T(8,128)S(1)} %get-tuple-element.74, ...), kind=kLoop, calls=%fused_computation.1 | loop fusion | flops 12582912 | bytes 1179648 | tf_op jit(solution)/shard_map/convert_element_type | solution.py:26
  40.5 0.0 copy-done
  40.5 2.2 %pad_maximum_fusion.matrix_ref = bf16[4,16,256,128]{3,2,1,0:T(8,128)(2,1)} fusion(bf16[1,16,256,128]{3,2,1,0:T(8,128)(2,1)S(1)} %add_convert_fusion, bf16[1,16,256,128]{3,2,1,0:T(8,128)(2,1)S(1)} %add_convert_fusion.1, bf16[1,16,256,128]{3,2,1,0:T(8,128)(2,1)S(1)} %add_convert_fusion.2, bf16[1,16,256,128]{3,2,1,0:T(8,128)(2,1)S(1)} %copy-done), kind=kLoop, calls=%fused_computation | loop fusion | flops 6291456 | bytes 8388608 | tf_op jit(solution)/shard_map/stack | solution.py:189
  42.8 2.4 %all-to-all-done.rows_ref = bf16[128,4,2176]{2,1,0:T(4,128)(2,1)} async-done(((bf16[128,4,2176]{2,1,0:T(4,128)(2,1)}), bf16[128,4,2176]{2,1,0:T(4,128)(2,1)}, u32[]{:S(2)}, u32[]{:S(2)}) %all-to-all-start) | async-done | bytes 2228256 | tf_op jit(solution)/shard_map/all_to_all | solution.py:182
  45.2 7.9 %shard_map.83 = f32[64,2048]{1,0:T(8,128)} custom-call(bf16[128,4,2176]{2,1,0:T(4,128)(2,1)} %all-to-all-done.rows_ref, bf16[4,16,256,128]{3,2,1,0:T(8,128)(2,1)} %pad_maximum_fusion.matrix_ref, f32[16,256,128]{2,1,0:T(8,128)} %bitcast.46, f32[64,1]{1,0:T(8,128)} %copy.12.fold_ref), custom_call_target="tpu_custom_call" | custom-call | tf_op jit(solution)/shard_map/pallas_call | solution.py:91
  (7 shorter events, 0.1 us)
Async XLA Ops:
  3.7 11.9 %copy-start.2 = (bf16[1,4,8,2048]{3,2,1,0:T(8,128)(2,1)S(1)}, bf16[1,4,8,2048]{3,2,1,0:T(8,128)(2,1)}, u32[]{:S(2)}) copy-start(bf16[1,4,8,2048]{3,2,1,0:T(8,128)(2,1)} %param.12) | copy-start | bytes 393220
  3.7 12.0 %copy-start.3 = (s32[1,4,2048]{2,1,0:T(4,128)S(1)}, s32[1,4,2048]{2,1,0:T(4,128)}, u32[]{:S(2)}) copy-start(s32[1,4,2048]{2,1,0:T(4,128)} %param.13) | copy-start | bytes 98308
  3.7 41.5 %all-to-all-start = ((bf16[128,4,2176]{2,1,0:T(4,128)(2,1)}), bf16[128,4,2176]{2,1,0:T(4,128)(2,1)}, u32[]{:S(2)}, u32[]{:S(2)}) async-start(bf16[128,4,2176]{2,1,0:T(4,128)(2,1)} %shard_map.82), calls=%async_computation | async-start | bytes 4456448 | tf_op jit(solution)/shard_map/all_to_all | solution.py:182
  15.6 4.4 %copy-start.4 = (s32[1,64]{1,0:T(1,128)S(1)}, s32[1,64]{1,0:T(1,128)}, u32[]{:S(2)}) copy-start(s32[1,64]{1,0:T(1,128)} %param.15) | copy-start | bytes 772
  15.6 4.4 %copy-start.1 = (f32[31,2048]{1,0:T(8,128)S(1)}, f32[31,2048]{1,0:T(8,128)}, u32[]{:S(2)}) copy-start(f32[31,2048]{1,0:T(8,128)} %param.14) | copy-start | bytes 761860
  27.6 1.6 %slice-start = ((f32[16,128,383]{2,1,0:T(8,128)}), f32[16,128,256]{2,1,0:T(8,128)S(1)}, s32[]{:S(2)}) async-start(f32[16,128,383]{2,1,0:T(8,128)} %reshape.884), calls=%async_computation.1 | async-start | bytes 4194304 | tf_op jit(solution)/shard_map/slice | solution.py:120
  31.0 9.5 %copy-start = (bf16[1,16,256,128]{3,2,1,0:T(8,128)(2,1)S(1)}, bf16[1,16,256,128]{3,2,1,0:T(8,128)(2,1)}, u32[]{:S(2)}) copy-start(bf16[1,16,256,128]{3,2,1,0:T(8,128)(2,1)} %add_convert_fusion.3) | copy-start | bytes 3145732

commit v12 on v11

--- a/solution.py
+++ b/solution.py
@@ -9,6 +9,7 @@
 
 META = 128
 PAD = 16
+BAND = 160
 
 
 def moveout_matrix(coef_rows, shift_rows):
@@ -72,7 +73,7 @@
     def _():
         for inner in range(per_step):
             start = pl.multiple_of(((step - 1) * per_step + inner) * 128, 128)
-            window = stack_ref[:, pl.ds(start, 384)][:, 128 - PAD:384 - PAD]
+            window = stack_ref[:, pl.ds(start, 384)][:, 128 - PAD:128 - PAD + BAND]
             filtered = jnp.dot(
                 window,
                 taps_ref[inner],
@@ -86,7 +87,7 @@
     sources, capacity, width = rows.shape
     bins = fold_share.shape[0]
     classes, groups = matrices.shape[0], matrices.shape[1]
-    per_step = 4
+    per_step = 8
     steps = groups // per_step
     return pl.pallas_call(
         moveout_kernel,
@@ -96,7 +97,7 @@
             pl.BlockSpec(
                 (classes, per_step, 256, 128), lambda g: (0, jnp.minimum(g, steps - 1), 0, 0)
             ),
-            pl.BlockSpec((per_step, 256, 128), lambda g: (jnp.maximum(g - 1, 0), 0, 0)),
+            pl.BlockSpec((per_step, BAND, 128), lambda g: (jnp.maximum(g - 1, 0), 0, 0)),
             pl.BlockSpec((bins, 1), lambda g: (0, 0)),
         ],
         out_specs=pl.BlockSpec((bins, per_step * 128), lambda g: (0, jnp.maximum(g - 1, 0))),
@@ -117,7 +118,7 @@
     lead = PAD - half
     placed = jnp.pad(placed, ((0, 0), (0, 0), (lead, span - taps_count - lead)))
     flat = placed.reshape(groups, 128 * span)[:, : 128 * (span - 1)]
-    skewed = flat.reshape(groups, 128, span - 1)[:, :, :256]
+    skewed = flat.reshape(groups, 128, span - 1)[:, :, :BAND]
     return jnp.transpose(skewed, (0, 2, 1))
 
 

time: 53.4 us -> 52.5 us (0.983)
  Pallas kernels: 11.6 us -> 10.8 us
    pallas_call x1, Pallas kernels: 7.91 us -> 7.09 us  [moveout_stack(): pl.pallas_call(moveout_kernel, grid=(steps + 1,), in_specs=[pl.BlockSpec(...]
where the time goes in v12:
time: 52.5 us; the launch traced here: 52.3 us
  other arithmetic  15.1 us (29%)
  starting transfers between devices  11.9 us (23%)
  local copies, waits for them, and re-layouts  11.8 us (22%)
  Pallas kernels  10.8 us (21%)
  waiting for transfers between devices  2.6 us (5%)
    convert_element_type x4, other arithmetic, moveout_matrix(): return matrix.astype(jnp.bfloat16)  12.8 us
    all_to_all x1, starting transfers between devices, body(): lax.all_to_all(send, ('tile', 'line'), split_axis=0, concat_axis=0, tiled...  11.9 us
    pallas_call x1, Pallas kernels, moveout_stack(): pl.pallas_call(moveout_kernel, grid=(steps + 1,), in_specs=[pl.BlockSpec(...  7.09 us
    reshape x1, local copies, waits for them, and re-layouts, filter_matrix(): skewed = flat.reshape(groups, 128, span - 1)[:, :, :BAND]  4.53 us
    pallas_call x1, Pallas kernels, build_send(): pl.pallas_call(functools.partial(send_kernel, bins=bins, tiles=tiles), in...  3.67 us
    unnamed x12, local copies, waits for them, and re-layouts  3.53 us
    all_to_all x1, waiting for transfers between devices, body(): lax.all_to_all(send, ('tile', 'line'), split_axis=0, concat_axis=0, tiled...  2.6 us
    another operation x1, other arithmetic, body(): jnp.stack([moveout_matrix(nmo_coef[0, offset_index], band_shift[0, offset...  2.23 us
  transfers between devices with their start and end apart: 1, of which 1 were waited for; matrix products, arithmetic and copies ran while one was open for 48% of the time, Pallas kernels for 0%

profile of v12, /device:TPU:1, one launch (start us, length us, event | category | flops | bytes accessed | tf_op | source)
XLA Modules:
  0.0 52.3 jit_solution(4339096309456883852)
XLA Ops:
  0.0 3.7 %shard_map.82 = bf16[128,4,2176]{2,1,0:T(4,128)(2,1)} custom-call(s32[256]{0:T(256)} %line_ref.1, s32[256]{0:T(256)} %bin_ref.1, s32[2]{0:T(128)} %offset_ref.1, bf16[256,2048]{1,0:T(8,128)(2,1)} %traces_ref.1), custom_call_target="tpu_custom_call" | custom-call | tf_op jit(solution)/shard_map/pallas_call | solution.py:164
  3.7 0.0 copy-start.2
  3.7 0.0 copy-start.3
  3.7 11.9 %all-to-all-start = ((bf16[128,4,2176]{2,1,0:T(4,128)(2,1)}), bf16[128,4,2176]{2,1,0:T(4,128)(2,1)}, u32[]{:S(2)}, u32[]{:S(2)}) async-start(bf16[128,4,2176]{2,1,0:T(4,128)(2,1)} %shard_map.82), calls=%async_computation | async-start | bytes 4456448 | tf_op jit(solution)/shard_map/all_to_all | solution.py:183
  15.6 0.0 copy-done.2
  15.6 0.0 copy-start.4
  15.6 0.0 copy-start.1
  15.6 0.0 copy-done.3
  15.7 0.1 fusion
  15.8 0.1 fusion.2
  15.9 4.0 %add_convert_fusion.3 = bf16[1,16,256,128]{3,2,1,0:T(8,128)(2,1)} fusion(f32[16,128]{1,0:T(8,128)S(1)} %bitcast.74, s32[16,128]{1,0:T(8,128)S(1)} %get-tuple-element.52, f32[16,128]{1,0:T(8,128)S(1)} %bitcast.75, s32[16,128]{1,0:T(8,128)S(1)} %get-tuple-element.51, f32[16,128]{1,0:T(8,128)S(1)} %bitcast.76, s32[16,128]{1,0:T(8,128)S(1)} %get-tuple-element.50, ...), kind=kLoop, calls=%fused_computation.28 | loop fusion | flops 12582912 | bytes 1179648 | tf_op jit(solution)/shard_map/convert_element_type | solution.py:27
  20.0 0.0 copy-done.4
  20.0 0.0 copy-done.1
  20.0 0.4 copy.13
  20.3 0.7 %pad.4 = f32[16,128,384]{2,1,0:T(8,128)S(1)} pad(f32[16,128,31]{2,1,0:T(8,128)S(1)} %bitcast.47, f32[]{:T(128)} %constant.8.clone.1), padding=0_0x0_0x1_352 | pad | bytes 3399684 | tf_op jit(solution)/shard_map/jit(_pad)/pad | solution.py:119
  21.0 1.8 %copy.15 = f32[2,8,128,384]{3,1,2,0:T(8,128)S(1)} copy(f32[2,8,128,384]{3,2,1,0:T(8,128)S(1)} %bitcast.44) | data formatting | bytes 6291456
  22.8 0.2 slice.264
  23.0 4.5 %reshape.884 = f32[16,128,383]{2,1,0:T(8,128)} reshape(f32[16,49024]{1,0:T(8,128)S(1)} %slice.264) | data formatting | bytes 6275072 | tf_op jit(solution)/shard_map/reshape | solution.py:121
  27.6 0.0 slice-start
  27.6 1.6 %slice-done = f32[16,128,160]{2,1,0:T(8,128)S(1)} async-done(((f32[16,128,383]{2,1,0:T(8,128)}), f32[16,128,160]{2,1,0:T(8,128)S(1)}, s32[]{:S(2)}) %slice-start) | async-done | bytes 1310744 | tf_op jit(solution)/shard_map/slice | solution.py:121
  29.1 1.7 %copy.14 = f32[16,128,160]{1,2,0:T(8,128)} copy(f32[16,128,160]{2,1,0:T(8,128)S(1)} %slice-done) | data formatting | bytes 2621440
  30.8 0.0 copy-start
  30.8 0.7 %copy.12.fold_ref = f32[64,1]{1,0:T(8,128)} copy(f32[64,1]{0,1:T(1,128)S(1)} %convert_bitcast_fusion) | data formatting | bytes 512 | tf_op jit(solution)/shard_map/convert_element_type | solution.py:196
  31.6 2.9 %add_convert_fusion.2 = bf16[1,16,256,128]{3,2,1,0:T(8,128)(2,1)S(1)} fusion(f32[16,128]{1,0:T(8,128)S(1)} %bitcast.71, s32[16,128]{1,0:T(8,128)S(1)} %get-tuple-element.60, f32[16,128]{1,0:T(8,128)S(1)} %bitcast.70, s32[16,128]{1,0:T(8,128)S(1)} %get-tuple-element.59, f32[16,128]{1,0:T(8,128)S(1)} %bitcast.69, s32[16,128]{1,0:T(8,128)S(1)} %get-tuple-element.58, ...), kind=kLoop, calls=%fused_computation.19 | loop fusion | flops 12582912 | bytes 1179648 | tf_op jit(solution)/shard_map/convert_element_type | solution.py:27
  34.5 2.9 %add_convert_fusion.1 = bf16[1,16,256,128]{3,2,1,0:T(8,128)(2,1)S(1)} fusion(f32[16,128]{1,0:T(8,128)S(1)} %bitcast.58, s32[16,128]{1,0:T(8,128)S(1)} %get-tuple-element.68, f32[16,128]{1,0:T(8,128)S(1)} %bitcast.59, s32[16,128]{1,0:T(8,128)S(1)} %get-tuple-element.67, f32[16,128]{1,0:T(8,128)S(1)} %bitcast.60, s32[16,128]{1,0:T(8,128)S(1)} %get-tuple-element.66, ...), kind=kLoop, calls=%fused_computation.10 | loop fusion | flops 12582912 | bytes 1179648 | tf_op jit(solution)/shard_map/convert_element_type | solution.py:27
  37.4 2.9 %add_convert_fusion = bf16[1,16,256,128]{3,2,1,0:T(8,128)(2,1)S(1)} fusion(f32[16,128]{1,0:T(8,128)S(1)} %bitcast.55, s32[16,128]{1,0:T(8,128)S(1)} %get-tuple-element.76, f32[16,128]{1,0:T(8,128)S(1)} %bitcast.54, s32[16,128]{1,0:T(8,128)S(1)} %get-tuple-element.75, f32[16,128]{1,0:T(8,128)S(1)} %bitcast.53, s32[16,128]{1,0:T(8,128)S(1)} %get-tuple-element.74, ...), kind=kLoop, calls=%fused_computation.1 | loop fusion | flops 12582912 | bytes 1179648 | tf_op jit(solution)/shard_map/convert_element_type | solution.py:27
  40.4 0.0 copy-done
  40.4 2.2 %pad_maximum_fusion.matrix_ref = bf16[4,16,256,128]{3,2,1,0:T(8,128)(2,1)} fusion(bf16[1,16,256,128]{3,2,1,0:T(8,128)(2,1)S(1)} %add_convert_fusion, bf16[1,16,256,128]{3,2,1,0:T(8,128)(2,1)S(1)} %add_convert_fusion.1, bf16[1,16,256,128]{3,2,1,0:T(8,128)(2,1)S(1)} %add_convert_fusion.2, bf16[1,16,256,128]{3,2,1,0:T(8,128)(2,1)S(1)} %copy-done), kind=kLoop, calls=%fused_computation | loop fusion | flops 6291456 | bytes 8388608 | tf_op jit(solution)/shard_map/stack | solution.py:190
  42.6 2.6 %all-to-all-done.rows_ref = bf16[128,4,2176]{2,1,0:T(4,128)(2,1)} async-done(((bf16[128,4,2176]{2,1,0:T(4,128)(2,1)}), bf16[128,4,2176]{2,1,0:T(4,128)(2,1)}, u32[]{:S(2)}, u32[]{:S(2)}) %all-to-all-start) | async-done | bytes 2228256 | tf_op jit(solution)/shard_map/all_to_all | solution.py:183
  45.2 7.1 %shard_map.83 = f32[64,2048]{1,0:T(8,128)} custom-call(bf16[128,4,2176]{2,1,0:T(4,128)(2,1)} %all-to-all-done.rows_ref, bf16[4,16,256,128]{3,2,1,0:T(8,128)(2,1)} %pad_maximum_fusion.matrix_ref, f32[16,160,128]{2,1,0:T(8,128)} %bitcast.46, f32[64,1]{1,0:T(8,128)} %copy.12.fold_ref), custom_call_target="tpu_custom_call" | custom-call | tf_op jit(solution)/shard_map/pallas_call | solution.py:92
  (7 shorter events, 0.1 us)
Async XLA Ops:
  3.7 11.9 %copy-start.2 = (bf16[1,4,8,2048]{3,2,1,0:T(8,128)(2,1)S(1)}, bf16[1,4,8,2048]{3,2,1,0:T(8,128)(2,1)}, u32[]{:S(2)}) copy-start(bf16[1,4,8,2048]{3,2,1,0:T(8,128)(2,1)} %param.12) | copy-start | bytes 393220
  3.7 12.0 %copy-start.3 = (s32[1,4,2048]{2,1,0:T(4,128)S(1)}, s32[1,4,2048]{2,1,0:T(4,128)}, u32[]{:S(2)}) copy-start(s32[1,4,2048]{2,1,0:T(4,128)} %param.13) | copy-start | bytes 98308
  3.7 41.5 %all-to-all-start = ((bf16[128,4,2176]{2,1,0:T(4,128)(2,1)}), bf16[128,4,2176]{2,1,0:T(4,128)(2,1)}, u32[]{:S(2)}, u32[]{:S(2)}) async-start(bf16[128,4,2176]{2,1,0:T(4,128)(2,1)} %shard_map.82), calls=%async_computation | async-start | bytes 4456448 | tf_op jit(solution)/shard_map/all_to_all | solution.py:183
  15.6 4.4 %copy-start.4 = (s32[1,64]{1,0:T(1,128)S(1)}, s32[1,64]{1,0:T(1,128)}, u32[]{:S(2)}) copy-start(s32[1,64]{1,0:T(1,128)} %param.15) | copy-start | bytes 772
  15.6 4.4 %copy-start.1 = (f32[31,2048]{1,0:T(8,128)S(1)}, f32[31,2048]{1,0:T(8,128)}, u32[]{:S(2)}) copy-start(f32[31,2048]{1,0:T(8,128)} %param.14) | copy-start | bytes 761860
  27.6 1.6 %slice-start = ((f32[16,128,383]{2,1,0:T(8,128)}), f32[16,128,160]{2,1,0:T(8,128)S(1)}, s32[]{:S(2)}) async-start(f32[16,128,383]{2,1,0:T(8,128)} %reshape.884), calls=%async_computation.1 | async-start | bytes 4194304 | tf_op jit(solution)/shard_map/slice | solution.py:121
  30.8 9.5 %copy-start = (bf16[1,16,256,128]{3,2,1,0:T(8,128)(2,1)S(1)}, bf16[1,16,256,128]{3,2,1,0:T(8,128)(2,1)}, u32[]{:S(2)}) copy-start(bf16[1,16,256,128]{3,2,1,0:T(8,128)(2,1)} %add_convert_fusion.3) | copy-start | bytes 3145732

commit v13 on v12

--- a/solution.py
+++ b/solution.py
@@ -77,7 +77,7 @@
             filtered = jnp.dot(
                 window,
                 taps_ref[inner],
-                precision=lax.Precision.HIGHEST,
+                precision=lax.Precision.HIGH,
                 preferred_element_type=jnp.float32,
             )
             out_ref[:, inner * 128:(inner + 1) * 128] = filtered / fold_ref[...]

time: 52.5 us -> 52 us (level)
  Pallas kernels: 10.8 us -> 10.2 us
    pallas_call x1, Pallas kernels: 7.09 us -> 6.56 us  [moveout_stack(): pl.pallas_call(moveout_kernel, grid=(steps + 1,), in_specs=[pl.BlockSpec(...]
  transfers between devices with their start and end apart: 1 -> 1, of which waited for: 1 -> 1; matrix products, arithmetic and copies ran while one was open for 48% -> 49% of each run, Pallas kernels for 0% -> 0%
where the time goes in v13:
time: 52 us; the launch traced here: 51.8 us
  other arithmetic  15.1 us (29%)
  starting transfers between devices  11.9 us (23%)
  local copies, waits for them, and re-layouts  11.8 us (23%)
  Pallas kernels  10.2 us (20%)
  waiting for transfers between devices  2.6 us (5%)
    convert_element_type x4, other arithmetic, moveout_matrix(): return matrix.astype(jnp.bfloat16)  12.8 us
    all_to_all x1, starting transfers between devices, body(): lax.all_to_all(send, ('tile', 'line'), split_axis=0, concat_axis=0, tiled...  11.9 us
    pallas_call x1, Pallas kernels, moveout_stack(): pl.pallas_call(moveout_kernel, grid=(steps + 1,), in_specs=[pl.BlockSpec(...  6.56 us
    reshape x1, local copies, waits for them, and re-layouts, filter_matrix(): skewed = flat.reshape(groups, 128, span - 1)[:, :, :BAND]  4.53 us
    pallas_call x1, Pallas kernels, build_send(): pl.pallas_call(functools.partial(send_kernel, bins=bins, tiles=tiles), in...  3.67 us
    unnamed x12, local copies, waits for them, and re-layouts  3.53 us
    all_to_all x1, waiting for transfers between devices, body(): lax.all_to_all(send, ('tile', 'line'), split_axis=0, concat_axis=0, tiled...  2.6 us
    another operation x1, other arithmetic, body(): jnp.stack([moveout_matrix(nmo_coef[0, offset_index], band_shift[0, offset...  2.23 us
  transfers between devices with their start and end apart: 1, of which 1 were waited for; matrix products, arithmetic and copies ran while one was open for 49% of the time, Pallas kernels for 0%

profile of v13, /device:TPU:1, one launch (start us, length us, event | category | flops | bytes accessed | tf_op | source)
XLA Modules:
  0.0 51.8 jit_solution(15922167819935951632)
XLA Ops:
  0.0 3.7 %shard_map.82 = bf16[128,4,2176]{2,1,0:T(4,128)(2,1)} custom-call(s32[256]{0:T(256)} %line_ref.1, s32[256]{0:T(256)} %bin_ref.1, s32[2]{0:T(128)} %offset_ref.1, bf16[256,2048]{1,0:T(8,128)(2,1)} %traces_ref.1), custom_call_target="tpu_custom_call" | custom-call | tf_op jit(solution)/shard_map/pallas_call | solution.py:164
  3.7 0.0 copy-start.2
  3.7 0.0 copy-start.3
  3.7 11.9 %all-to-all-start = ((bf16[128,4,2176]{2,1,0:T(4,128)(2,1)}), bf16[128,4,2176]{2,1,0:T(4,128)(2,1)}, u32[]{:S(2)}, u32[]{:S(2)}) async-start(bf16[128,4,2176]{2,1,0:T(4,128)(2,1)} %shard_map.82), calls=%async_computation | async-start | bytes 4456448 | tf_op jit(solution)/shard_map/all_to_all | solution.py:183
  15.6 0.0 copy-done.2
  15.6 0.0 copy-start.4
  15.6 0.0 copy-start.1
  15.6 0.0 copy-done.3
  15.7 0.1 fusion
  15.8 0.1 fusion.2
  15.9 4.0 %add_convert_fusion.3 = bf16[1,16,256,128]{3,2,1,0:T(8,128)(2,1)} fusion(f32[16,128]{1,0:T(8,128)S(1)} %bitcast.74, s32[16,128]{1,0:T(8,128)S(1)} %get-tuple-element.52, f32[16,128]{1,0:T(8,128)S(1)} %bitcast.75, s32[16,128]{1,0:T(8,128)S(1)} %get-tuple-element.51, f32[16,128]{1,0:T(8,128)S(1)} %bitcast.76, s32[16,128]{1,0:T(8,128)S(1)} %get-tuple-element.50, ...), kind=kLoop, calls=%fused_computation.28 | loop fusion | flops 12582912 | bytes 1179648 | tf_op jit(solution)/shard_map/convert_element_type | solution.py:27
  20.0 0.0 copy-done.4
  20.0 0.0 copy-done.1
  20.0 0.4 copy.13
  20.3 0.7 %pad.4 = f32[16,128,384]{2,1,0:T(8,128)S(1)} pad(f32[16,128,31]{2,1,0:T(8,128)S(1)} %bitcast.47, f32[]{:T(128)} %constant.8.clone.1), padding=0_0x0_0x1_352 | pad | bytes 3399684 | tf_op jit(solution)/shard_map/jit(_pad)/pad | solution.py:119
  21.0 1.8 %copy.15 = f32[2,8,128,384]{3,1,2,0:T(8,128)S(1)} copy(f32[2,8,128,384]{3,2,1,0:T(8,128)S(1)} %bitcast.44) | data formatting | bytes 6291456
  22.8 0.2 slice.264
  23.0 4.5 %reshape.884 = f32[16,128,383]{2,1,0:T(8,128)} reshape(f32[16,49024]{1,0:T(8,128)S(1)} %slice.264) | data formatting | bytes 6275072 | tf_op jit(solution)/shard_map/reshape | solution.py:121
  27.6 0.0 slice-start
  27.6 1.6 %slice-done = f32[16,128,160]{2,1,0:T(8,128)S(1)} async-done(((f32[16,128,383]{2,1,0:T(8,128)}), f32[16,128,160]{2,1,0:T(8,128)S(1)}, s32[]{:S(2)}) %slice-start) | async-done | bytes 1310744 | tf_op jit(solution)/shard_map/slice | solution.py:121
  29.1 1.7 %copy.14 = f32[16,128,160]{1,2,0:T(8,128)} copy(f32[16,128,160]{2,1,0:T(8,128)S(1)} %slice-done) | data formatting | bytes 2621440
  30.8 0.0 copy-start
  30.8 0.7 %copy.12.fold_ref = f32[64,1]{1,0:T(8,128)} copy(f32[64,1]{0,1:T(1,128)S(1)} %convert_bitcast_fusion) | data formatting | bytes 512 | tf_op jit(solution)/shard_map/convert_element_type | solution.py:196
  31.6 2.9 %add_convert_fusion.2 = bf16[1,16,256,128]{3,2,1,0:T(8,128)(2,1)S(1)} fusion(f32[16,128]{1,0:T(8,128)S(1)} %bitcast.71, s32[16,128]{1,0:T(8,128)S(1)} %get-tuple-element.60, f32[16,128]{1,0:T(8,128)S(1)} %bitcast.70, s32[16,128]{1,0:T(8,128)S(1)} %get-tuple-element.59, f32[16,128]{1,0:T(8,128)S(1)} %bitcast.69, s32[16,128]{1,0:T(8,128)S(1)} %get-tuple-element.58, ...), kind=kLoop, calls=%fused_computation.19 | loop fusion | flops 12582912 | bytes 1179648 | tf_op jit(solution)/shard_map/convert_element_type | solution.py:27
  34.5 2.9 %add_convert_fusion.1 = bf16[1,16,256,128]{3,2,1,0:T(8,128)(2,1)S(1)} fusion(f32[16,128]{1,0:T(8,128)S(1)} %bitcast.58, s32[16,128]{1,0:T(8,128)S(1)} %get-tuple-element.68, f32[16,128]{1,0:T(8,128)S(1)} %bitcast.59, s32[16,128]{1,0:T(8,128)S(1)} %get-tuple-element.67, f32[16,128]{1,0:T(8,128)S(1)} %bitcast.60, s32[16,128]{1,0:T(8,128)S(1)} %get-tuple-element.66, ...), kind=kLoop, calls=%fused_computation.10 | loop fusion | flops 12582912 | bytes 1179648 | tf_op jit(solution)/shard_map/convert_element_type | solution.py:27
  37.4 2.9 %add_convert_fusion = bf16[1,16,256,128]{3,2,1,0:T(8,128)(2,1)S(1)} fusion(f32[16,128]{1,0:T(8,128)S(1)} %bitcast.55, s32[16,128]{1,0:T(8,128)S(1)} %get-tuple-element.76, f32[16,128]{1,0:T(8,128)S(1)} %bitcast.54, s32[16,128]{1,0:T(8,128)S(1)} %get-tuple-element.75, f32[16,128]{1,0:T(8,128)S(1)} %bitcast.53, s32[16,128]{1,0:T(8,128)S(1)} %get-tuple-element.74, ...), kind=kLoop, calls=%fused_computation.1 | loop fusion | flops 12582912 | bytes 1179648 | tf_op jit(solution)/shard_map/convert_element_type | solution.py:27
  40.4 0.0 copy-done
  40.4 2.2 %pad_maximum_fusion.matrix_ref = bf16[4,16,256,128]{3,2,1,0:T(8,128)(2,1)} fusion(bf16[1,16,256,128]{3,2,1,0:T(8,128)(2,1)S(1)} %add_convert_fusion, bf16[1,16,256,128]{3,2,1,0:T(8,128)(2,1)S(1)} %add_convert_fusion.1, bf16[1,16,256,128]{3,2,1,0:T(8,128)(2,1)S(1)} %add_convert_fusion.2, bf16[1,16,256,128]{3,2,1,0:T(8,128)(2,1)S(1)} %copy-done), kind=kLoop, calls=%fused_computation | loop fusion | flops 6291456 | bytes 8388608 | tf_op jit(solution)/shard_map/stack | solution.py:190
  42.6 2.6 %all-to-all-done.rows_ref = bf16[128,4,2176]{2,1,0:T(4,128)(2,1)} async-done(((bf16[128,4,2176]{2,1,0:T(4,128)(2,1)}), bf16[128,4,2176]{2,1,0:T(4,128)(2,1)}, u32[]{:S(2)}, u32[]{:S(2)}) %all-to-all-start) | async-done | bytes 2228256 | tf_op jit(solution)/shard_map/all_to_all | solution.py:183
  45.2 6.6 %shard_map.83 = f32[64,2048]{1,0:T(8,128)} custom-call(bf16[128,4,2176]{2,1,0:T(4,128)(2,1)} %all-to-all-done.rows_ref, bf16[4,16,256,128]{3,2,1,0:T(8,128)(2,1)} %pad_maximum_fusion.matrix_ref, f32[16,160,128]{2,1,0:T(8,128)} %bitcast.46, f32[64,1]{1,0:T(8,128)} %copy.12.fold_ref), custom_call_target="tpu_custom_call" | custom-call | tf_op jit(solution)/shard_map/pallas_call | solution.py:92
  (7 shorter events, 0.1 us)
Async XLA Ops:
  3.7 11.9 %copy-start.2 = (bf16[1,4,8,2048]{3,2,1,0:T(8,128)(2,1)S(1)}, bf16[1,4,8,2048]{3,2,1,0:T(8,128)(2,1)}, u32[]{:S(2)}) copy-start(bf16[1,4,8,2048]{3,2,1,0:T(8,128)(2,1)} %param.12) | copy-start | bytes 393220
  3.7 12.0 %copy-start.3 = (s32[1,4,2048]{2,1,0:T(4,128)S(1)}, s32[1,4,2048]{2,1,0:T(4,128)}, u32[]{:S(2)}) copy-start(s32[1,4,2048]{2,1,0:T(4,128)} %param.13) | copy-start | bytes 98308
  3.7 41.5 %all-to-all-start = ((bf16[128,4,2176]{2,1,0:T(4,128)(2,1)}), bf16[128,4,2176]{2,1,0:T(4,128)(2,1)}, u32[]{:S(2)}, u32[]{:S(2)}) async-start(bf16[128,4,2176]{2,1,0:T(4,128)(2,1)} %shard_map.82), calls=%async_computation | async-start | bytes 4456448 | tf_op jit(solution)/shard_map/all_to_all | solution.py:183
  15.6 4.4 %copy-start.4 = (s32[1,64]{1,0:T(1,128)S(1)}, s32[1,64]{1,0:T(1,128)}, u32[]{:S(2)}) copy-start(s32[1,64]{1,0:T(1,128)} %param.15) | copy-start | bytes 772
  15.6 4.4 %copy-start.1 = (f32[31,2048]{1,0:T(8,128)S(1)}, f32[31,2048]{1,0:T(8,128)}, u32[]{:S(2)}) copy-start(f32[31,2048]{1,0:T(8,128)} %param.14) | copy-start | bytes 761860
  27.6 1.6 %slice-start = ((f32[16,128,383]{2,1,0:T(8,128)}), f32[16,128,160]{2,1,0:T(8,128)S(1)}, s32[]{:S(2)}) async-start(f32[16,128,383]{2,1,0:T(8,128)} %reshape.884), calls=%async_computation.1 | async-start | bytes 4194304 | tf_op jit(solution)/shard_map/slice | solution.py:121
  30.8 9.5 %copy-start = (bf16[1,16,256,128]{3,2,1,0:T(8,128)(2,1)S(1)}, bf16[1,16,256,128]{3,2,1,0:T(8,128)(2,1)}, u32[]{:S(2)}) copy-start(bf16[1,16,256,128]{3,2,1,0:T(8,128)(2,1)} %add_convert_fusion.3) | copy-start | bytes 3145732
